TPU v7x, 128 devices: a whole 4x4x4 slice. The times are simulated.
128 devices in a mesh: group: 4 (over z), member: 32 (over x, y, core).
Axes of the slice: x: 4, y: 4, z: 4, core: 2. Of those that a mesh axis runs over, the one named last changes fastest.
Arguments:
- passage_hidden: bfloat16 [16384, 768], P(('group', 'member')), may hold values from -6 to 6
- query_hidden: bfloat16 [65536, 768], P(('group', 'member')), may hold values from -96 to 96
- proj_weight: bfloat16 [768, 768], replicated, may hold values from -0.21875 to 0.21875
- cluster: int32 [16384], P(('group', 'member')), may hold values from 0 to 3, as said below
- place: int32 [16384], P(('group', 'member')), may hold values from 0 to 4095, as said below
- positive: int32 [65536], P(('group', 'member')), may hold values from 0 to 4095
- loss_weight: float32 [65536], P(('group', 'member')), may hold values from 8 to 64
Outputs:
- loss: float32 [65536], P(('group', 'member'))
- grad_query_hidden: bfloat16 [65536, 768], P(('group', 'member'))
- grad_passage_hidden: bfloat16 [16384, 768], P(('group', 'member'))
- grad_weight: float32 [768, 768], replicated
Inputs may be any that keep to these rules, and one draw needn't show every extreme that they name: Every cluster group holds exactly 4096 passages. Within one cluster group each row 0 to 4095 is taken by exactly one passage. Call the owner of a passage the device cluster * 32 + place // 128; every device owns 128 passages, every device sends at most 2 passages to one owner and exactly 2 to some owner, and the count that device d sends to owner o depends only on o - d modulo 128.
All inputs are finite; a program needn't handle non-finite values.
Results may differ from a plain program's by a relative error of at most 0.0095.
Values may be sent and summed in bfloat16 or wider, within the bound.
No kernel may reach another device: no remote copies, remote signals or barrier semaphores. Data moves between devices by JAX's collectives and lax.ppermute only.
A program may use at most 128 MiB of HBM per device.

v0:
```python
import math

import jax
import jax.numpy as jnp
from jax import lax
from jax.sharding import PartitionSpec as P


def contract(left, right, left_dim, right_dim):
    return lax.dot_general(
        left, right, (((left_dim,), (right_dim,)), ((), ())), preferred_element_type=jnp.float32
    )


def shards(passage_hidden, query_hidden, proj_weight, cluster, place, positive, loss_weight):
    rows, width = passage_hidden.shape
    members = lax.axis_size("member")
    groups = lax.axis_size("group")
    devices = members * groups
    group_rows = rows * members
    capacity = 2 * rows // devices
    factor = 1.0 / math.sqrt(width)
    passage_emb = jnp.dot(passage_hidden, proj_weight, preferred_element_type=jnp.float32).astype(
        jnp.bfloat16
    )
    query_emb = jnp.dot(query_hidden, proj_weight, preferred_element_type=jnp.float32).astype(
        jnp.bfloat16
    )
    target = cluster * group_rows + place
    owner = target // rows
    slot = target % rows
    order = jnp.arange(rows, dtype=jnp.int32)
    earlier_same = (owner[:, None] == owner[None, :]) & (order[:, None] > order[None, :])
    rank = jnp.sum(earlier_same.astype(jnp.int32), axis=1)
    position = owner * capacity + rank
    send_rows = jnp.zeros((devices * capacity, width), jnp.bfloat16).at[position].set(passage_emb)
    send_slots = jnp.full((devices * capacity,), rows, jnp.int32).at[position].set(slot)
    got_rows, got_slots = (
        lax.all_to_all(send_rows, ("group", "member"), split_axis=0, concat_axis=0, tiled=True),
        lax.all_to_all(send_slots, ("group", "member"), split_axis=0, concat_axis=0, tiled=True),
    )
    relaid = jnp.zeros((rows, width), jnp.bfloat16).at[got_slots].set(got_rows, mode="drop")
    group_passages = lax.all_gather(relaid, "member", axis=0, tiled=True)
    scores = contract(query_emb, group_passages, 1, 1) * factor
    top = jnp.max(scores, axis=1, keepdims=True)
    lse = top[:, 0] + jnp.log(jnp.sum(jnp.exp(scores - top), axis=1))
    hit = jnp.arange(group_rows, dtype=jnp.int32)[None, :] == positive[:, None]
    loss = lse - jnp.sum(jnp.where(hit, scores, 0.0), axis=1)
    coef = (
        loss_weight[:, None] * (jnp.exp(scores - lse[:, None]) - hit.astype(jnp.float32)) * factor
    ).astype(jnp.bfloat16)
    query_grad = jnp.dot(coef, group_passages, preferred_element_type=jnp.float32).astype(
        jnp.bfloat16
    )
    own_columns = lax.axis_index("member") * rows + order
    group_lse, group_weight, group_target = (
        lax.all_gather(lse, "member", axis=0, tiled=True),
        lax.all_gather(loss_weight, "member", axis=0, tiled=True),
        lax.all_gather(positive, "member", axis=0, tiled=True),
    )
    piece = lax.all_gather(query_emb, "member", axis=0, tiled=True)
    part_scores = contract(piece, relaid, 1, 1) * factor
    part_hit = own_columns[None, :] == group_target[:, None]
    part_coef = (
        group_weight[:, None]
        * (jnp.exp(part_scores - group_lse[:, None]) - part_hit.astype(jnp.float32))
        * factor
    ).astype(jnp.bfloat16)
    relaid_grad = contract(part_coef, piece, 0, 0).astype(jnp.bfloat16)
    back_rows = relaid_grad[jnp.minimum(got_slots, rows - 1)]
    returned = lax.all_to_all(
        back_rows, ("group", "member"), split_axis=0, concat_axis=0, tiled=True
    )
    passage_grad = returned[position]
    grad_passage_hidden = contract(passage_grad, proj_weight, 1, 1).astype(jnp.bfloat16)
    grad_query_hidden = contract(query_grad, proj_weight, 1, 1).astype(jnp.bfloat16)
    local_weight = contract(passage_hidden, passage_grad, 0, 0) + contract(
        query_hidden, query_grad, 0, 0
    )
    grad_weight = lax.psum(local_weight, ("group", "member")) / devices
    return (loss, grad_query_hidden, grad_passage_hidden, grad_weight)


def solution(mesh):
    in_specs = (
        P(("group", "member"), None),
        P(("group", "member"), None),
        P(),
        P(("group", "member")),
        P(("group", "member")),
        P(("group", "member")),
        P(("group", "member")),
    )
    out_specs = (
        P(("group", "member")),
        P(("group", "member"), None),
        P(("group", "member"), None),
        P(),
    )
    return jax.shard_map(shards, mesh=mesh, in_specs=in_specs, out_specs=out_specs, check_vma=False)
```

profile of v0, /device:TPU:1, one launch (start us, length us, event | category | flops | bytes accessed | tf_op | source)
XLA Modules:
  0.0 406.6 jit_solution(16163417750775660717)
XLA Ops:
  7.2 0.8 and_select_fusion
  8.0 0.7 and_select_fusion.1
  8.7 0.2 convert_reduce_fusion
  8.8 1.0 scatter_custom_fusion
  9.8 0.8 all_to_all.24
  10.6 11.5 %all-to-all-start = ((s32[128,2,1]{1,2,0:T(1,128)}), s32[128,2,1]{1,2,0:T(1,128)S(1)}, u32[]{:S(2)}, u32[]{:S(2)}) async-start(s32[128,2,1]{1,2,0:T(1,128)} %bitcast), calls=%async_computation | async-start | bytes 131072 | tf_op jit(solution)/shard_map/all_to_all | solution.py:40
  22.1 1.3 convolution_convert_fusion.3
  23.4 1.2 scatter_custom_fusion.1
  24.6 0.9 all_to_all.27
  25.5 6.1 %all-to-all-done = s32[128,2,1]{1,2,0:T(1,128)S(1)} async-done(((s32[128,2,1]{1,2,0:T(1,128)}), s32[128,2,1]{1,2,0:T(1,128)S(1)}, u32[]{:S(2)}, u32[]{:S(2)}) %all-to-all-start) | async-done | bytes 1056 | tf_op jit(solution)/shard_map/all_to_all | solution.py:40
  31.7 4.4 %all-to-all-start.1 = ((bf16[128,2,768]{2,1,0:T(2,128)(2,1)}), bf16[128,2,768]{2,1,0:T(2,128)(2,1)S(1)}, u32[]{:S(2)}, u32[]{:S(2)}) async-start(bf16[128,2,768]{2,1,0:T(2,128)(2,1)} %all_to_all.27), calls=%async_computation.1 | async-start | bytes 786432 | tf_op jit(solution)/shard_map/all_to_all | solution.py:39
  36.1 0.0 all-gather.6.cloned.1.call-start
  36.1 0.5 broadcast.123
  36.6 0.8 reduce.3
  37.4 0.1 all_to_all.26
  37.6 10.6 %all-to-all-done.1 = bf16[128,2,768]{2,1,0:T(2,128)(2,1)S(1)} async-done(((bf16[128,2,768]{2,1,0:T(2,128)(2,1)}), bf16[128,2,768]{2,1,0:T(2,128)(2,1)S(1)}, u32[]{:S(2)}, u32[]{:S(2)}) %all-to-all-start.1) | async-done | bytes 393248 | tf_op jit(solution)/shard_map/all_to_all | solution.py:39
  48.2 0.1 reshape.115
  48.4 2.2 scatter_custom_fusion.2
  50.6 0.0 all-gather.6.cloned.1.call-update
  50.7 0.0 all-gather.8.cloned.1.call-start
  50.7 2.8 convolution_convert_fusion.1
  53.5 0.0 all-gather.8.cloned.1.call-update
  53.5 23.2 %all-gather = f32[32,1,512]{2,1,0:T(1,128)S(1)} all-gather(f32[1,1,512]{2,1,0:T(1,128)S(1)} %bitcast.44), channel_id=1, replica_groups=mesh['group'=4,'member'=32] {'member'}, dimensions={0}, use_global_device_ids=true | all-gather | bytes 67584 | tf_op jit(solution)/shard_map/all_gather | solution.py:58
  76.7 23.5 %all-gather.2 = s32[32,1,512]{2,1,0:T(1,128)S(1)} all-gather(s32[1,1,512]{2,1,0:T(1,128)S(1)} %bitcast.41), channel_id=1, replica_groups=mesh['group'=4,'member'=32] {'member'}, dimensions={0}, use_global_device_ids=true | all-gather | bytes 67584 | tf_op jit(solution)/shard_map/all_gather | solution.py:59
  100.2 0.0 all-gather.6.cloned.1.call-done
  100.3 5.9 %multiply_reduce_fusion = (f32[512]{0:T(512)S(1)}, f32[512,4096]{1,0:T(8,128)S(1)}) fusion(bf16[512,768]{1,0:T(8,128)(2,1)} %convolution_convert_fusion.1, bf16[4096,768]{1,0:T(8,128)(2,1)} %all-gather.6.cloned.1.call-done), kind=kOutput, calls=%fused_computation.16 | convolution fusion | flops 3225419264 | bytes 15468544 | tf_op jit(solution)/shard_map/dot_general | solution.py:10
  106.2 3.6 copy-done.1
  109.8 3.1 select_reduce_fusion
  112.9 0.6 fusion.19
  113.5 22.6 %all-gather.1 = f32[32,1,512]{2,1,0:T(1,128)S(1)} all-gather(f32[1,1,512]{2,1,0:T(1,128)S(1)} %bitcast.42), channel_id=1, replica_groups=mesh['group'=4,'member'=32] {'member'}, dimensions={0}, use_global_device_ids=true | all-gather | bytes 67584 | tf_op jit(solution)/shard_map/all_gather | solution.py:57
  136.1 53.8 %all-gather.8.cloned.1.call-done = bf16[16384,768]{1,0:T(8,128)(2,1)} async-done(((bf16[512,768]{1,0:T(8,128)(2,1)}), bf16[16384,768]{1,0:T(8,128)(2,1)}) %all-gather.8.cloned.1.call-update) | async-done | bytes 25165840 | tf_op jit(solution)/shard_map/all_gather | solution.py:61
  189.9 13.4 %fusion.5.clone.6 = bf16[16384,128]{1,0:T(8,128)(2,1)S(1)} fusion(bf16[16384,768]{1,0:T(8,128)(2,1)} %all-gather.8.cloned.1.call-done, bf16[128,768]{1,0:T(8,128)(2,1)S(1)} %copy-done.3, s32[128]{0:T(128)S(1)} %iota_add_fusion, f32[16384]{0:T(1024)S(1)} %bitcast.40, f32[16384]{0:T(1024)S(1)} %bitcast.38, s32[16384]{0:T(1024)S(1)} %bitcast.39), kind=kOutput, calls=%fused_computation.11.clone.clone.clone.clone.clone.1 | convolution fusion | flops 3238002688 | bytes 29753856 | tf_op jit(solution)/shard_map/dot_general | solution.py:10
  203.4 10.2 %fusion.9 = bf16[128,768]{1,0:T(8,128)(2,1)S(1)} fusion(bf16[16384,768]{1,0:T(8,128)(2,1)} %all-gather.8.cloned.1.call-done, bf16[16384,128]{1,0:T(8,128)(2,1)S(1)} %fusion.5.clone.6), kind=kOutput, calls=%fused_computation.26 | convolution fusion | flops 3221323776 | bytes 29556736 | tf_op jit(solution)/shard_map/dot_general | solution.py:10
  213.6 1.2 gather_fusion
  214.8 0.9 all_to_all.30
  215.7 7.7 %all-to-all-start.2 = ((bf16[128,2,768]{2,1,0:T(2,128)(2,1)}), bf16[128,2,768]{2,1,0:T(2,128)(2,1)}, u32[]{:S(2)}, u32[]{:S(2)}) async-start(bf16[128,2,768]{2,1,0:T(2,128)(2,1)} %all_to_all.30), calls=%async_computation.2 | async-start | bytes 786432 | tf_op jit(solution)/shard_map/all_to_all | solution.py:71
  223.4 0.0 all-reduce.2.cloned.1.call-start
  223.5 10.4 %fusion.7 = bf16[512,768]{1,0:T(8,128)(2,1)S(1)} fusion(bf16[4096,768]{1,0:T(8,128)(2,1)} %all-gather.6.cloned.1.call-done, f32[512,4096]{1,0:T(8,128)} %copy-done.1, f32[512]{0:T(512)S(1)} %get-tuple-element.23, f32[512]{0:T(512)S(1)} %copy-done.6, s32[512]{0:T(512)S(1)} %copy-done.5), kind=kOutput, calls=%fused_computation.21 | convolution fusion | flops 3238395904 | bytes 15472640 | tf_op jit(solution)/shard_map/dot_general | solution.py:52
  233.9 0.9 copy-done.2
  234.8 0.8 fusion.20
  235.6 1.9 all_to_all.32
  237.5 2.7 gather_fusion.1
  240.2 2.9 add_bitcast_fusion
  243.1 2.8 convolution_convert_fusion
  246.0 2.1 convolution_convert_fusion.2
  248.1 148.2 %all-reduce.2.cloned.1.call-done = f32[768,768]{0,1:T(8,128)} async-done(((f32[768,768]{0,1:T(8,128)}), f32[768,768]{0,1:T(8,128)}) %all-reduce.2.cloned.1.call-update) | async-done | bytes 2359312 | tf_op jit(solution)/shard_map/psum | solution.py:80
  396.3 1.8 broadcast_multiply_fusion
  398.2 2.0 copy.16
  (19 shorter events, 0.1 us)
Async XLA Ops:
  7.2 14.9 %copy-start = (bf16[768,768]{1,0:T(8,128)(2,1)S(1)}, bf16[768,768]{1,0:T(8,128)(2,1)}, u32[]{:S(2)}) copy-start(bf16[768,768]{1,0:T(8,128)(2,1)} %param.9) | copy-start | bytes 3538948
  7.2 46.3 %copy-start.6 = (f32[512]{0:T(512)S(1)}, f32[512]{0:T(512)}, u32[]{:S(2)}) copy-start(f32[512]{0:T(512)} %param.13) | copy-start | bytes 6148
  7.2 69.5 %copy-start.5 = (s32[512]{0:T(512)S(1)}, s32[512]{0:T(512)}, u32[]{:S(2)}) copy-start(s32[512]{0:T(512)} %param.12) | copy-start | bytes 6148
  10.6 21.1 %all-to-all-start = ((s32[128,2,1]{1,2,0:T(1,128)}), s32[128,2,1]{1,2,0:T(1,128)S(1)}, u32[]{:S(2)}, u32[]{:S(2)}) async-start(s32[128,2,1]{1,2,0:T(1,128)} %bitcast), calls=%async_computation | async-start | bytes 131072 | tf_op jit(solution)/shard_map/all_to_all | solution.py:40
  31.7 16.6 %all-to-all-start.1 = ((bf16[128,2,768]{2,1,0:T(2,128)(2,1)}), bf16[128,2,768]{2,1,0:T(2,128)(2,1)S(1)}, u32[]{:S(2)}, u32[]{:S(2)}) async-start(bf16[128,2,768]{2,1,0:T(2,128)(2,1)} %all_to_all.27), calls=%async_computation.1 | async-start | bytes 786432 | tf_op jit(solution)/shard_map/all_to_all | solution.py:39
  36.1 64.2 %all-gather.6.cloned.1.call-start = ((), (), s32[]{:S(2)}) async-start(), calls=%async_computation.3 | async-start | bytes 6488064 | tf_op jit(solution)/shard_map/all_gather | solution.py:43
  50.7 139.2 %all-gather.8.cloned.1.call-start = ((), (), s32[]{:S(2)}) async-start(), calls=%async_computation.4 | async-start | bytes 25952256 | tf_op jit(solution)/shard_map/all_gather | solution.py:61
  106.2 3.6 copy-start.1
  106.2 83.7 %copy-start.3 = (bf16[128,768]{1,0:T(8,128)(2,1)S(1)}, bf16[128,768]{1,0:T(8,128)(2,1)}, u32[]{:S(2)}) copy-start(bf16[128,768]{1,0:T(8,128)(2,1)} %scatter_custom_fusion.2) | copy-start | bytes 589828
  215.7 19.9 %all-to-all-start.2 = ((bf16[128,2,768]{2,1,0:T(2,128)(2,1)}), bf16[128,2,768]{2,1,0:T(2,128)(2,1)}, u32[]{:S(2)}, u32[]{:S(2)}) async-start(bf16[128,2,768]{2,1,0:T(2,128)(2,1)} %all_to_all.30), calls=%async_computation.2 | async-start | bytes 786432 | tf_op jit(solution)/shard_map/all_to_all | solution.py:71
  223.4 172.9 %all-reduce.2.cloned.1.call-start = ((), (), s32[]{:S(2)}) async-start(), calls=%async_computation.5 | async-start | bytes 4718592 | tf_op jit(solution)/shard_map/psum | solution.py:80
  223.4 11.3 %copy-start.4 = (bf16[512,768]{1,0:T(8,128)(2,1)S(1)}, bf16[512,768]{1,0:T(8,128)(2,1)}, u32[]{:S(2)}) copy-start(bf16[512,768]{1,0:T(8,128)(2,1)} %param.8) | copy-start | bytes 2359300
  233.9 0.9 copy-start.2
Sparse Core Ops, SparseCore 0:
  50.8 45.5 all-gather.5
  99.2 90.6 all-gather.7
  243.3 153.0 all-reduce.1
where the time goes:
time: 407 us
  waiting for transfers between devices  219 us (54%)
  blocking collectives  69.3 us (17%)
  matrix products  52.8 us (13%)
  starting transfers between devices  23.7 us (6%)
  local copies, waits for them, and re-layouts  20 us (5%)
  between operations  14 us (3%)
  other arithmetic  7.92 us (2%)
    psum x1, waiting for transfers between devices, shards(): grad_weight = lax.psum(local_weight, ('group', 'member')) / devices  148 us
    all_gather x1, waiting for transfers between devices, shards(): piece = lax.all_gather(query_emb, 'member', axis=0, tiled=True)  53.8 us
    dot_general x7, matrix products, contract(): lax.dot_general(left, right, (((left_dim,), (right_dim,)), ((), ())), pre...  38.3 us
    all_gather x1, blocking collectives, shards(): lax.all_gather(positive, 'member', axis=0, tiled=True)  23.5 us
    all_gather x1, blocking collectives, shards(): lax.all_gather(loss_weight, 'member', axis=0, tiled=True)  23.2 us
    all_gather x1, blocking collectives, shards(): lax.all_gather(lse, 'member', axis=0, tiled=True)  22.6 us
    all_to_all x1, starting transfers between devices, shards(): lax.all_to_all(send_slots, ('group', 'member'), split_axis=0, concat_axis...  11.5 us
    all_to_all x1, waiting for transfers between devices, shards(): lax.all_to_all(send_rows, ('group', 'member'), split_axis=0, concat_axis=...  10.6 us
  transfers between devices with their start and end apart: 6, of which 4 were waited for; matrix products, arithmetic and copies ran while one was open for 8% of the time, Pallas kernels for 0%

commit v1 on v0

--- a/solution.py
+++ b/solution.py
@@ -33,14 +33,17 @@
     earlier_same = (owner[:, None] == owner[None, :]) & (order[:, None] > order[None, :])
     rank = jnp.sum(earlier_same.astype(jnp.int32), axis=1)
     position = owner * capacity + rank
-    send_rows = jnp.zeros((devices * capacity, width), jnp.bfloat16).at[position].set(passage_emb)
+    both = jnp.concatenate([passage_emb, passage_hidden], axis=1)
+    send_rows = jnp.zeros((devices * capacity, 2 * width), jnp.bfloat16).at[position].set(both)
     send_slots = jnp.full((devices * capacity,), rows, jnp.int32).at[position].set(slot)
     got_rows, got_slots = (
         lax.all_to_all(send_rows, ("group", "member"), split_axis=0, concat_axis=0, tiled=True),
         lax.all_to_all(send_slots, ("group", "member"), split_axis=0, concat_axis=0, tiled=True),
     )
-    relaid = jnp.zeros((rows, width), jnp.bfloat16).at[got_slots].set(got_rows, mode="drop")
-    group_passages = lax.all_gather(relaid, "member", axis=0, tiled=True)
+    relaid = jnp.zeros((rows, 2 * width), jnp.bfloat16).at[got_slots].set(got_rows, mode="drop")
+    group_both = lax.all_gather(relaid, "member", axis=0, tiled=True)
+    group_passages = group_both[:, :width]
+    group_hidden = group_both[:, width:]
     scores = contract(query_emb, group_passages, 1, 1) * factor
     top = jnp.max(scores, axis=1, keepdims=True)
     lse = top[:, 0] + jnp.log(jnp.sum(jnp.exp(scores - top), axis=1))
@@ -52,21 +55,17 @@
     query_grad = jnp.dot(coef, group_passages, preferred_element_type=jnp.float32).astype(
         jnp.bfloat16
     )
-    own_columns = lax.axis_index("member") * rows + order
-    group_lse, group_weight, group_target = (
-        lax.all_gather(lse, "member", axis=0, tiled=True),
-        lax.all_gather(loss_weight, "member", axis=0, tiled=True),
-        lax.all_gather(positive, "member", axis=0, tiled=True),
+    partial = contract(coef, query_emb, 0, 0)
+    local_weight = contract(query_hidden, query_grad, 0, 0) + contract(group_hidden, partial, 0, 0)
+    grad_weight = lax.psum(local_weight, ("group", "member")) / devices
+    pieces = lax.all_to_all(
+        partial.astype(jnp.bfloat16).reshape(members, rows, width),
+        "member",
+        split_axis=0,
+        concat_axis=0,
+        tiled=True,
     )
-    piece = lax.all_gather(query_emb, "member", axis=0, tiled=True)
-    part_scores = contract(piece, relaid, 1, 1) * factor
-    part_hit = own_columns[None, :] == group_target[:, None]
-    part_coef = (
-        group_weight[:, None]
-        * (jnp.exp(part_scores - group_lse[:, None]) - part_hit.astype(jnp.float32))
-        * factor
-    ).astype(jnp.bfloat16)
-    relaid_grad = contract(part_coef, piece, 0, 0).astype(jnp.bfloat16)
+    relaid_grad = jnp.sum(pieces.astype(jnp.float32), axis=0).astype(jnp.bfloat16)
     back_rows = relaid_grad[jnp.minimum(got_slots, rows - 1)]
     returned = lax.all_to_all(
         back_rows, ("group", "member"), split_axis=0, concat_axis=0, tiled=True
@@ -74,10 +73,6 @@
     passage_grad = returned[position]
     grad_passage_hidden = contract(passage_grad, proj_weight, 1, 1).astype(jnp.bfloat16)
     grad_query_hidden = contract(query_grad, proj_weight, 1, 1).astype(jnp.bfloat16)
-    local_weight = contract(passage_hidden, passage_grad, 0, 0) + contract(
-        query_hidden, query_grad, 0, 0
-    )
-    grad_weight = lax.psum(local_weight, ("group", "member")) / devices
     return (loss, grad_query_hidden, grad_passage_hidden, grad_weight)
 
 

time: 407 us -> 362 us (0.89)
  blocking collectives: 69.3 us -> 0 us
  waiting for transfers between devices: 219 us -> 247 us
  matrix products: 52.8 us -> 34.5 us
  starting transfers between devices: 23.7 us -> 36 us
  other arithmetic: 7.92 us -> 17.6 us
  local copies, waits for them, and re-layouts: 20 us -> 12.4 us
    all_gather x3 -> x0, blocking collectives: 69.3 us -> none  [the longest x1 23.5 us: shards(): lax.all_gather(positive, 'member', axis=0, tiled=True)]
    all_to_all x0 -> x1, waiting for transfers between devices: none -> 60.8 us  [shards(): lax.all_to_all(partial.astype(jnp.bfloat16).reshape(members, rows, width)...]
    psum x1, waiting for transfers between devices: 148 us -> 107 us  [shards(): grad_weight = lax.psum(local_weight, ('group', 'member')) / devices]
    dot_general x7 -> x6, matrix products: 38.3 us -> 24.8 us  [contract(): lax.dot_general(left, right, (((left_dim,), (right_dim,)), ((), ())), pre...]
    all_to_all x1, starting transfers between devices: 7.72 us -> 14.2 us  [shards(): lax.all_to_all(back_rows, ('group', 'member'), split_axis=0, concat_axis=...]
    all_to_all x0 -> x1, starting transfers between devices: none -> 5.49 us  [shards(): lax.all_to_all(partial.astype(jnp.bfloat16).reshape(members, rows, width)...]
    all_gather x2 -> x1, waiting for transfers between devices: 53.8 us -> 58.7 us  [shards(): group_both = lax.all_gather(relaid, 'member', axis=0, tiled=True)]
    unnamed x15 -> x13, local copies, waits for them, and re-layouts: 6.45 us -> 1.99 us
  transfers between devices with their start and end apart: 6 -> 6, of which waited for: 4 -> 5; matrix products, arithmetic and copies ran while one was open for 8% -> 9% of each run, Pallas kernels for 0% -> 0%
where the time goes in v1:
time: 362 us; the launch traced here: 361 us
  waiting for transfers between devices  247 us (68%)
  starting transfers between devices  36 us (10%)
  matrix products  34.5 us (10%)
  other arithmetic  17.6 us (5%)
  between operations  14.3 us (4%)
  local copies, waits for them, and re-layouts  12.4 us (3%)
    psum x1, waiting for transfers between devices, shards(): grad_weight = lax.psum(local_weight, ('group', 'member')) / devices  107 us
    all_to_all x1, waiting for transfers between devices, shards(): lax.all_to_all(partial.astype(jnp.bfloat16).reshape(members, rows, width)...  60.8 us
    all_gather x1, waiting for transfers between devices, shards(): group_both = lax.all_gather(relaid, 'member', axis=0, tiled=True)  58.7 us
    dot_general x6, matrix products, contract(): lax.dot_general(left, right, (((left_dim,), (right_dim,)), ((), ())), pre...  24.8 us
    all_to_all x1, waiting for transfers between devices, shards(): lax.all_to_all(send_rows, ('group', 'member'), split_axis=0, concat_axis=...  14.7 us
    all_to_all x1, starting transfers between devices, shards(): lax.all_to_all(back_rows, ('group', 'member'), split_axis=0, concat_axis=...  14.2 us
    all_to_all x1, starting transfers between devices, shards(): lax.all_to_all(send_slots, ('group', 'member'), split_axis=0, concat_axis...  11.5 us
    dot_general x1, matrix products, shards(): jnp.dot(coef, group_passages, preferred_element_type=jnp.float32)  7.61 us
  transfers between devices with their start and end apart: 6, of which 5 were waited for; matrix products, arithmetic and copies ran while one was open for 9% of the time, Pallas kernels for 0%

profile of v1, /device:TPU:1, one launch (start us, length us, event | category | flops | bytes accessed | tf_op | source)
XLA Modules:
  0.0 361.5 jit_solution(6530808918512203172)
XLA Ops:
  7.2 0.0 copy-start
  7.2 0.8 and_select_fusion
  8.0 0.7 and_select_fusion.1
  8.7 0.2 convert_reduce_fusion
  8.9 1.0 scatter_custom_fusion
  9.9 0.8 all_to_all.27
  10.6 11.5 %all-to-all-start = ((s32[128,2,1]{1,2,0:T(1,128)}), s32[128,2,1]{1,2,0:T(1,128)S(1)}, u32[]{:S(2)}, u32[]{:S(2)}) async-start(s32[128,2,1]{1,2,0:T(1,128)} %bitcast), calls=%async_computation | async-start | bytes 131072 | tf_op jit(solution)/shard_map/all_to_all | solution.py:41
  22.1 1.3 convolution_convert_fusion.3
  23.4 1.9 scatter_custom_fusion.1
  25.3 1.2 all_to_all.30
  26.4 5.3 %all-to-all-done = s32[128,2,1]{1,2,0:T(1,128)S(1)} async-done(((s32[128,2,1]{1,2,0:T(1,128)}), s32[128,2,1]{1,2,0:T(1,128)S(1)}, u32[]{:S(2)}, u32[]{:S(2)}) %all-to-all-start) | async-done | bytes 1056 | tf_op jit(solution)/shard_map/all_to_all | solution.py:41
  31.7 4.5 %all-to-all-start.1 = ((bf16[128,2,1536]{2,1,0:T(2,128)(2,1)}), bf16[128,2,1536]{2,1,0:T(2,128)(2,1)S(1)}, u32[]{:S(2)}, u32[]{:S(2)}) async-start(bf16[128,2,1536]{2,1,0:T(2,128)(2,1)} %all_to_all.30), calls=%async_computation.1 | async-start | bytes 1572864 | tf_op jit(solution)/shard_map/all_to_all | solution.py:40
  36.2 0.0 all-gather.2.cloned.1.call-start
  36.3 0.5 broadcast.104
  36.8 0.8 reduce.4
  37.6 0.1 all_to_all.29
  37.7 14.7 %all-to-all-done.1 = bf16[128,2,1536]{2,1,0:T(2,128)(2,1)S(1)} async-done(((bf16[128,2,1536]{2,1,0:T(2,128)(2,1)}), bf16[128,2,1536]{2,1,0:T(2,128)(2,1)S(1)}, u32[]{:S(2)}, u32[]{:S(2)}) %all-to-all-start.1) | async-done | bytes 786464 | tf_op jit(solution)/shard_map/all_to_all | solution.py:40
  52.4 0.3 reshape.112
  52.7 2.5 scatter_custom_fusion.2
  55.2 0.0 all-gather.2.cloned.1.call-update
  55.2 0.8 convolution_convert_fusion.1
  56.0 0.0 copy-start.4
  56.0 58.7 %all-gather.2.cloned.1.call-done = bf16[4096,1536]{1,0:T(8,128)(2,1)} async-done(((bf16[128,1536]{1,0:T(8,128)(2,1)}), bf16[4096,1536]{1,0:T(8,128)(2,1)}) %all-gather.2.cloned.1.call-update) | async-done | bytes 12582928 | tf_op jit(solution)/shard_map/all_gather | solution.py:44
  114.8 5.7 %multiply_reduce_fusion = (f32[512]{0:T(512)S(1)}, f32[512,4096]{1,0:T(8,128)S(1)}) fusion(bf16[512,768]{1,0:T(8,128)(2,1)S(1)} %convolution_convert_fusion.1, bf16[4096,1536]{1,0:T(8,128)(2,1)} %all-gather.2.cloned.1.call-done), kind=kOutput, calls=%fused_computation.9 | convolution fusion | flops 3225419264 | bytes 15468544 | tf_op jit(solution)/shard_map/dot_general | solution.py:10
  120.5 0.0 copy-start.5
  120.5 3.1 select_reduce_fusion
  123.6 0.6 fusion.19
  124.2 3.9 %multiply_convert_fusion = bf16[512,4096]{1,0:T(8,128)(2,1)S(1)} fusion(f32[512,4096]{1,0:T(8,128)S(1)} %get-tuple-element.29, f32[512]{0:T(512)S(1)} %get-tuple-element.23, f32[512]{0:T(512)S(1)} %copy-done.5, s32[512]{0:T(512)S(1)} %copy-done.4), kind=kLoop, calls=%fused_computation.5 | loop fusion | flops 16777216 | bytes 12589056 | tf_op jit(solution)/shard_map/convert_element_type | solution.py:54
  128.1 5.4 %fusion.20 = bf16[4096,768]{1,0:T(8,128)(2,1)} fusion(bf16[512,4096]{1,0:T(8,128)(2,1)S(1)} %multiply_convert_fusion, bf16[512,768]{1,0:T(8,128)(2,1)S(1)} %convolution_convert_fusion.1), kind=kOutput, calls=%fused_computation.48 | convolution fusion | flops 3221225472 | bytes 11272192 | tf_op jit(solution)/shard_map/dot_general | solution.py:10
  133.5 5.5 %all-to-all-start.2 = ((bf16[32,128,768]{2,1,0:T(8,128)(2,1)}), bf16[32,128,768]{2,1,0:T(8,128)(2,1)}, u32[]{:S(2)}, u32[]{:S(2)}) async-start(bf16[32,128,768]{2,1,0:T(8,128)(2,1)} %bitcast.25), calls=%async_computation.2 | async-start | bytes 12582912 | tf_op jit(solution)/shard_map/all_to_all | solution.py:61
  139.0 0.3 all-reduce.2.cloned.1.call-start
  139.3 7.6 %fusion.6 = bf16[512,768]{1,0:T(8,128)(2,1)S(1)} fusion(bf16[512,4096]{1,0:T(8,128)(2,1)} %copy-done.2, bf16[4096,1536]{1,0:T(8,128)(2,1)} %all-gather.2.cloned.1.call-done), kind=kOutput, calls=%fused_computation.19 | convolution fusion | flops 3221618688 | bytes 11272192 | tf_op jit(solution)/shard_map/dot_general | solution.py:55
  146.9 8.5 %fusion = f32[768,768]{0,1:T(8,128)S(1)} fusion(bf16[4096,768]{1,0:T(8,128)(2,1)S(1)} %copy-done.1, bf16[4096,1536]{1,0:T(8,128)(2,1)} %all-gather.2.cloned.1.call-done), kind=kOutput, calls=%fused_computation.10 | convolution fusion | flops 4831838208 | bytes 14942208 | tf_op jit(solution)/shard_map/dot_general | solution.py:10
  155.5 2.2 bitcast_add_fusion
  157.7 0.0 all-reduce.2.cloned.1.call-update
  157.8 60.8 %all-to-all-done.2 = bf16[32,128,768]{2,1,0:T(8,128)(2,1)} async-done(((bf16[32,128,768]{2,1,0:T(8,128)(2,1)}), bf16[32,128,768]{2,1,0:T(8,128)(2,1)}, u32[]{:S(2)}, u32[]{:S(2)}) %all-to-all-start.2) | async-done | bytes 6291488 | tf_op jit(solution)/shard_map/all_to_all | solution.py:61
  218.5 3.8 %reduce_sum.42 = bf16[128,768]{1,0:T(8,128)(2,1)S(1)} reduce(bf16[32,128,768]{2,1,0:T(8,128)(2,1)} %all-to-all-done.2, bf16[]{:T(256)} %constant.20.clone.1), dimensions={0}, to_apply=%region_7.8 | reduce | flops 3047424 | bytes 6488066 | tf_op jit(solution)/shard_map/reduce_sum | solution.py:68
  222.3 1.2 gather_fusion
  223.5 0.9 all_to_all.34
  224.4 14.2 %all-to-all-start.3 = ((bf16[128,2,768]{2,1,0:T(2,128)(2,1)}), bf16[128,2,768]{2,1,0:T(2,128)(2,1)}, u32[]{:S(2)}, u32[]{:S(2)}) async-start(bf16[128,2,768]{2,1,0:T(2,128)(2,1)} %all_to_all.34), calls=%async_computation.3 | async-start | bytes 786432 | tf_op jit(solution)/shard_map/all_to_all | solution.py:70
  238.6 1.7 convolution_convert_fusion
  240.3 107.3 %all-reduce.2.cloned.1.call-done = f32[768,768]{0,1:T(8,128)} async-done(((f32[768,768]{0,1:T(8,128)}), f32[768,768]{0,1:T(8,128)}) %all-reduce.2.cloned.1.call-update) | async-done | bytes 2359312 | tf_op jit(solution)/shard_map/psum | solution.py:60
  347.6 1.8 broadcast_multiply_fusion
  349.5 2.0 copy.20
  351.4 0.0 all-to-all-done.3
  351.4 1.1 all_to_all.36
  352.6 0.9 gather_fusion.1
  353.4 1.2 convolution_convert_fusion.2
  (13 shorter events, 0.0 us)
Async XLA Ops:
  7.2 15.0 %copy-start = (bf16[768,768]{1,0:T(8,128)(2,1)S(1)}, bf16[768,768]{1,0:T(8,128)(2,1)}, u32[]{:S(2)}) copy-start(bf16[768,768]{1,0:T(8,128)(2,1)} %param.9) | copy-start | bytes 3538948
  7.2 48.0 %copy-start.3 = (bf16[512,768]{1,0:T(8,128)(2,1)S(1)}, bf16[512,768]{1,0:T(8,128)(2,1)}, u32[]{:S(2)}) copy-start(bf16[512,768]{1,0:T(8,128)(2,1)} %param.8) | copy-start | bytes 2359300
  10.6 21.1 %all-to-all-start = ((s32[128,2,1]{1,2,0:T(1,128)}), s32[128,2,1]{1,2,0:T(1,128)S(1)}, u32[]{:S(2)}, u32[]{:S(2)}) async-start(s32[128,2,1]{1,2,0:T(1,128)} %bitcast), calls=%async_computation | async-start | bytes 131072 | tf_op jit(solution)/shard_map/all_to_all | solution.py:41
  31.7 20.7 %all-to-all-start.1 = ((bf16[128,2,1536]{2,1,0:T(2,128)(2,1)}), bf16[128,2,1536]{2,1,0:T(2,128)(2,1)S(1)}, u32[]{:S(2)}, u32[]{:S(2)}) async-start(bf16[128,2,1536]{2,1,0:T(2,128)(2,1)} %all_to_all.30), calls=%async_computation.1 | async-start | bytes 1572864 | tf_op jit(solution)/shard_map/all_to_all | solution.py:40
  36.2 78.5 %all-gather.2.cloned.1.call-start = ((), (), s32[]{:S(2)}) async-start(), calls=%async_computation.4 | async-start | bytes 12976128 | tf_op jit(solution)/shard_map/all_gather | solution.py:44
  56.0 64.5 %copy-start.4 = (s32[512]{0:T(512)S(1)}, s32[512]{0:T(512)}, u32[]{:S(2)}) copy-start(s32[512]{0:T(512)} %param.12) | copy-start | bytes 6148
  120.5 3.7 %copy-start.5 = (f32[512]{0:T(512)S(1)}, f32[512]{0:T(512)}, u32[]{:S(2)}) copy-start(f32[512]{0:T(512)} %param.13) | copy-start | bytes 6148
  128.1 5.4 %copy-start.2 = (bf16[512,4096]{1,0:T(8,128)(2,1)}, bf16[512,4096]{1,0:T(8,128)(2,1)S(1)}, u32[]{:S(2)}) copy-start(bf16[512,4096]{1,0:T(8,128)(2,1)S(1)} %multiply_convert_fusion) | copy-start | bytes 12582916
  133.5 85.0 %all-to-all-start.2 = ((bf16[32,128,768]{2,1,0:T(8,128)(2,1)}), bf16[32,128,768]{2,1,0:T(8,128)(2,1)}, u32[]{:S(2)}, u32[]{:S(2)}) async-start(bf16[32,128,768]{2,1,0:T(8,128)(2,1)} %bitcast.25), calls=%async_computation.2 | async-start | bytes 12582912 | tf_op jit(solution)/shard_map/all_to_all | solution.py:61
  139.0 208.6 %all-reduce.2.cloned.1.call-start = ((), (), s32[]{:S(2)}) async-start(), calls=%async_computation.5 | async-start | bytes 4718592 | tf_op jit(solution)/shard_map/psum | solution.py:60
  139.3 7.6 %copy-start.1 = (bf16[4096,768]{1,0:T(8,128)(2,1)S(1)}, bf16[4096,768]{1,0:T(8,128)(2,1)}, u32[]{:S(2)}) copy-start(bf16[4096,768]{1,0:T(8,128)(2,1)} %fusion.20) | copy-start | bytes 18874372
  224.4 127.0 %all-to-all-start.3 = ((bf16[128,2,768]{2,1,0:T(2,128)(2,1)}), bf16[128,2,768]{2,1,0:T(2,128)(2,1)}, u32[]{:S(2)}, u32[]{:S(2)}) async-start(bf16[128,2,768]{2,1,0:T(2,128)(2,1)} %all_to_all.34), calls=%async_computation.3 | async-start | bytes 786432 | tf_op jit(solution)/shard_map/all_to_all | solution.py:70
Sparse Core Ops, SparseCore 0:
  55.3 59.3 all-gather.1
  157.9 189.7 all-reduce.1

commit v2 on v1

--- a/solution.py
+++ b/solution.py
@@ -57,7 +57,12 @@
     )
     partial = contract(coef, query_emb, 0, 0)
     local_weight = contract(query_hidden, query_grad, 0, 0) + contract(group_hidden, partial, 0, 0)
-    grad_weight = lax.psum(local_weight, ("group", "member")) / devices
+    weight_rows = width // members
+    weight_pieces = lax.all_to_all(
+        local_weight.reshape(members, weight_rows, width), "member", 0, 0, tiled=True
+    )
+    weight_share = lax.psum(jnp.sum(weight_pieces, axis=0), "group")
+    grad_weight = lax.all_gather(weight_share, "member", axis=0, tiled=True) / devices
     pieces = lax.all_to_all(
         partial.astype(jnp.bfloat16).reshape(members, rows, width),
         "member",

time: 362 us -> 308 us (0.85)
  waiting for transfers between devices: 247 us -> 166 us
  blocking collectives: 0 us -> 36.7 us
  matrix products: 34.5 us -> 24.4 us
    psum x1, waiting for transfers between devices: 107 us -> 42.9 us  [shards(): weight_share = lax.psum(jnp.sum(weight_pieces, axis=0), 'group')]
    all_to_all x0 -> x1, blocking collectives: none -> 36.7 us  [shards(): lax.all_to_all(local_weight.reshape(members, weight_rows, width), 'member...]
    all_to_all x1, waiting for transfers between devices: 60.8 us -> 34.4 us  [shards(): lax.all_to_all(partial.astype(jnp.bfloat16).reshape(members, rows, width)...]
    all_to_all x1, waiting for transfers between devices: 0.01 us -> 10.5 us  [shards(): lax.all_to_all(back_rows, ('group', 'member'), split_axis=0, concat_axis=...]
    dot_general x6, matrix products: 24.8 us -> 18.9 us  [contract(): lax.dot_general(left, right, (((left_dim,), (right_dim,)), ((), ())), pre...]
    dot_general x1, matrix products: 7.61 us -> 3.46 us  [shards(): jnp.dot(coef, group_passages, preferred_element_type=jnp.float32)]
  transfers between devices with their start and end apart: 6 -> 7, of which waited for: 5 -> 6; matrix products, arithmetic and copies ran while one was open for 9% -> 5% of each run, Pallas kernels for 0% -> 0%
where the time goes in v2:
time: 308 us; the launch traced here: 307 us
  waiting for transfers between devices  166 us (54%)
  blocking collectives  36.7 us (12%)
  starting transfers between devices  36.3 us (12%)
  matrix products  24.4 us (8%)
  other arithmetic  19.7 us (6%)
  between operations  14.1 us (5%)
  local copies, waits for them, and re-layouts  9.5 us (3%)
    all_gather x1, waiting for transfers between devices, shards(): group_both = lax.all_gather(relaid, 'member', axis=0, tiled=True)  58.7 us
    psum x1, waiting for transfers between devices, shards(): weight_share = lax.psum(jnp.sum(weight_pieces, axis=0), 'group')  42.9 us
    all_to_all x1, blocking collectives, shards(): lax.all_to_all(local_weight.reshape(members, weight_rows, width), 'member...  36.7 us
    all_to_all x1, waiting for transfers between devices, shards(): lax.all_to_all(partial.astype(jnp.bfloat16).reshape(members, rows, width)...  34.4 us
    dot_general x6, matrix products, contract(): lax.dot_general(left, right, (((left_dim,), (right_dim,)), ((), ())), pre...  18.9 us
    all_to_all x1, starting transfers between devices, shards(): lax.all_to_all(back_rows, ('group', 'member'), split_axis=0, concat_axis=...  15.5 us
    all_to_all x1, waiting for transfers between devices, shards(): lax.all_to_all(send_rows, ('group', 'member'), split_axis=0, concat_axis=...  14.7 us
    all_to_all x1, starting transfers between devices, shards(): lax.all_to_all(send_slots, ('group', 'member'), split_axis=0, concat_axis...  11.5 us
  transfers between devices with their start and end apart: 7, of which 6 were waited for; matrix products, arithmetic and copies ran while one was open for 5% of the time, Pallas kernels for 0%

profile of v2, /device:TPU:1, one launch (start us, length us, event | category | flops | bytes accessed | tf_op | source)
XLA Modules:
  0.0 307.0 jit_solution(11621493822044809868)
XLA Ops:
  7.2 0.8 and_select_fusion
  8.0 0.7 and_select_fusion.1
  8.7 0.2 convert_reduce_fusion
  8.9 1.0 scatter_custom_fusion
  9.9 0.8 all_to_all.30
  10.6 11.5 %all-to-all-start = ((s32[128,2,1]{1,2,0:T(1,128)}), s32[128,2,1]{1,2,0:T(1,128)S(1)}, u32[]{:S(2)}, u32[]{:S(2)}) async-start(s32[128,2,1]{1,2,0:T(1,128)} %bitcast), calls=%async_computation | async-start | bytes 131072 | tf_op jit(solution)/shard_map/all_to_all | solution.py:41
  22.1 1.3 convolution_convert_fusion.3
  23.4 1.9 scatter_custom_fusion.1
  25.3 1.2 all_to_all.33
  26.4 5.3 %all-to-all-done = s32[128,2,1]{1,2,0:T(1,128)S(1)} async-done(((s32[128,2,1]{1,2,0:T(1,128)}), s32[128,2,1]{1,2,0:T(1,128)S(1)}, u32[]{:S(2)}, u32[]{:S(2)}) %all-to-all-start) | async-done | bytes 1056 | tf_op jit(solution)/shard_map/all_to_all | solution.py:41
  31.7 4.5 %all-to-all-start.1 = ((bf16[128,2,1536]{2,1,0:T(2,128)(2,1)}), bf16[128,2,1536]{2,1,0:T(2,128)(2,1)S(1)}, u32[]{:S(2)}, u32[]{:S(2)}) async-start(bf16[128,2,1536]{2,1,0:T(2,128)(2,1)} %all_to_all.33), calls=%async_computation.1 | async-start | bytes 1572864 | tf_op jit(solution)/shard_map/all_to_all | solution.py:40
  36.2 0.0 all-gather.3.cloned.1.call-start
  36.3 0.5 broadcast.104
  36.8 0.8 reduce.4
  37.6 0.1 all_to_all.32
  37.7 14.7 %all-to-all-done.1 = bf16[128,2,1536]{2,1,0:T(2,128)(2,1)S(1)} async-done(((bf16[128,2,1536]{2,1,0:T(2,128)(2,1)}), bf16[128,2,1536]{2,1,0:T(2,128)(2,1)S(1)}, u32[]{:S(2)}, u32[]{:S(2)}) %all-to-all-start.1) | async-done | bytes 786464 | tf_op jit(solution)/shard_map/all_to_all | solution.py:40
  52.4 0.3 reshape.116
  52.7 2.5 scatter_custom_fusion.2
  55.2 0.0 all-gather.3.cloned.1.call-update
  55.2 0.8 convolution_convert_fusion.1
  56.0 58.7 %all-gather.3.cloned.1.call-done = bf16[4096,1536]{1,0:T(8,128)(2,1)} async-done(((bf16[128,1536]{1,0:T(8,128)(2,1)}), bf16[4096,1536]{1,0:T(8,128)(2,1)}) %all-gather.3.cloned.1.call-update) | async-done | bytes 12582928 | tf_op jit(solution)/shard_map/all_gather | solution.py:44
  114.8 5.7 %multiply_reduce_fusion = (f32[512]{0:T(512)S(1)}, f32[512,4096]{1,0:T(8,128)S(1)}) fusion(bf16[512,768]{1,0:T(8,128)(2,1)S(1)} %convolution_convert_fusion.1, bf16[4096,1536]{1,0:T(8,128)(2,1)} %all-gather.3.cloned.1.call-done), kind=kOutput, calls=%fused_computation.9 | convolution fusion | flops 3225419264 | bytes 15468544 | tf_op jit(solution)/shard_map/dot_general | solution.py:10
  120.5 3.1 %select_reduce_fusion = (f32[512]{0:T(512)S(1)}, f32[512]{0:T(512)S(1)}) fusion(f32[512,4096]{1,0:T(8,128)S(1)} %get-tuple-element.13, s32[512]{0:T(512)S(1)} %copy-done.5, f32[512]{0:T(512)S(1)} %get-tuple-element.12), kind=kLoop, calls=%fused_computation.6 | loop fusion | flops 12581888 | bytes 8396800 | tf_op jit(solution)/shard_map/reduce_sum | solution.py:51
  123.6 0.6 fusion.19
  124.2 3.9 %multiply_convert_fusion = bf16[512,4096]{1,0:T(8,128)(2,1)S(1)} fusion(f32[512,4096]{1,0:T(8,128)S(1)} %get-tuple-element.13, f32[512]{0:T(512)S(1)} %get-tuple-element.7, f32[512]{0:T(512)S(1)} %copy-done.6, s32[512]{0:T(512)S(1)} %copy-done.5), kind=kLoop, calls=%fused_computation.5 | loop fusion | flops 16777216 | bytes 12589056 | tf_op jit(solution)/shard_map/convert_element_type | solution.py:54
  128.1 4.0 %fusion.20 = bf16[4096,768]{1,0:T(8,128)(2,1)S(1)} fusion(bf16[512,4096]{1,0:T(8,128)(2,1)S(1)} %multiply_convert_fusion, bf16[512,768]{1,0:T(8,128)(2,1)S(1)} %convolution_convert_fusion.1), kind=kOutput, calls=%fused_computation.48 | convolution fusion | flops 3221225472 | bytes 11272192 | tf_op jit(solution)/shard_map/dot_general | solution.py:10
  132.2 3.5 %fusion.6 = bf16[512,768]{1,0:T(8,128)(2,1)S(1)} fusion(bf16[512,4096]{1,0:T(8,128)(2,1)S(1)} %multiply_convert_fusion, bf16[4096,1536]{1,0:T(8,128)(2,1)S(1)} %bitcast.31), kind=kOutput, calls=%fused_computation.19 | convolution fusion | flops 3221618688 | bytes 11272192 | tf_op jit(solution)/shard_map/dot_general | solution.py:55
  135.7 5.4 %fusion = f32[768,768]{1,0:T(8,128)S(1)} fusion(bf16[4096,768]{1,0:T(8,128)(2,1)S(1)} %fusion.20, bf16[4096,1536]{1,0:T(8,128)(2,1)S(1)} %bitcast.31), kind=kOutput, calls=%fused_computation.10 | convolution fusion | flops 4831838208 | bytes 14942208 | tf_op jit(solution)/shard_map/dot_general | solution.py:10
  141.1 0.9 bitcast_add_fusion
  142.0 36.7 %all_to_all.46 = f32[32,24,768]{2,1,0:T(8,128)S(1)} all-to-all(f32[32,24,768]{2,1,0:T(8,128)S(1)} %bitcast.26), channel_id=1, replica_groups=mesh['group'=4,'member'=32] {'member'}, dimensions={0} | all-to-all | bytes 4718592 | tf_op jit(solution)/shard_map/all_to_all | solution.py:61
  178.7 4.7 %all-to-all-start.2 = ((bf16[32,128,768]{2,1,0:T(8,128)(2,1)}), bf16[32,128,768]{2,1,0:T(8,128)(2,1)}, u32[]{:S(2)}, u32[]{:S(2)}) async-start(bf16[32,128,768]{2,1,0:T(8,128)(2,1)} %bitcast.27), calls=%async_computation.2 | async-start | bytes 12582912 | tf_op jit(solution)/shard_map/all_to_all | solution.py:66
  183.4 0.0 all-reduce.2.cloned.1.call-start
  183.4 0.8 reduce_sum.52
  184.2 0.0 all-reduce.2.cloned.1.call-update
  184.2 0.0 all-gather.5.cloned.1.call-start
  184.2 42.9 %all-reduce.2.cloned.1.call-done = f32[24,768]{1,0:T(8,128)} async-done(((f32[24,768]{1,0:T(8,128)}), f32[24,768]{1,0:T(8,128)}) %all-reduce.2.cloned.1.call-update) | async-done | bytes 73744 | tf_op jit(solution)/shard_map/psum | solution.py:64
  227.1 0.0 all-gather.5.cloned.1.call-update
  227.2 34.4 %all-to-all-done.2 = bf16[32,128,768]{2,1,0:T(8,128)(2,1)} async-done(((bf16[32,128,768]{2,1,0:T(8,128)(2,1)}), bf16[32,128,768]{2,1,0:T(8,128)(2,1)}, u32[]{:S(2)}, u32[]{:S(2)}) %all-to-all-start.2) | async-done | bytes 6291488 | tf_op jit(solution)/shard_map/all_to_all | solution.py:66
  261.6 3.7 %reduce_sum.51 = bf16[128,768]{1,0:T(8,128)(2,1)S(1)} reduce(bf16[32,128,768]{2,1,0:T(8,128)(2,1)} %all-to-all-done.2, bf16[]{:T(256)} %constant.20.clone.1), dimensions={0}, to_apply=%region_7.8 | reduce | flops 3047424 | bytes 6488066 | tf_op jit(solution)/shard_map/reduce_sum | solution.py:73
  265.3 1.2 gather_fusion
  266.5 0.9 all_to_all.37
  267.4 15.5 %all-to-all-start.3 = ((bf16[128,2,768]{2,1,0:T(2,128)(2,1)}), bf16[128,2,768]{2,1,0:T(2,128)(2,1)S(1)}, u32[]{:S(2)}, u32[]{:S(2)}) async-start(bf16[128,2,768]{2,1,0:T(2,128)(2,1)} %all_to_all.37), calls=%async_computation.3 | async-start | bytes 786432 | tf_op jit(solution)/shard_map/all_to_all | solution.py:75
  282.9 1.7 convolution_convert_fusion
  284.6 10.5 %all-to-all-done.3 = bf16[128,2,768]{2,1,0:T(2,128)(2,1)S(1)} async-done(((bf16[128,2,768]{2,1,0:T(2,128)(2,1)}), bf16[128,2,768]{2,1,0:T(2,128)(2,1)S(1)}, u32[]{:S(2)}, u32[]{:S(2)}) %all-to-all-start.3) | async-done | bytes 393248 | tf_op jit(solution)/shard_map/all_to_all | solution.py:75
  295.0 0.1 all_to_all.39
  295.2 0.9 gather_fusion.1
  296.0 1.2 convolution_convert_fusion.2
  297.3 3.2 %broadcast_multiply_fusion = f32[768,768]{1,0:T(8,128)} fusion(f32[768,768]{1,0:T(8,128)} %all-gather.5.cloned.1.call-done), kind=kLoop, calls=%fused_computation.20 | loop fusion | flops 589824 | bytes 4718592 | tf_op jit(solution)/shard_map/div | solution.py:65
  (26 shorter events, 0.1 us)
Async XLA Ops:
  7.2 15.0 %copy-start = (bf16[768,768]{1,0:T(8,128)(2,1)S(1)}, bf16[768,768]{1,0:T(8,128)(2,1)}, u32[]{:S(2)}) copy-start(bf16[768,768]{1,0:T(8,128)(2,1)} %param.9) | copy-start | bytes 3538948
  7.2 48.0 %copy-start.2 = (bf16[512,768]{1,0:T(8,128)(2,1)S(1)}, bf16[512,768]{1,0:T(8,128)(2,1)}, u32[]{:S(2)}) copy-start(bf16[512,768]{1,0:T(8,128)(2,1)} %param.8) | copy-start | bytes 2359300
  10.6 21.1 %all-to-all-start = ((s32[128,2,1]{1,2,0:T(1,128)}), s32[128,2,1]{1,2,0:T(1,128)S(1)}, u32[]{:S(2)}, u32[]{:S(2)}) async-start(s32[128,2,1]{1,2,0:T(1,128)} %bitcast), calls=%async_computation | async-start | bytes 131072 | tf_op jit(solution)/shard_map/all_to_all | solution.py:41
  31.7 20.7 %all-to-all-start.1 = ((bf16[128,2,1536]{2,1,0:T(2,128)(2,1)}), bf16[128,2,1536]{2,1,0:T(2,128)(2,1)S(1)}, u32[]{:S(2)}, u32[]{:S(2)}) async-start(bf16[128,2,1536]{2,1,0:T(2,128)(2,1)} %all_to_all.33), calls=%async_computation.1 | async-start | bytes 1572864 | tf_op jit(solution)/shard_map/all_to_all | solution.py:40
  36.2 78.5 %all-gather.3.cloned.1.call-start = ((), (), s32[]{:S(2)}) async-start(), calls=%async_computation.5 | async-start | bytes 12976128 | tf_op jit(solution)/shard_map/all_gather | solution.py:44
  56.0 64.5 %copy-start.5 = (s32[512]{0:T(512)S(1)}, s32[512]{0:T(512)}, u32[]{:S(2)}) copy-start(s32[512]{0:T(512)} %param.12) | copy-start | bytes 6148
  120.5 3.7 %copy-start.6 = (f32[512]{0:T(512)S(1)}, f32[512]{0:T(512)}, u32[]{:S(2)}) copy-start(f32[512]{0:T(512)} %param.13) | copy-start | bytes 6148
  124.2 7.9 %slice-start = ((s8[12582912]{0:T(1024)(128)(4,1)}), s8[4194304]{0:T(1024)(128)(4,1)S(1)}, s32[]{:S(2)}) async-start(s8[12582912]{0:T(1024)(128)(4,1)} %bitcast.30), calls=%async_computation.8 | async-start | bytes 8388608
  124.2 7.9 %slice-start.1 = ((s8[12582912]{0:T(1024)(128)(4,1)}), s8[4194304]{0:T(1024)(128)(4,1)S(1)}, s32[]{:S(2)}) async-start(s8[12582912]{0:T(1024)(128)(4,1)} %bitcast.30), calls=%async_computation.9 | async-start | bytes 8388608
  128.1 4.0 %slice-start.2 = ((s8[12582912]{0:T(1024)(128)(4,1)}), s8[4194304]{0:T(1024)(128)(4,1)S(1)}, s32[]{:S(2)}) async-start(s8[12582912]{0:T(1024)(128)(4,1)} %bitcast.30), calls=%async_computation.10 | async-start | bytes 8388608
  132.2 3.5 %copy-start.1 = (bf16[4096,768]{1,0:T(8,128)(2,1)}, bf16[4096,768]{1,0:T(8,128)(2,1)S(1)}, u32[]{:S(2)}) copy-start(bf16[4096,768]{1,0:T(8,128)(2,1)S(1)} %fusion.20) | copy-start | bytes 18874372
  135.6 5.5 %copy-start.3 = (bf16[512,768]{1,0:T(8,128)(2,1)}, bf16[512,768]{1,0:T(8,128)(2,1)S(1)}, u32[]{:S(2)}) copy-start(bf16[512,768]{1,0:T(8,128)(2,1)S(1)} %fusion.6) | copy-start | bytes 2359300
  178.7 82.9 %all-to-all-start.2 = ((bf16[32,128,768]{2,1,0:T(8,128)(2,1)}), bf16[32,128,768]{2,1,0:T(8,128)(2,1)}, u32[]{:S(2)}, u32[]{:S(2)}) async-start(bf16[32,128,768]{2,1,0:T(8,128)(2,1)} %bitcast.27), calls=%async_computation.2 | async-start | bytes 12582912 | tf_op jit(solution)/shard_map/all_to_all | solution.py:66
  183.4 43.8 %all-reduce.2.cloned.1.call-start = ((), (), s32[]{:S(2)}) async-start(), calls=%async_computation.6 | async-start | bytes 147456 | tf_op jit(solution)/shard_map/psum | solution.py:64
  184.2 98.7 %copy-start.4 = (bf16[512,768]{1,0:T(8,128)(2,1)S(1)}, bf16[512,768]{1,0:T(8,128)(2,1)}, u32[]{:S(2)}) copy-start(bf16[512,768]{1,0:T(8,128)(2,1)} %copy-done.3) | copy-start | bytes 2359300
  184.2 113.1 %all-gather.5.cloned.1.call-start = ((), (), s32[]{:S(2)}) async-start(), calls=%async_computation.7 | async-start | bytes 2433024 | tf_op jit(solution)/shard_map/all_gather | solution.py:65
  267.4 27.6 %all-to-all-start.3 = ((bf16[128,2,768]{2,1,0:T(2,128)(2,1)}), bf16[128,2,768]{2,1,0:T(2,128)(2,1)S(1)}, u32[]{:S(2)}, u32[]{:S(2)}) async-start(bf16[128,2,768]{2,1,0:T(2,128)(2,1)} %all_to_all.37), calls=%async_computation.3 | async-start | bytes 786432 | tf_op jit(solution)/shard_map/all_to_all | solution.py:75
Sparse Core Ops, SparseCore 0:
  55.3 59.3 all-gather.2
  187.1 40.0 all-reduce.1
  229.4 56.8 all-gather.4

commit v3 on v1

--- a/solution.py
+++ b/solution.py
@@ -57,7 +57,10 @@
     )
     partial = contract(coef, query_emb, 0, 0)
     local_weight = contract(query_hidden, query_grad, 0, 0) + contract(group_hidden, partial, 0, 0)
-    grad_weight = lax.psum(local_weight, ("group", "member")) / devices
+    weight_share = lax.psum(
+        lax.psum_scatter(local_weight, "member", scatter_dimension=0, tiled=True), "group"
+    )
+    grad_weight = lax.all_gather(weight_share, "member", axis=0, tiled=True) / devices
     pieces = lax.all_to_all(
         partial.astype(jnp.bfloat16).reshape(members, rows, width),
         "member",

time: 362 us -> 352 us (0.972)
  matrix products: 34.5 us -> 24.6 us
    unnamed x2 -> x5, waiting for transfers between devices: 0.03 us -> 97.9 us
    psum x1, waiting for transfers between devices: 107 us -> 42.6 us  [shards(): lax.psum(lax.psum_scatter(local_weight, 'member', scatter_dimension=0, ti...]
    all_to_all x1, waiting for transfers between devices: 60.8 us -> 0.01 us  [shards(): lax.all_to_all(partial.astype(jnp.bfloat16).reshape(members, rows, width)...]
    all_gather x0 -> x1, waiting for transfers between devices: none -> 16.9 us  [shards(): lax.all_gather(weight_share, 'member', axis=0, tiled=True) / devices]
    all_to_all x1, waiting for transfers between devices: 0.01 us -> 10.7 us  [shards(): lax.all_to_all(back_rows, ('group', 'member'), split_axis=0, concat_axis=...]
    dot_general x6, matrix products: 24.8 us -> 19.1 us  [contract(): lax.dot_general(left, right, (((left_dim,), (right_dim,)), ((), ())), pre...]
    dot_general x1, matrix products: 7.61 us -> 3.46 us  [shards(): jnp.dot(coef, group_passages, preferred_element_type=jnp.float32)]
  transfers between devices with their start and end apart: 6 -> 8, of which waited for: 5 -> 7; matrix products, arithmetic and copies ran while one was open for 9% -> 5% of each run, Pallas kernels for 0% -> 0%
where the time goes in v3:
time: 352 us
  waiting for transfers between devices  247 us (70%)
  starting transfers between devices  32.7 us (9%)
  matrix products  24.6 us (7%)
  other arithmetic  18.9 us (5%)
  local copies, waits for them, and re-layouts  15 us (4%)
  between operations  14.1 us (4%)
    unnamed x5, waiting for transfers between devices  97.9 us
    all_gather x1, waiting for transfers between devices, shards(): group_both = lax.all_gather(relaid, 'member', axis=0, tiled=True)  58.5 us
    psum x1, waiting for transfers between devices, shards(): lax.psum(lax.psum_scatter(local_weight, 'member', scatter_dimension=0, ti...  42.6 us
    dot_general x6, matrix products, contract(): lax.dot_general(left, right, (((left_dim,), (right_dim,)), ((), ())), pre...  19.1 us
    all_gather x1, waiting for transfers between devices, shards(): lax.all_gather(weight_share, 'member', axis=0, tiled=True) / devices  16.9 us
    all_to_all x1, waiting for transfers between devices, shards(): lax.all_to_all(send_rows, ('group', 'member'), split_axis=0, concat_axis=...  14.7 us
    all_to_all x1, starting transfers between devices, shards(): lax.all_to_all(send_slots, ('group', 'member'), split_axis=0, concat_axis...  11.5 us
    all_to_all x1, starting transfers between devices, shards(): lax.all_to_all(back_rows, ('group', 'member'), split_axis=0, concat_axis=...  10.9 us
  transfers between devices with their start and end apart: 8, of which 7 were waited for; matrix products, arithmetic and copies ran while one was open for 5% of the time, Pallas kernels for 0%

profile of v3, /device:TPU:1, one launch (start us, length us, event | category | flops | bytes accessed | tf_op | source)
XLA Modules:
  0.0 351.9 jit_solution(7055950275922341475)
XLA Ops:
  7.2 0.8 and_select_fusion
  8.0 0.7 and_select_fusion.1
  8.7 0.2 convert_reduce_fusion
  8.9 1.0 scatter_custom_fusion
  9.9 0.8 all_to_all.27
  10.6 11.5 %all-to-all-start = ((s32[128,2,1]{1,2,0:T(1,128)}), s32[128,2,1]{1,2,0:T(1,128)S(1)}, u32[]{:S(2)}, u32[]{:S(2)}) async-start(s32[128,2,1]{1,2,0:T(1,128)} %bitcast), calls=%async_computation | async-start | bytes 131072 | tf_op jit(solution)/shard_map/all_to_all | solution.py:41
  22.1 1.3 convolution_convert_fusion.3
  23.4 1.9 scatter_custom_fusion.1
  25.3 1.2 all_to_all.30
  26.4 5.2 %all-to-all-done = s32[128,2,1]{1,2,0:T(1,128)S(1)} async-done(((s32[128,2,1]{1,2,0:T(1,128)}), s32[128,2,1]{1,2,0:T(1,128)S(1)}, u32[]{:S(2)}, u32[]{:S(2)}) %all-to-all-start) | async-done | bytes 1056 | tf_op jit(solution)/shard_map/all_to_all | solution.py:41
  31.7 4.5 %all-to-all-start.1 = ((bf16[128,2,1536]{2,1,0:T(2,128)(2,1)}), bf16[128,2,1536]{2,1,0:T(2,128)(2,1)S(1)}, u32[]{:S(2)}, u32[]{:S(2)}) async-start(bf16[128,2,1536]{2,1,0:T(2,128)(2,1)} %all_to_all.30), calls=%async_computation.1 | async-start | bytes 1572864 | tf_op jit(solution)/shard_map/all_to_all | solution.py:40
  36.2 0.0 all-gather.3.cloned.1.call-start
  36.3 0.5 broadcast.104
  36.8 0.8 reduce.4
  37.6 0.1 all_to_all.29
  37.7 14.7 %all-to-all-done.1 = bf16[128,2,1536]{2,1,0:T(2,128)(2,1)S(1)} async-done(((bf16[128,2,1536]{2,1,0:T(2,128)(2,1)}), bf16[128,2,1536]{2,1,0:T(2,128)(2,1)S(1)}, u32[]{:S(2)}, u32[]{:S(2)}) %all-to-all-start.1) | async-done | bytes 786464 | tf_op jit(solution)/shard_map/all_to_all | solution.py:40
  52.4 0.3 reshape.112
  52.7 2.5 scatter_custom_fusion.2
  55.2 0.2 reduce-scatter.4.cloned.1.call-start
  55.5 0.8 convolution_convert_fusion.1
  56.3 58.5 %all-gather.3.cloned.1.call-done = bf16[4096,1536]{1,0:T(8,128)(2,1)} async-done(((bf16[128,1536]{1,0:T(8,128)(2,1)}), bf16[4096,1536]{1,0:T(8,128)(2,1)}) %all-gather.3.cloned.1.call-update) | async-done | bytes 12582928 | tf_op jit(solution)/shard_map/all_gather | solution.py:44
  114.8 5.7 %multiply_reduce_fusion = (f32[512]{0:T(512)S(1)}, f32[512,4096]{1,0:T(8,128)S(1)}) fusion(bf16[512,768]{1,0:T(8,128)(2,1)S(1)} %convolution_convert_fusion.1, bf16[4096,1536]{1,0:T(8,128)(2,1)} %all-gather.3.cloned.1.call-done), kind=kOutput, calls=%fused_computation.9 | convolution fusion | flops 3225419264 | bytes 15468544 | tf_op jit(solution)/shard_map/dot_general | solution.py:10
  120.5 3.1 select_reduce_fusion
  123.6 0.6 fusion.19
  124.2 3.9 %multiply_convert_fusion = bf16[512,4096]{1,0:T(8,128)(2,1)S(1)} fusion(f32[512,4096]{1,0:T(8,128)S(1)} %get-tuple-element.21, f32[512]{0:T(512)S(1)} %get-tuple-element.15, f32[512]{0:T(512)S(1)} %copy-done.7, s32[512]{0:T(512)S(1)} %copy-done.6), kind=kLoop, calls=%fused_computation.5 | loop fusion | flops 16777216 | bytes 12589056 | tf_op jit(solution)/shard_map/convert_element_type | solution.py:54
  128.1 4.0 %fusion.20 = bf16[4096,768]{1,0:T(8,128)(2,1)S(1)} fusion(bf16[512,4096]{1,0:T(8,128)(2,1)S(1)} %multiply_convert_fusion, bf16[512,768]{1,0:T(8,128)(2,1)S(1)} %convolution_convert_fusion.1), kind=kOutput, calls=%fused_computation.48 | convolution fusion | flops 3221225472 | bytes 11272192 | tf_op jit(solution)/shard_map/dot_general | solution.py:10
  132.2 3.5 fusion.6
  135.7 5.6 %fusion = f32[768,768]{0,1:T(8,128)S(1)} fusion(bf16[4096,768]{1,0:T(8,128)(2,1)S(1)} %fusion.20, bf16[4096,1536]{1,0:T(8,128)(2,1)S(1)} %bitcast.30), kind=kOutput, calls=%fused_computation.10 | convolution fusion | flops 4831838208 | bytes 14942208 | tf_op jit(solution)/shard_map/dot_general | solution.py:10
  141.3 0.8 bitcast_add_fusion
  142.2 2.0 copy.22
  144.2 5.5 %all-to-all-start.2 = ((bf16[32,128,768]{2,1,0:T(8,128)(2,1)}), bf16[32,128,768]{2,1,0:T(8,128)(2,1)}, u32[]{:S(2)}, u32[]{:S(2)}) async-start(bf16[32,128,768]{2,1,0:T(8,128)(2,1)} %bitcast.26), calls=%async_computation.2 | async-start | bytes 12582912 | tf_op jit(solution)/shard_map/all_to_all | solution.py:64
  149.7 0.0 all-reduce.2.cloned.1.call-start
  149.7 97.8 %reduce-scatter.4.cloned.1.call-done = f32[24,768]{1,0:T(8,128)} async-done(((f32[768,768]{1,0:T(8,128)}), f32[24,768]{1,0:T(8,128)}) %reduce-scatter.4.cloned.1.call-update) | async-done | bytes 73744
  247.5 1.8 copy.23
  249.3 0.0 all-gather.5.cloned.1.call-start
  249.4 42.6 %all-reduce.2.cloned.1.call-done = f32[24,768]{0,1:T(8,128)} async-done(((f32[24,768]{0,1:T(8,128)}), f32[24,768]{0,1:T(8,128)}) %all-reduce.2.cloned.1.call-update) | async-done | bytes 73744 | tf_op jit(solution)/shard_map/psum | solution.py:60
  292.0 1.8 copy.20
  293.8 3.7 %reduce_sum.42 = bf16[128,768]{1,0:T(8,128)(2,1)S(1)} reduce(bf16[32,128,768]{2,1,0:T(8,128)(2,1)} %all-to-all-done.2, bf16[]{:T(256)} %constant.20.clone.1), dimensions={0}, to_apply=%region_7.8 | reduce | flops 3047424 | bytes 6488066 | tf_op jit(solution)/shard_map/reduce_sum | solution.py:71
  297.5 1.2 gather_fusion
  298.7 0.9 all_to_all.34
  299.6 10.9 %all-to-all-start.3 = ((bf16[128,2,768]{2,1,0:T(2,128)(2,1)}), bf16[128,2,768]{2,1,0:T(2,128)(2,1)S(1)}, u32[]{:S(2)}, u32[]{:S(2)}) async-start(bf16[128,2,768]{2,1,0:T(2,128)(2,1)} %all_to_all.34), calls=%async_computation.3 | async-start | bytes 786432 | tf_op jit(solution)/shard_map/all_to_all | solution.py:73
  310.6 1.7 convolution_convert_fusion
  312.3 10.7 %all-to-all-done.3 = bf16[128,2,768]{2,1,0:T(2,128)(2,1)S(1)} async-done(((bf16[128,2,768]{2,1,0:T(2,128)(2,1)}), bf16[128,2,768]{2,1,0:T(2,128)(2,1)S(1)}, u32[]{:S(2)}, u32[]{:S(2)}) %all-to-all-start.3) | async-done | bytes 393248 | tf_op jit(solution)/shard_map/all_to_all | solution.py:73
  323.0 0.1 all_to_all.36
  323.2 0.9 gather_fusion.1
  324.0 1.2 convolution_convert_fusion.2
  325.2 16.9 %all-gather.5.cloned.1.call-done = f32[768,768]{1,0:T(8,128)} async-done(((f32[24,768]{1,0:T(8,128)}), f32[768,768]{1,0:T(8,128)}) %all-gather.5.cloned.1.call-update) | async-done | bytes 2359312 | tf_op jit(solution)/shard_map/all_gather | solution.py:63
  342.1 3.2 broadcast_multiply_fusion
  (32 shorter events, 0.2 us)
Async XLA Ops:
  7.2 15.0 %copy-start = (bf16[768,768]{1,0:T(8,128)(2,1)S(1)}, bf16[768,768]{1,0:T(8,128)(2,1)}, u32[]{:S(2)}) copy-start(bf16[768,768]{1,0:T(8,128)(2,1)} %param.9) | copy-start | bytes 3538948
  7.2 48.3 %copy-start.2 = (bf16[512,768]{1,0:T(8,128)(2,1)S(1)}, bf16[512,768]{1,0:T(8,128)(2,1)}, u32[]{:S(2)}) copy-start(bf16[512,768]{1,0:T(8,128)(2,1)} %param.8) | copy-start | bytes 2359300
  10.6 21.1 %all-to-all-start = ((s32[128,2,1]{1,2,0:T(1,128)}), s32[128,2,1]{1,2,0:T(1,128)S(1)}, u32[]{:S(2)}, u32[]{:S(2)}) async-start(s32[128,2,1]{1,2,0:T(1,128)} %bitcast), calls=%async_computation | async-start | bytes 131072 | tf_op jit(solution)/shard_map/all_to_all | solution.py:41
  31.7 20.7 %all-to-all-start.1 = ((bf16[128,2,1536]{2,1,0:T(2,128)(2,1)}), bf16[128,2,1536]{2,1,0:T(2,128)(2,1)S(1)}, u32[]{:S(2)}, u32[]{:S(2)}) async-start(bf16[128,2,1536]{2,1,0:T(2,128)(2,1)} %all_to_all.30), calls=%async_computation.1 | async-start | bytes 1572864 | tf_op jit(solution)/shard_map/all_to_all | solution.py:40
  36.2 78.5 %all-gather.3.cloned.1.call-start = ((), (), s32[]{:S(2)}) async-start(), calls=%async_computation.5 | async-start | bytes 12976128 | tf_op jit(solution)/shard_map/all_gather | solution.py:44
  55.2 192.3 %reduce-scatter.4.cloned.1.call-start = ((), (), s32[]{:S(2)}) async-start(), calls=%async_computation.8 | async-start | bytes 2433024
  56.3 64.2 %copy-start.6 = (s32[512]{0:T(512)S(1)}, s32[512]{0:T(512)}, u32[]{:S(2)}) copy-start(s32[512]{0:T(512)} %param.12) | copy-start | bytes 6148
  120.5 3.7 %copy-start.7 = (f32[512]{0:T(512)S(1)}, f32[512]{0:T(512)}, u32[]{:S(2)}) copy-start(f32[512]{0:T(512)} %param.13) | copy-start | bytes 6148
  124.2 7.9 %slice-start = ((s8[12582912]{0:T(1024)(128)(4,1)}), s8[4194304]{0:T(1024)(128)(4,1)S(1)}, s32[]{:S(2)}) async-start(s8[12582912]{0:T(1024)(128)(4,1)} %bitcast.29), calls=%async_computation.9 | async-start | bytes 8388608
  124.2 7.9 %slice-start.1 = ((s8[12582912]{0:T(1024)(128)(4,1)}), s8[4194304]{0:T(1024)(128)(4,1)S(1)}, s32[]{:S(2)}) async-start(s8[12582912]{0:T(1024)(128)(4,1)} %bitcast.29), calls=%async_computation.10 | async-start | bytes 8388608
  128.1 4.0 %slice-start.2 = ((s8[12582912]{0:T(1024)(128)(4,1)}), s8[4194304]{0:T(1024)(128)(4,1)S(1)}, s32[]{:S(2)}) async-start(s8[12582912]{0:T(1024)(128)(4,1)} %bitcast.29), calls=%async_computation.11 | async-start | bytes 8388608
  132.2 3.5 copy-start.1
  135.6 5.7 %copy-start.4 = (bf16[512,768]{1,0:T(8,128)(2,1)}, bf16[512,768]{1,0:T(8,128)(2,1)S(1)}, u32[]{:S(2)}) copy-start(bf16[512,768]{1,0:T(8,128)(2,1)S(1)} %fusion.6) | copy-start | bytes 2359300
  135.7 5.7 %copy-start.3 = (bf16[512,768]{1,0:T(8,128)(2,1)S(1)}, bf16[512,768]{1,0:T(8,128)(2,1)}, u32[]{:S(2)}) copy-start(bf16[512,768]{1,0:T(8,128)(2,1)} %param.8) | copy-start | bytes 2359300
  144.2 149.6 %all-to-all-start.2 = ((bf16[32,128,768]{2,1,0:T(8,128)(2,1)}), bf16[32,128,768]{2,1,0:T(8,128)(2,1)}, u32[]{:S(2)}, u32[]{:S(2)}) async-start(bf16[32,128,768]{2,1,0:T(8,128)(2,1)} %bitcast.26), calls=%async_computation.2 | async-start | bytes 12582912 | tf_op jit(solution)/shard_map/all_to_all | solution.py:64
  149.7 142.3 %all-reduce.2.cloned.1.call-start = ((), (), s32[]{:S(2)}) async-start(), calls=%async_computation.6 | async-start | bytes 786432 | tf_op jit(solution)/shard_map/psum | solution.py:60
  249.3 61.2 %copy-start.5 = (bf16[512,768]{1,0:T(8,128)(2,1)S(1)}, bf16[512,768]{1,0:T(8,128)(2,1)}, u32[]{:S(2)}) copy-start(bf16[512,768]{1,0:T(8,128)(2,1)} %copy-done.4) | copy-start | bytes 2359300
  249.3 92.8 %all-gather.5.cloned.1.call-start = ((), (), s32[]{:S(2)}) async-start(), calls=%async_computation.7 | async-start | bytes 2433024 | tf_op jit(solution)/shard_map/all_gather | solution.py:63
  299.6 23.4 %all-to-all-start.3 = ((bf16[128,2,768]{2,1,0:T(2,128)(2,1)}), bf16[128,2,768]{2,1,0:T(2,128)(2,1)S(1)}, u32[]{:S(2)}, u32[]{:S(2)}) async-start(bf16[128,2,768]{2,1,0:T(2,128)(2,1)} %all_to_all.34), calls=%async_computation.3 | async-start | bytes 786432 | tf_op jit(solution)/shard_map/all_to_all | solution.py:73
Sparse Core Ops, SparseCore 0:
  55.3 59.3 all-gather.2
  144.3 103.1 reduce-scatter.3
  250.5 41.4 all-reduce.1
  294.1 47.9 all-gather.4

commit v4 on v2

--- a/solution.py
+++ b/solution.py
@@ -33,13 +33,14 @@
     earlier_same = (owner[:, None] == owner[None, :]) & (order[:, None] > order[None, :])
     rank = jnp.sum(earlier_same.astype(jnp.int32), axis=1)
     position = owner * capacity + rank
-    both = jnp.concatenate([passage_emb, passage_hidden], axis=1)
-    send_rows = jnp.zeros((devices * capacity, 2 * width), jnp.bfloat16).at[position].set(both)
-    send_slots = jnp.full((devices * capacity,), rows, jnp.int32).at[position].set(slot)
-    got_rows, got_slots = (
-        lax.all_to_all(send_rows, ("group", "member"), split_axis=0, concat_axis=0, tiled=True),
-        lax.all_to_all(send_slots, ("group", "member"), split_axis=0, concat_axis=0, tiled=True),
-    )
+    tag_width = 128
+    tag = jnp.broadcast_to(slot.astype(jnp.bfloat16)[:, None], (rows, tag_width))
+    both = jnp.concatenate([passage_emb, passage_hidden, tag], axis=1)
+    send_rows = jnp.zeros((devices * capacity, 2 * width + tag_width), jnp.bfloat16)
+    send_rows = send_rows.at[:, 2 * width :].set(rows).at[position].set(both)
+    got = lax.all_to_all(send_rows, ("group", "member"), split_axis=0, concat_axis=0, tiled=True)
+    got_rows = got[:, : 2 * width]
+    got_slots = got[:, 2 * width].astype(jnp.int32)
     relaid = jnp.zeros((rows, 2 * width), jnp.bfloat16).at[got_slots].set(got_rows, mode="drop")
     group_both = lax.all_gather(relaid, "member", axis=0, tiled=True)
     group_passages = group_both[:, :width]

time: 308 us -> 299 us (0.971)
  blocking collectives: 36.7 us -> 64.9 us
  waiting for transfers between devices: 166 us -> 145 us
  starting transfers between devices: 36.3 us -> 20.3 us
    all_to_all x0 -> x1, blocking collectives: none -> 28.2 us  [shards(): lax.all_to_all(send_rows, ('group', 'member'), split_axis=0, concat_axis=...]
    all_to_all x2 -> x0, waiting for transfers between devices: 19.9 us -> none  [the longest x1 14.7 us: shards(): lax.all_to_all(send_rows, ('group', 'member'), split_axis=0, concat_axis=...]
    all_to_all x2 -> x0, starting transfers between devices: 16 us -> none  [the longest x1 11.5 us: shards(): lax.all_to_all(send_slots, ('group', 'member'), split_axis=0, concat_axis...]
  transfers between devices with their start and end apart: 7 -> 5, of which waited for: 6 -> 4; matrix products, arithmetic and copies ran while one was open for 5% -> 4% of each run, Pallas kernels for 0% -> 0%
where the time goes in v4:
time: 299 us; the launch traced here: 298 us
  waiting for transfers between devices  145 us (48%)
  blocking collectives  64.9 us (22%)
  matrix products  25.7 us (9%)
  starting transfers between devices  20.3 us (7%)
  other arithmetic  19.2 us (6%)
  between operations  14.1 us (5%)
  local copies, waits for them, and re-layouts  8.47 us (3%)
    all_gather x1, waiting for transfers between devices, shards(): group_both = lax.all_gather(relaid, 'member', axis=0, tiled=True)  57.6 us
    psum x1, waiting for transfers between devices, shards(): weight_share = lax.psum(jnp.sum(weight_pieces, axis=0), 'group')  42.9 us
    all_to_all x1, blocking collectives, shards(): lax.all_to_all(local_weight.reshape(members, weight_rows, width), 'member...  36.7 us
    all_to_all x1, waiting for transfers between devices, shards(): lax.all_to_all(partial.astype(jnp.bfloat16).reshape(members, rows, width)...  34.3 us
    all_to_all x1, blocking collectives, shards(): lax.all_to_all(send_rows, ('group', 'member'), split_axis=0, concat_axis=...  28.2 us
    dot_general x6, matrix products, contract(): lax.dot_general(left, right, (((left_dim,), (right_dim,)), ((), ())), pre...  19 us
    all_to_all x1, starting transfers between devices, shards(): lax.all_to_all(back_rows, ('group', 'member'), split_axis=0, concat_axis=...  15.5 us
    all_to_all x1, waiting for transfers between devices, shards(): lax.all_to_all(back_rows, ('group', 'member'), split_axis=0, concat_axis=...  10.5 us
  transfers between devices with their start and end apart: 5, of which 4 were waited for; matrix products, arithmetic and copies ran while one was open for 4% of the time, Pallas kernels for 0%

profile of v4, /device:TPU:1, one launch (start us, length us, event | category | flops | bytes accessed | tf_op | source)
XLA Modules:
  0.0 298.0 jit_solution(14139776370423312957)
XLA Ops:
  7.2 0.0 copy-start
  7.2 0.0 all-gather.3.cloned.1.call-start
  7.2 0.8 fusion.21
  8.0 0.7 and_select_fusion.1
  8.7 0.2 convert_reduce_fusion
  8.9 1.3 convolution_convert_fusion.3
  10.2 0.1 broadcast_in_dim.11
  10.3 0.1 scatter.22
  10.3 2.1 scatter_custom_fusion
  12.5 0.3 all_to_all.22
  12.8 28.2 %all_to_all.34 = bf16[128,2,1664]{2,1,0:T(2,128)(2,1)} all-to-all(bf16[128,2,1664]{2,1,0:T(2,128)(2,1)S(1)} %all_to_all.22), channel_id=1, replica_groups=mesh['group'=4,'member'=32] {'group','member'}, dimensions={0} | all-to-all | bytes 1703936 | tf_op jit(solution)/shard_map/all_to_all | solution.py:41
  41.0 2.4 all_to_all.24
  43.4 0.2 fusion.19
  43.6 2.5 scatter_custom_fusion.1
  46.0 0.0 all-gather.3.cloned.1.call-update
  46.1 1.9 convolution_convert_fusion.1
  48.0 0.0 copy-start.5
  48.0 57.6 %all-gather.3.cloned.1.call-done = bf16[4096,1536]{1,0:T(8,128)(2,1)} async-done(((bf16[128,1536]{1,0:T(8,128)(2,1)}), bf16[4096,1536]{1,0:T(8,128)(2,1)}) %all-gather.3.cloned.1.call-update) | async-done | bytes 12582928 | tf_op jit(solution)/shard_map/all_gather | solution.py:45
  105.6 5.8 %multiply_reduce_fusion = (f32[512]{0:T(512)S(1)}, f32[512,4096]{1,0:T(8,128)S(1)}) fusion(bf16[512,768]{1,0:T(8,128)(2,1)S(1)} %convolution_convert_fusion.1, bf16[4096,1536]{1,0:T(8,128)(2,1)} %all-gather.3.cloned.1.call-done), kind=kOutput, calls=%fused_computation.8 | convolution fusion | flops 3225419264 | bytes 15468544 | tf_op jit(solution)/shard_map/dot_general | solution.py:10
  111.4 0.0 copy-start.6
  111.5 3.1 %select_reduce_fusion = (f32[512]{0:T(512)S(1)}, f32[512]{0:T(512)S(1)}) fusion(f32[512,4096]{1,0:T(8,128)S(1)} %get-tuple-element.25, s32[512]{0:T(512)S(1)} %copy-done.5, f32[512]{0:T(512)S(1)} %get-tuple-element.24), kind=kLoop, calls=%fused_computation.5 | loop fusion | flops 12581888 | bytes 8396800 | tf_op jit(solution)/shard_map/reduce_sum | solution.py:52
  114.6 0.6 fusion.22
  115.2 3.9 %multiply_convert_fusion = bf16[512,4096]{1,0:T(8,128)(2,1)S(1)} fusion(f32[512,4096]{1,0:T(8,128)S(1)} %get-tuple-element.25, f32[512]{0:T(512)S(1)} %get-tuple-element.21, f32[512]{0:T(512)S(1)} %copy-done.6, s32[512]{0:T(512)S(1)} %copy-done.5), kind=kLoop, calls=%fused_computation.4 | loop fusion | flops 16777216 | bytes 12589056 | tf_op jit(solution)/shard_map/convert_element_type | solution.py:55
  119.1 4.0 %fusion.23 = bf16[4096,768]{1,0:T(8,128)(2,1)S(1)} fusion(bf16[512,4096]{1,0:T(8,128)(2,1)S(1)} %multiply_convert_fusion, bf16[512,768]{1,0:T(8,128)(2,1)S(1)} %convolution_convert_fusion.1), kind=kOutput, calls=%fused_computation.51 | convolution fusion | flops 3221225472 | bytes 11272192 | tf_op jit(solution)/shard_map/dot_general | solution.py:10
  123.1 3.5 %fusion.6 = bf16[512,768]{1,0:T(8,128)(2,1)S(1)} fusion(bf16[512,4096]{1,0:T(8,128)(2,1)S(1)} %multiply_convert_fusion, bf16[4096,1536]{1,0:T(8,128)(2,1)S(1)} %bitcast.24), kind=kOutput, calls=%fused_computation.18 | convolution fusion | flops 3221618688 | bytes 11272192 | tf_op jit(solution)/shard_map/dot_general | solution.py:56
  126.6 0.0 copy-start.3
  126.6 0.0 copy-start.2
  126.6 5.4 %fusion = f32[768,768]{1,0:T(8,128)S(1)} fusion(bf16[4096,768]{1,0:T(8,128)(2,1)S(1)} %fusion.23, bf16[4096,1536]{1,0:T(8,128)(2,1)S(1)} %bitcast.24), kind=kOutput, calls=%fused_computation.9 | convolution fusion | flops 4831838208 | bytes 14942208 | tf_op jit(solution)/shard_map/dot_general | solution.py:10
  132.1 0.9 bitcast_add_fusion
  133.0 36.7 %all_to_all.35 = f32[32,24,768]{2,1,0:T(8,128)S(1)} all-to-all(f32[32,24,768]{2,1,0:T(8,128)S(1)} %bitcast.21), channel_id=1, replica_groups=mesh['group'=4,'member'=32] {'member'}, dimensions={0} | all-to-all | bytes 4718592 | tf_op jit(solution)/shard_map/all_to_all | solution.py:62
  169.7 4.7 %all-to-all-start.1 = ((bf16[32,128,768]{2,1,0:T(8,128)(2,1)}), bf16[32,128,768]{2,1,0:T(8,128)(2,1)}, u32[]{:S(2)}, u32[]{:S(2)}) async-start(bf16[32,128,768]{2,1,0:T(8,128)(2,1)} %bitcast.22), calls=%async_computation.1 | async-start | bytes 12582912 | tf_op jit(solution)/shard_map/all_to_all | solution.py:67
  174.4 0.0 all-reduce.3.cloned.1.call-start
  174.4 0.8 reduce_sum.52
  175.2 0.0 all-reduce.3.cloned.1.call-update
  175.2 0.0 all-gather.5.cloned.1.call-start
  175.2 42.9 %all-reduce.3.cloned.1.call-done = f32[24,768]{1,0:T(8,128)} async-done(((f32[24,768]{1,0:T(8,128)}), f32[24,768]{1,0:T(8,128)}) %all-reduce.3.cloned.1.call-update) | async-done | bytes 73744 | tf_op jit(solution)/shard_map/psum | solution.py:65
  218.2 0.0 all-gather.5.cloned.1.call-update
  218.2 34.3 %all-to-all-done.1 = bf16[32,128,768]{2,1,0:T(8,128)(2,1)} async-done(((bf16[32,128,768]{2,1,0:T(8,128)(2,1)}), bf16[32,128,768]{2,1,0:T(8,128)(2,1)}, u32[]{:S(2)}, u32[]{:S(2)}) %all-to-all-start.1) | async-done | bytes 6291488 | tf_op jit(solution)/shard_map/all_to_all | solution.py:67
  252.6 3.7 %reduce_sum.51 = bf16[128,768]{1,0:T(8,128)(2,1)S(1)} reduce(bf16[32,128,768]{2,1,0:T(8,128)(2,1)} %all-to-all-done.1, bf16[]{:T(256)} %constant.66.clone.1), dimensions={0}, to_apply=%region_6.7 | reduce | flops 3047424 | bytes 6488066 | tf_op jit(solution)/shard_map/reduce_sum | solution.py:74
  256.3 1.2 gather_fusion
  257.5 0.9 all_to_all.26
  258.4 15.5 %all-to-all-start.2 = ((bf16[128,2,768]{2,1,0:T(2,128)(2,1)}), bf16[128,2,768]{2,1,0:T(2,128)(2,1)S(1)}, u32[]{:S(2)}, u32[]{:S(2)}) async-start(bf16[128,2,768]{2,1,0:T(2,128)(2,1)} %all_to_all.26), calls=%async_computation.2 | async-start | bytes 786432 | tf_op jit(solution)/shard_map/all_to_all | solution.py:76
  273.9 1.7 convolution_convert_fusion
  275.6 10.5 %all-to-all-done.2 = bf16[128,2,768]{2,1,0:T(2,128)(2,1)S(1)} async-done(((bf16[128,2,768]{2,1,0:T(2,128)(2,1)}), bf16[128,2,768]{2,1,0:T(2,128)(2,1)S(1)}, u32[]{:S(2)}, u32[]{:S(2)}) %all-to-all-start.2) | async-done | bytes 393248 | tf_op jit(solution)/shard_map/all_to_all | solution.py:76
  286.0 0.1 all_to_all.28
  286.2 0.9 gather_fusion.1
  287.0 1.2 convolution_convert_fusion.2
  288.3 3.2 %broadcast_multiply_fusion = f32[768,768]{1,0:T(8,128)} fusion(f32[768,768]{1,0:T(8,128)} %all-gather.5.cloned.1.call-done), kind=kLoop, calls=%fused_computation.19 | loop fusion | flops 589824 | bytes 4718592 | tf_op jit(solution)/shard_map/div | solution.py:66
  (22 shorter events, 0.1 us)
Async XLA Ops:
  7.2 1.7 copy-start
  7.2 98.5 %all-gather.3.cloned.1.call-start = ((), (), s32[]{:S(2)}) async-start(), calls=%async_computation.4 | async-start | bytes 12976128 | tf_op jit(solution)/shard_map/all_gather | solution.py:45
  48.0 63.5 %copy-start.5 = (s32[512]{0:T(512)S(1)}, s32[512]{0:T(512)}, u32[]{:S(2)}) copy-start(s32[512]{0:T(512)} %param.14) | copy-start | bytes 6148
  111.4 3.7 %copy-start.6 = (f32[512]{0:T(512)S(1)}, f32[512]{0:T(512)}, u32[]{:S(2)}) copy-start(f32[512]{0:T(512)} %param.15) | copy-start | bytes 6148
  115.2 7.9 %slice-start = ((s8[12582912]{0:T(1024)(128)(4,1)}), s8[4194304]{0:T(1024)(128)(4,1)S(1)}, s32[]{:S(2)}) async-start(s8[12582912]{0:T(1024)(128)(4,1)} %bitcast.23), calls=%async_computation.7 | async-start | bytes 8388608
  115.2 7.9 %slice-start.1 = ((s8[12582912]{0:T(1024)(128)(4,1)}), s8[4194304]{0:T(1024)(128)(4,1)S(1)}, s32[]{:S(2)}) async-start(s8[12582912]{0:T(1024)(128)(4,1)} %bitcast.23), calls=%async_computation.8 | async-start | bytes 8388608
  119.1 4.0 %slice-start.2 = ((s8[12582912]{0:T(1024)(128)(4,1)}), s8[4194304]{0:T(1024)(128)(4,1)S(1)}, s32[]{:S(2)}) async-start(s8[12582912]{0:T(1024)(128)(4,1)} %bitcast.23), calls=%async_computation.9 | async-start | bytes 8388608
  123.1 3.5 %copy-start.1 = (bf16[4096,768]{1,0:T(8,128)(2,1)}, bf16[4096,768]{1,0:T(8,128)(2,1)S(1)}, u32[]{:S(2)}) copy-start(bf16[4096,768]{1,0:T(8,128)(2,1)S(1)} %fusion.23) | copy-start | bytes 18874372
  126.6 5.5 %copy-start.3 = (bf16[512,768]{1,0:T(8,128)(2,1)}, bf16[512,768]{1,0:T(8,128)(2,1)S(1)}, u32[]{:S(2)}) copy-start(bf16[512,768]{1,0:T(8,128)(2,1)S(1)} %fusion.6) | copy-start | bytes 2359300
  126.6 5.5 %copy-start.2 = (bf16[512,768]{1,0:T(8,128)(2,1)S(1)}, bf16[512,768]{1,0:T(8,128)(2,1)}, u32[]{:S(2)}) copy-start(bf16[512,768]{1,0:T(8,128)(2,1)} %param.10) | copy-start | bytes 2359300
  169.7 82.9 %all-to-all-start.1 = ((bf16[32,128,768]{2,1,0:T(8,128)(2,1)}), bf16[32,128,768]{2,1,0:T(8,128)(2,1)}, u32[]{:S(2)}, u32[]{:S(2)}) async-start(bf16[32,128,768]{2,1,0:T(8,128)(2,1)} %bitcast.22), calls=%async_computation.1 | async-start | bytes 12582912 | tf_op jit(solution)/shard_map/all_to_all | solution.py:67
  174.4 43.8 %all-reduce.3.cloned.1.call-start = ((), (), s32[]{:S(2)}) async-start(), calls=%async_computation.5 | async-start | bytes 147456 | tf_op jit(solution)/shard_map/psum | solution.py:65
  175.2 98.7 %copy-start.4 = (bf16[512,768]{1,0:T(8,128)(2,1)S(1)}, bf16[512,768]{1,0:T(8,128)(2,1)}, u32[]{:S(2)}) copy-start(bf16[512,768]{1,0:T(8,128)(2,1)} %copy-done.3) | copy-start | bytes 2359300
  175.2 113.1 %all-gather.5.cloned.1.call-start = ((), (), s32[]{:S(2)}) async-start(), calls=%async_computation.6 | async-start | bytes 2433024 | tf_op jit(solution)/shard_map/all_gather | solution.py:66
  258.4 27.6 %all-to-all-start.2 = ((bf16[128,2,768]{2,1,0:T(2,128)(2,1)}), bf16[128,2,768]{2,1,0:T(2,128)(2,1)S(1)}, u32[]{:S(2)}, u32[]{:S(2)}) async-start(bf16[128,2,768]{2,1,0:T(2,128)(2,1)} %all_to_all.26), calls=%async_computation.2 | async-start | bytes 786432 | tf_op jit(solution)/shard_map/all_to_all | solution.py:76
Sparse Core Ops, SparseCore 0:
  46.2 59.4 all-gather.2
  178.1 40.0 all-reduce.2
  220.4 56.7 all-gather.4

commit v5 on v4

--- a/solution.py
+++ b/solution.py
@@ -12,7 +12,7 @@
     )
 
 
-def shards(passage_hidden, query_hidden, proj_weight, cluster, place, positive, loss_weight):
+def body(passage_hidden, query_hidden, proj_weight, cluster, place, positive, loss_weight):
     rows, width = passage_hidden.shape
     members = lax.axis_size("member")
     groups = lax.axis_size("group")
@@ -62,7 +62,12 @@
     weight_pieces = lax.all_to_all(
         local_weight.reshape(members, weight_rows, width), "member", 0, 0, tiled=True
     )
-    weight_share = lax.psum(jnp.sum(weight_pieces, axis=0), "group")
+    weight_share = jnp.sum(weight_pieces, axis=0)
+    step = 1
+    while step < groups:
+        pairs = [(index, index ^ step) for index in range(groups)]
+        weight_share = weight_share + lax.ppermute(weight_share, "group", pairs)
+        step *= 2
     grad_weight = lax.all_gather(weight_share, "member", axis=0, tiled=True) / devices
     pieces = lax.all_to_all(
         partial.astype(jnp.bfloat16).reshape(members, rows, width),
@@ -98,4 +103,4 @@
         P(("group", "member"), None),
         P(),
     )
-    return jax.shard_map(shards, mesh=mesh, in_specs=in_specs, out_specs=out_specs, check_vma=False)
+    return jax.shard_map(body, mesh=mesh, in_specs=in_specs, out_specs=out_specs, check_vma=False)

time: 299 us -> 302 us (1.010)
  starting transfers between devices: 20.3 us -> 26.2 us
  waiting for transfers between devices: 145 us -> 141 us
    psum x1 -> x0, waiting for transfers between devices: 42.9 us -> none  [shards(): weight_share = lax.psum(jnp.sum(weight_pieces, axis=0), 'group')]
    all_to_all x2, waiting for transfers between devices: 44.8 us -> 78.3 us  [the longest x1 67.8 us: body(): lax.all_to_all(partial.astype(jnp.bfloat16).reshape(members, rows, width)...]
    ppermute x0 -> x2, waiting for transfers between devices: none -> 4.78 us  [body(): weight_share = weight_share + lax.ppermute(weight_share, 'group', pairs)]
    ppermute x0 -> x2, starting transfers between devices: none -> 4.22 us  [body(): weight_share = weight_share + lax.ppermute(weight_share, 'group', pairs)]
  transfers between devices with their start and end apart: 5 -> 6, of which waited for: 4 -> 5; matrix products, arithmetic and copies ran while one was open for 4% -> 4% of each run, Pallas kernels for 0% -> 0%
where the time goes in v5:
time: 302 us; the launch traced here: 301 us
  waiting for transfers between devices  141 us (47%)
  blocking collectives  64.9 us (21%)
  starting transfers between devices  26.2 us (9%)
  matrix products  25.7 us (9%)
  other arithmetic  20.9 us (7%)
  between operations  14.4 us (5%)
  local copies, waits for them, and re-layouts  8.47 us (3%)
    all_to_all x1, waiting for transfers between devices, body(): lax.all_to_all(partial.astype(jnp.bfloat16).reshape(members, rows, width)...  67.8 us
    all_gather x1, waiting for transfers between devices, body(): group_both = lax.all_gather(relaid, 'member', axis=0, tiled=True)  57.6 us
    all_to_all x1, blocking collectives, body(): lax.all_to_all(local_weight.reshape(members, weight_rows, width), 'member...  36.7 us
    all_to_all x1, blocking collectives, body(): lax.all_to_all(send_rows, ('group', 'member'), split_axis=0, concat_axis=...  28.2 us
    dot_general x6, matrix products, contract(): lax.dot_general(left, right, (((left_dim,), (right_dim,)), ((), ())), pre...  19 us
    all_to_all x1, starting transfers between devices, body(): lax.all_to_all(back_rows, ('group', 'member'), split_axis=0, concat_axis=...  17.2 us
    all_to_all x1, waiting for transfers between devices, body(): lax.all_to_all(back_rows, ('group', 'member'), split_axis=0, concat_axis=...  10.5 us
  transfers between devices with their start and end apart: 6, of which 5 were waited for; matrix products, arithmetic and copies ran while one was open for 4% of the time, Pallas kernels for 0%

profile of v5, /device:TPU:1, one launch (start us, length us, event | category | flops | bytes accessed | tf_op | source)
XLA Modules:
  0.0 301.2 jit_solution(12567064937749943793)
XLA Ops:
  7.2 0.0 copy-start
  7.2 0.0 all-gather.3.cloned.1.call-start
  7.2 0.8 fusion.21
  8.0 0.7 and_select_fusion.1
  8.7 0.2 convert_reduce_fusion
  8.9 1.3 convolution_convert_fusion.3
  10.2 0.1 broadcast_in_dim.11
  10.3 0.1 scatter.22
  10.3 2.1 scatter_custom_fusion
  12.5 0.3 all_to_all.22
  12.8 28.2 %all_to_all.34 = bf16[128,2,1664]{2,1,0:T(2,128)(2,1)} all-to-all(bf16[128,2,1664]{2,1,0:T(2,128)(2,1)S(1)} %all_to_all.22), channel_id=1, replica_groups=mesh['group'=4,'member'=32] {'group','member'}, dimensions={0} | all-to-all | bytes 1703936 | tf_op jit(solution)/shard_map/all_to_all | solution.py:41
  41.0 2.4 all_to_all.24
  43.4 0.2 fusion.19
  43.6 2.5 scatter_custom_fusion.1
  46.0 0.0 all-gather.3.cloned.1.call-update
  46.1 1.9 convolution_convert_fusion.1
  48.0 0.0 copy-start.5
  48.0 57.6 %all-gather.3.cloned.1.call-done = bf16[4096,1536]{1,0:T(8,128)(2,1)} async-done(((bf16[128,1536]{1,0:T(8,128)(2,1)}), bf16[4096,1536]{1,0:T(8,128)(2,1)}) %all-gather.3.cloned.1.call-update) | async-done | bytes 12582928 | tf_op jit(solution)/shard_map/all_gather | solution.py:45
  105.6 5.8 %multiply_reduce_fusion = (f32[512]{0:T(512)S(1)}, f32[512,4096]{1,0:T(8,128)S(1)}) fusion(bf16[512,768]{1,0:T(8,128)(2,1)S(1)} %convolution_convert_fusion.1, bf16[4096,1536]{1,0:T(8,128)(2,1)} %all-gather.3.cloned.1.call-done), kind=kOutput, calls=%fused_computation.8 | convolution fusion | flops 3225419264 | bytes 15468544 | tf_op jit(solution)/shard_map/dot_general | solution.py:10
  111.5 3.1 %select_reduce_fusion = (f32[512]{0:T(512)S(1)}, f32[512]{0:T(512)S(1)}) fusion(f32[512,4096]{1,0:T(8,128)S(1)} %get-tuple-element.25, s32[512]{0:T(512)S(1)} %copy-done.5, f32[512]{0:T(512)S(1)} %get-tuple-element.24), kind=kLoop, calls=%fused_computation.5 | loop fusion | flops 12581888 | bytes 8396800 | tf_op jit(solution)/shard_map/reduce_sum | solution.py:52
  114.6 0.6 fusion.22
  115.2 3.9 %multiply_convert_fusion = bf16[512,4096]{1,0:T(8,128)(2,1)S(1)} fusion(f32[512,4096]{1,0:T(8,128)S(1)} %get-tuple-element.25, f32[512]{0:T(512)S(1)} %get-tuple-element.21, f32[512]{0:T(512)S(1)} %copy-done.6, s32[512]{0:T(512)S(1)} %copy-done.5), kind=kLoop, calls=%fused_computation.4 | loop fusion | flops 16777216 | bytes 12589056 | tf_op jit(solution)/shard_map/convert_element_type | solution.py:55
  119.1 4.0 %fusion.23 = bf16[4096,768]{1,0:T(8,128)(2,1)S(1)} fusion(bf16[512,4096]{1,0:T(8,128)(2,1)S(1)} %multiply_convert_fusion, bf16[512,768]{1,0:T(8,128)(2,1)S(1)} %convolution_convert_fusion.1), kind=kOutput, calls=%fused_computation.51 | convolution fusion | flops 3221225472 | bytes 11272192 | tf_op jit(solution)/shard_map/dot_general | solution.py:10
  123.1 3.5 %fusion.6 = bf16[512,768]{1,0:T(8,128)(2,1)S(1)} fusion(bf16[512,4096]{1,0:T(8,128)(2,1)S(1)} %multiply_convert_fusion, bf16[4096,1536]{1,0:T(8,128)(2,1)S(1)} %bitcast.24), kind=kOutput, calls=%fused_computation.18 | convolution fusion | flops 3221618688 | bytes 11272192 | tf_op jit(solution)/shard_map/dot_general | solution.py:56
  126.6 5.4 %fusion = f32[768,768]{1,0:T(8,128)S(1)} fusion(bf16[4096,768]{1,0:T(8,128)(2,1)S(1)} %fusion.23, bf16[4096,1536]{1,0:T(8,128)(2,1)S(1)} %bitcast.24), kind=kOutput, calls=%fused_computation.9 | convolution fusion | flops 4831838208 | bytes 14942208 | tf_op jit(solution)/shard_map/dot_general | solution.py:10
  132.1 0.9 bitcast_add_fusion
  133.0 36.7 %all_to_all.35 = f32[32,24,768]{2,1,0:T(8,128)S(1)} all-to-all(f32[32,24,768]{2,1,0:T(8,128)S(1)} %bitcast.21), channel_id=1, replica_groups=mesh['group'=4,'member'=32] {'member'}, dimensions={0} | all-to-all | bytes 4718592 | tf_op jit(solution)/shard_map/all_to_all | solution.py:62
  169.7 4.7 %all-to-all-start.1 = ((bf16[32,128,768]{2,1,0:T(8,128)(2,1)}), bf16[32,128,768]{2,1,0:T(8,128)(2,1)}, u32[]{:S(2)}, u32[]{:S(2)}) async-start(bf16[32,128,768]{2,1,0:T(8,128)(2,1)} %bitcast.22), calls=%async_computation.1 | async-start | bytes 12582912 | tf_op jit(solution)/shard_map/all_to_all | solution.py:72
  174.4 0.0 all-gather.5.cloned.1.call-start
  174.4 0.8 reduce_sum.52
  175.2 1.3 collective-permute-start
  176.5 2.5 collective-permute-done
  179.0 0.9 add.53
  179.9 2.9 collective-permute-start.1
  182.8 2.2 collective-permute-done.1
  185.1 0.6 add.54
  185.7 0.0 all-gather.5.cloned.1.call-update
  185.8 67.8 %all-to-all-done.1 = bf16[32,128,768]{2,1,0:T(8,128)(2,1)} async-done(((bf16[32,128,768]{2,1,0:T(8,128)(2,1)}), bf16[32,128,768]{2,1,0:T(8,128)(2,1)}, u32[]{:S(2)}, u32[]{:S(2)}) %all-to-all-start.1) | async-done | bytes 6291488 | tf_op jit(solution)/shard_map/all_to_all | solution.py:72
  253.6 3.9 %reduce_sum.51 = bf16[128,768]{1,0:T(8,128)(2,1)S(1)} reduce(bf16[32,128,768]{2,1,0:T(8,128)(2,1)} %all-to-all-done.1, bf16[]{:T(256)} %constant.66.clone.1), dimensions={0}, to_apply=%region_6.7 | reduce | flops 3047424 | bytes 6488066 | tf_op jit(solution)/shard_map/reduce_sum | solution.py:79
  257.4 1.2 gather_fusion
  258.6 0.9 all_to_all.26
  259.5 17.2 %all-to-all-start.2 = ((bf16[128,2,768]{2,1,0:T(2,128)(2,1)}), bf16[128,2,768]{2,1,0:T(2,128)(2,1)S(1)}, u32[]{:S(2)}, u32[]{:S(2)}) async-start(bf16[128,2,768]{2,1,0:T(2,128)(2,1)} %all_to_all.26), calls=%async_computation.2 | async-start | bytes 786432 | tf_op jit(solution)/shard_map/all_to_all | solution.py:81
  276.7 1.7 convolution_convert_fusion
  278.4 10.5 %all-to-all-done.2 = bf16[128,2,768]{2,1,0:T(2,128)(2,1)S(1)} async-done(((bf16[128,2,768]{2,1,0:T(2,128)(2,1)}), bf16[128,2,768]{2,1,0:T(2,128)(2,1)S(1)}, u32[]{:S(2)}, u32[]{:S(2)}) %all-to-all-start.2) | async-done | bytes 393248 | tf_op jit(solution)/shard_map/all_to_all | solution.py:81
  288.8 0.1 all_to_all.28
  289.0 0.9 gather_fusion.1
  289.9 1.2 convolution_convert_fusion.2
  291.1 3.2 %broadcast_multiply_fusion = f32[768,768]{1,0:T(8,128)} fusion(f32[768,768]{1,0:T(8,128)} %all-gather.5.cloned.1.call-done), kind=kLoop, calls=%fused_computation.19 | loop fusion | flops 589824 | bytes 4718592 | tf_op jit(solution)/shard_map/div | solution.py:71
  (25 shorter events, 0.1 us)
Async XLA Ops:
  7.2 1.7 copy-start
  7.2 98.5 %all-gather.3.cloned.1.call-start = ((), (), s32[]{:S(2)}) async-start(), calls=%async_computation.4 | async-start | bytes 12976128 | tf_op jit(solution)/shard_map/all_gather | solution.py:45
  48.0 63.5 %copy-start.5 = (s32[512]{0:T(512)S(1)}, s32[512]{0:T(512)}, u32[]{:S(2)}) copy-start(s32[512]{0:T(512)} %param.14) | copy-start | bytes 6148
  111.4 3.7 %copy-start.6 = (f32[512]{0:T(512)S(1)}, f32[512]{0:T(512)}, u32[]{:S(2)}) copy-start(f32[512]{0:T(512)} %param.15) | copy-start | bytes 6148
  115.2 7.9 %slice-start = ((s8[12582912]{0:T(1024)(128)(4,1)}), s8[4194304]{0:T(1024)(128)(4,1)S(1)}, s32[]{:S(2)}) async-start(s8[12582912]{0:T(1024)(128)(4,1)} %bitcast.23), calls=%async_computation.6 | async-start | bytes 8388608
  115.2 7.9 %slice-start.1 = ((s8[12582912]{0:T(1024)(128)(4,1)}), s8[4194304]{0:T(1024)(128)(4,1)S(1)}, s32[]{:S(2)}) async-start(s8[12582912]{0:T(1024)(128)(4,1)} %bitcast.23), calls=%async_computation.7 | async-start | bytes 8388608
  119.1 4.0 %slice-start.2 = ((s8[12582912]{0:T(1024)(128)(4,1)}), s8[4194304]{0:T(1024)(128)(4,1)S(1)}, s32[]{:S(2)}) async-start(s8[12582912]{0:T(1024)(128)(4,1)} %bitcast.23), calls=%async_computation.8 | async-start | bytes 8388608
  123.1 3.5 %copy-start.1 = (bf16[4096,768]{1,0:T(8,128)(2,1)}, bf16[4096,768]{1,0:T(8,128)(2,1)S(1)}, u32[]{:S(2)}) copy-start(bf16[4096,768]{1,0:T(8,128)(2,1)S(1)} %fusion.23) | copy-start | bytes 18874372
  126.6 5.5 %copy-start.3 = (bf16[512,768]{1,0:T(8,128)(2,1)}, bf16[512,768]{1,0:T(8,128)(2,1)S(1)}, u32[]{:S(2)}) copy-start(bf16[512,768]{1,0:T(8,128)(2,1)S(1)} %fusion.6) | copy-start | bytes 2359300
  126.6 5.5 %copy-start.2 = (bf16[512,768]{1,0:T(8,128)(2,1)S(1)}, bf16[512,768]{1,0:T(8,128)(2,1)}, u32[]{:S(2)}) copy-start(bf16[512,768]{1,0:T(8,128)(2,1)} %param.10) | copy-start | bytes 2359300
  169.7 83.9 %all-to-all-start.1 = ((bf16[32,128,768]{2,1,0:T(8,128)(2,1)}), bf16[32,128,768]{2,1,0:T(8,128)(2,1)}, u32[]{:S(2)}, u32[]{:S(2)}) async-start(bf16[32,128,768]{2,1,0:T(8,128)(2,1)} %bitcast.22), calls=%async_computation.1 | async-start | bytes 12582912 | tf_op jit(solution)/shard_map/all_to_all | solution.py:72
  174.4 116.7 %all-gather.5.cloned.1.call-start = ((), (), s32[]{:S(2)}) async-start(), calls=%async_computation.5 | async-start | bytes 2433024 | tf_op jit(solution)/shard_map/all_gather | solution.py:71
  175.2 101.5 %copy-start.4 = (bf16[512,768]{1,0:T(8,128)(2,1)S(1)}, bf16[512,768]{1,0:T(8,128)(2,1)}, u32[]{:S(2)}) copy-start(bf16[512,768]{1,0:T(8,128)(2,1)} %copy-done.3) | copy-start | bytes 2359300
  175.2 3.8 %collective-permute-start = (f32[24,768]{1,0:T(8,128)}, f32[24,768]{1,0:T(8,128)S(1)}, u32[]{:S(2)}, u32[]{:S(2)}) collective-permute-start(f32[24,768]{1,0:T(8,128)} %reduce_sum.52), channel_id=1, source_target_pairs={{0,32},{32,0},{64,96},{96,64},{1,33},{33,1},{65,97},{97,65},{2,34}... | collective-permute-start | bytes 221192 | tf_op jit(solution)/shard_map/ppermute | solution.py:69
  179.9 5.2 %collective-permute-start.1 = (f32[24,768]{1,0:T(8,128)S(1)}, f32[24,768]{1,0:T(8,128)S(1)}, u32[]{:S(2)}, u32[]{:S(2)}) collective-permute-start(f32[24,768]{1,0:T(8,128)S(1)} %add.53), channel_id=1, source_target_pairs={{0,64},{32,96},{64,0},{96,32},{1,65},{33,97},{65,1},{97,33},{2,66}... | collective-permute-start | bytes 221192 | tf_op jit(solution)/shard_map/ppermute | solution.py:69
  259.5 29.3 %all-to-all-start.2 = ((bf16[128,2,768]{2,1,0:T(2,128)(2,1)}), bf16[128,2,768]{2,1,0:T(2,128)(2,1)S(1)}, u32[]{:S(2)}, u32[]{:S(2)}) async-start(bf16[128,2,768]{2,1,0:T(2,128)(2,1)} %all_to_all.26), calls=%async_computation.2 | async-start | bytes 786432 | tf_op jit(solution)/shard_map/all_to_all | solution.py:81
Sparse Core Ops, SparseCore 0:
  46.2 59.4 all-gather.2
  185.9 77.1 all-gather.4

commit v6 on v5

--- a/solution.py
+++ b/solution.py
@@ -4,6 +4,10 @@
 import jax.numpy as jnp
 from jax import lax
 from jax.sharding import PartitionSpec as P
+
+
+MEMBER = ("chip", "core")
+ALL = ("group", "chip", "core")
 
 
 def contract(left, right, left_dim, right_dim):
@@ -14,7 +18,7 @@
 
 def body(passage_hidden, query_hidden, proj_weight, cluster, place, positive, loss_weight):
     rows, width = passage_hidden.shape
-    members = lax.axis_size("member")
+    members = lax.axis_size("chip") * lax.axis_size("core")
     groups = lax.axis_size("group")
     devices = members * groups
     group_rows = rows * members
@@ -38,11 +42,11 @@
     both = jnp.concatenate([passage_emb, passage_hidden, tag], axis=1)
     send_rows = jnp.zeros((devices * capacity, 2 * width + tag_width), jnp.bfloat16)
     send_rows = send_rows.at[:, 2 * width :].set(rows).at[position].set(both)
-    got = lax.all_to_all(send_rows, ("group", "member"), split_axis=0, concat_axis=0, tiled=True)
+    got = lax.all_to_all(send_rows, ALL, split_axis=0, concat_axis=0, tiled=True)
     got_rows = got[:, : 2 * width]
     got_slots = got[:, 2 * width].astype(jnp.int32)
     relaid = jnp.zeros((rows, 2 * width), jnp.bfloat16).at[got_slots].set(got_rows, mode="drop")
-    group_both = lax.all_gather(relaid, "member", axis=0, tiled=True)
+    group_both = lax.all_gather(relaid, MEMBER, axis=0, tiled=True)
     group_passages = group_both[:, :width]
     group_hidden = group_both[:, width:]
     scores = contract(query_emb, group_passages, 1, 1) * factor
@@ -60,7 +64,7 @@
     local_weight = contract(query_hidden, query_grad, 0, 0) + contract(group_hidden, partial, 0, 0)
     weight_rows = width // members
     weight_pieces = lax.all_to_all(
-        local_weight.reshape(members, weight_rows, width), "member", 0, 0, tiled=True
+        local_weight.reshape(members, weight_rows, width), MEMBER, 0, 0, tiled=True
     )
     weight_share = jnp.sum(weight_pieces, axis=0)
     step = 1
@@ -68,18 +72,20 @@
         pairs = [(index, index ^ step) for index in range(groups)]
         weight_share = weight_share + lax.ppermute(weight_share, "group", pairs)
         step *= 2
-    grad_weight = lax.all_gather(weight_share, "member", axis=0, tiled=True) / devices
+    grad_weight = lax.all_gather(weight_share, MEMBER, axis=0, tiled=True) / devices
+    chips = lax.axis_size("chip")
+    core = lax.axis_index("core")
+    split = partial.reshape(chips, 2, rows, width)
+    kept = jnp.where(core == 0, split[:, 0], split[:, 1])
+    given = jnp.where(core == 0, split[:, 1], split[:, 0]).astype(jnp.bfloat16)
+    paired = kept + lax.ppermute(given, "core", [(0, 1), (1, 0)]).astype(jnp.float32)
     pieces = lax.all_to_all(
-        partial.astype(jnp.bfloat16).reshape(members, rows, width),
-        "member",
-        split_axis=0,
-        concat_axis=0,
-        tiled=True,
+        paired.astype(jnp.bfloat16), "chip", split_axis=0, concat_axis=0, tiled=True
     )
     relaid_grad = jnp.sum(pieces.astype(jnp.float32), axis=0).astype(jnp.bfloat16)
     back_rows = relaid_grad[jnp.minimum(got_slots, rows - 1)]
     returned = lax.all_to_all(
-        back_rows, ("group", "member"), split_axis=0, concat_axis=0, tiled=True
+        back_rows, ALL, split_axis=0, concat_axis=0, tiled=True
     )
     passage_grad = returned[position]
     grad_passage_hidden = contract(passage_grad, proj_weight, 1, 1).astype(jnp.bfloat16)
@@ -88,19 +94,23 @@
 
 
 def solution(mesh):
+    groups, members = mesh.devices.shape
+    mesh = jax.sharding.Mesh(
+        mesh.devices.reshape(groups, members // 2, 2), ("group", "chip", "core")
+    )
     in_specs = (
-        P(("group", "member"), None),
-        P(("group", "member"), None),
+        P(("group", "chip", "core"), None),
+        P(("group", "chip", "core"), None),
         P(),
-        P(("group", "member")),
-        P(("group", "member")),
-        P(("group", "member")),
-        P(("group", "member")),
+        P(("group", "chip", "core")),
+        P(("group", "chip", "core")),
+        P(("group", "chip", "core")),
+        P(("group", "chip", "core")),
     )
     out_specs = (
-        P(("group", "member")),
-        P(("group", "member"), None),
-        P(("group", "member"), None),
+        P(("group", "chip", "core")),
+        P(("group", "chip", "core"), None),
+        P(("group", "chip", "core"), None),
         P(),
     )
     return jax.shard_map(body, mesh=mesh, in_specs=in_specs, out_specs=out_specs, check_vma=False)

time: 302 us -> 284 us (0.940)
  waiting for transfers between devices: 141 us -> 111 us
  other arithmetic: 20.9 us -> 30.8 us
  matrix products: 25.7 us -> 31.9 us
  starting transfers between devices: 26.2 us -> 22.4 us
    all_to_all x2, waiting for transfers between devices: 78.3 us -> 48.9 us  [the longest x1 38.4 us: body(): lax.all_to_all(paired.astype(jnp.bfloat16), 'chip', split_axis=0, concat_...]
    convert_element_type x0 -> x2, other arithmetic: none -> 11.3 us  [the longest x1 8.58 us: body(): paired.astype(jnp.bfloat16)]
    dot_general x1, matrix products: 3.46 us -> 7.93 us  [body(): jnp.dot(coef, group_passages, preferred_element_type=jnp.float32)]
    all_to_all x2, starting transfers between devices: 21.9 us -> 17.6 us  [the longest x1 13 us: body(): lax.all_to_all(back_rows, ALL, split_axis=0, concat_axis=0, tiled=True)]
  transfers between devices with their start and end apart: 6 -> 7, of which waited for: 5 -> 5; matrix products, arithmetic and copies ran while one was open for 4% -> 13% of each run, Pallas kernels for 0% -> 0%
where the time goes in v6:
time: 284 us; the launch traced here: 283 us
  waiting for transfers between devices  111 us (39%)
  blocking collectives  64.9 us (23%)
  matrix products  31.9 us (11%)
  other arithmetic  30.8 us (11%)
  starting transfers between devices  22.4 us (8%)
  between operations  14.3 us (5%)
  local copies, waits for them, and re-layouts  8.46 us (3%)
    all_gather x1, waiting for transfers between devices, body(): group_both = lax.all_gather(relaid, MEMBER, axis=0, tiled=True)  57.4 us
    all_to_all x1, waiting for transfers between devices, body(): lax.all_to_all(paired.astype(jnp.bfloat16), 'chip', split_axis=0, concat_...  38.4 us
    all_to_all x1, blocking collectives, body(): lax.all_to_all(local_weight.reshape(members, weight_rows, width), MEMBER,...  36.7 us
    all_to_all x1, blocking collectives, body(): lax.all_to_all(send_rows, ALL, split_axis=0, concat_axis=0, tiled=True)  28.2 us
    dot_general x6, matrix products, contract(): lax.dot_general(left, right, (((left_dim,), (right_dim,)), ((), ())), pre...  20.8 us
    all_to_all x1, starting transfers between devices, body(): lax.all_to_all(back_rows, ALL, split_axis=0, concat_axis=0, tiled=True)  13 us
    all_to_all x1, waiting for transfers between devices, body(): lax.all_to_all(back_rows, ALL, split_axis=0, concat_axis=0, tiled=True)  10.5 us
    convert_element_type x1, other arithmetic, body(): paired.astype(jnp.bfloat16)  8.58 us
  transfers between devices with their start and end apart: 7, of which 5 were waited for; matrix products, arithmetic and copies ran while one was open for 13% of the time, Pallas kernels for 0%

profile of v6, /device:TPU:1, one launch (start us, length us, event | category | flops | bytes accessed | tf_op | source)
XLA Modules:
  0.0 283.4 jit_solution(14247015769897291554)
XLA Ops:
  7.2 0.0 all-gather.3.cloned.1.call-start
  7.2 0.8 fusion.25
  8.0 0.7 and_select_fusion.1
  8.7 0.2 convert_reduce_fusion
  8.9 1.3 convolution_convert_fusion.3
  10.2 0.1 broadcast_in_dim.11
  10.3 0.1 scatter.22
  10.3 2.1 scatter_custom_fusion
  12.5 0.3 all_to_all.22
  12.8 28.2 %all_to_all.34 = bf16[128,2,1664]{2,1,0:T(2,128)(2,1)} all-to-all(bf16[128,2,1664]{2,1,0:T(2,128)(2,1)S(1)} %all_to_all.22), channel_id=1, replica_groups=mesh['group'=4,'chip'=16,'core'=2] {'group','chip','core'}, dimensions={0} | all-to-all | bytes 1703936 | tf_op jit(solution)/shard_map/all_to_all | solution.py:45
  41.0 2.4 all_to_all.24
  43.4 0.2 fusion.23
  43.6 2.5 scatter_custom_fusion.1
  46.0 0.0 all-gather.3.cloned.1.call-update
  46.1 0.2 all-gather.5.cloned.1.call-start
  46.3 1.9 convolution_convert_fusion.1
  48.2 57.4 %all-gather.3.cloned.1.call-done = bf16[4096,1536]{1,0:T(8,128)(2,1)} async-done(((bf16[128,1536]{1,0:T(8,128)(2,1)}), bf16[4096,1536]{1,0:T(8,128)(2,1)}) %all-gather.3.cloned.1.call-update) | async-done | bytes 12582928 | tf_op jit(solution)/shard_map/all_gather | solution.py:49
  105.6 5.7 %multiply_reduce_fusion = (f32[512]{0:T(512)S(1)}, f32[512,4096]{1,0:T(8,128)S(1)}) fusion(bf16[512,768]{1,0:T(8,128)(2,1)S(1)} %convolution_convert_fusion.1, bf16[4096,1536]{1,0:T(8,128)(2,1)} %all-gather.3.cloned.1.call-done), kind=kOutput, calls=%fused_computation.8 | convolution fusion | flops 3225419264 | bytes 15468544 | tf_op jit(solution)/shard_map/dot_general | solution.py:14
  111.4 3.1 %select_reduce_fusion = (f32[512]{0:T(512)S(1)}, f32[512]{0:T(512)S(1)}) fusion(f32[512,4096]{1,0:T(8,128)S(1)} %get-tuple-element.25, s32[512]{0:T(512)S(1)} %copy-done.5, f32[512]{0:T(512)S(1)} %get-tuple-element.24), kind=kLoop, calls=%fused_computation.5 | loop fusion | flops 12581888 | bytes 8396800 | tf_op jit(solution)/shard_map/reduce_sum | solution.py:56
  114.5 0.6 fusion.26
  115.1 3.9 %multiply_convert_fusion = bf16[512,4096]{1,0:T(8,128)(2,1)S(1)} fusion(f32[512,4096]{1,0:T(8,128)S(1)} %get-tuple-element.25, f32[512]{0:T(512)S(1)} %get-tuple-element.21, f32[512]{0:T(512)S(1)} %copy-done.6, s32[512]{0:T(512)S(1)} %copy-done.5), kind=kLoop, calls=%fused_computation.4 | loop fusion | flops 16777216 | bytes 12589056 | tf_op jit(solution)/shard_map/convert_element_type | solution.py:59
  119.0 3.6 %fusion.27 = f32[4096,768]{1,0:T(8,128)S(1)} fusion(bf16[512,4096]{1,0:T(8,128)(2,1)S(1)} %multiply_convert_fusion, bf16[512,768]{1,0:T(8,128)(2,1)S(1)} %convolution_convert_fusion.1), kind=kOutput, calls=%fused_computation.57 | convolution fusion | flops 3221225472 | bytes 17563648 | tf_op jit(solution)/shard_map/dot_general | solution.py:14
  122.7 2.7 fusion.9
  125.4 0.3 collective-permute-start
  125.7 7.9 %fusion.10 = bf16[512,768]{1,0:T(8,128)(2,1)S(1)} fusion(bf16[512,4096]{1,0:T(8,128)(2,1)S(1)} %multiply_convert_fusion, bf16[4096,1536]{1,0:T(8,128)(2,1)} %all-gather.3.cloned.1.call-done), kind=kOutput, calls=%fused_computation.24 | convolution fusion | flops 3221618688 | bytes 11272192 | tf_op jit(solution)/shard_map/dot_general | solution.py:60
  133.6 7.6 %fusion = f32[768,768]{1,0:T(8,128)S(1)} fusion(f32[4096,768]{1,0:T(8,128)S(1)} %fusion.27, bf16[4096,1536]{1,0:T(8,128)(2,1)} %all-gather.3.cloned.1.call-done), kind=kOutput, calls=%fused_computation.9 | convolution fusion | flops 4831838208 | bytes 21233664 | tf_op jit(solution)/shard_map/dot_general | solution.py:14
  141.3 0.9 bitcast_add_fusion
  142.2 36.7 %all_to_all.35 = f32[32,24,768]{2,1,0:T(8,128)S(1)} all-to-all(f32[32,24,768]{2,1,0:T(8,128)S(1)} %bitcast.47), channel_id=1, replica_groups=mesh['group'=4,'chip'=16,'core'=2] {'chip','core'}, dimensions={0} | all-to-all | bytes 4718592 | tf_op jit(solution)/shard_map/all_to_all | solution.py:66
  178.9 0.8 reduce_sum.52
  179.6 1.3 collective-permute-start.1
  180.9 2.6 collective-permute-done.1
  183.5 0.9 add.57
  184.4 2.9 %collective-permute-start.2 = (f32[24,768]{1,0:T(8,128)S(1)}, f32[24,768]{1,0:T(8,128)S(1)}, u32[]{:S(2)}, u32[]{:S(2)}) collective-permute-start(f32[24,768]{1,0:T(8,128)S(1)} %add.57), channel_id=1, source_target_pairs={{0,64},{32,96},{64,0},{96,32},{1,65},{33,97},{65,1},{97,33},{2,66}... | collective-permute-start | bytes 221192 | tf_op jit(solution)/shard_map/ppermute | solution.py:73
  187.3 1.8 collective-permute-done.2
  189.1 0.6 add.58
  189.8 8.6 %fusion.4 = bf16[16,128,768]{2,1,0:T(8,128)(2,1)} fusion(bf16[16,128,768]{2,1,0:T(8,128)(2,1)} %collective-permute-done, f32[16,2,128,768]{3,2,1,0:T(8,128)} %bitcast.46, pred[]{:T(512)S(6)} %eq.38), kind=kLoop, calls=%fused_computation.14 | loop fusion | flops 6291456 | bytes 18874368 | tf_op jit(solution)/shard_map/convert_element_type | solution.py:83
  198.4 4.6 %all-to-all-start.1 = ((bf16[16,128,768]{2,1,0:T(8,128)(2,1)}), bf16[16,128,768]{2,1,0:T(8,128)(2,1)}, u32[]{:S(2)}, u32[]{:S(2)}) async-start(bf16[16,128,768]{2,1,0:T(8,128)(2,1)} %fusion.4), calls=%async_computation.1 | async-start | bytes 6291456 | tf_op jit(solution)/shard_map/all_to_all | solution.py:82
  203.0 38.4 %all-to-all-done.1 = bf16[16,128,768]{2,1,0:T(8,128)(2,1)} async-done(((bf16[16,128,768]{2,1,0:T(8,128)(2,1)}), bf16[16,128,768]{2,1,0:T(8,128)(2,1)}, u32[]{:S(2)}, u32[]{:S(2)}) %all-to-all-start.1) | async-done | bytes 3145760 | tf_op jit(solution)/shard_map/all_to_all | solution.py:82
  241.4 2.4 reduce_sum.51
  243.8 1.2 gather_fusion
  245.0 0.9 all_to_all.26
  245.9 13.0 %all-to-all-start.2 = ((bf16[128,2,768]{2,1,0:T(2,128)(2,1)}), bf16[128,2,768]{2,1,0:T(2,128)(2,1)S(1)}, u32[]{:S(2)}, u32[]{:S(2)}) async-start(bf16[128,2,768]{2,1,0:T(2,128)(2,1)} %all_to_all.26), calls=%async_computation.2 | async-start | bytes 786432 | tf_op jit(solution)/shard_map/all_to_all | solution.py:87
  259.0 1.7 convolution_convert_fusion
  260.7 10.5 %all-to-all-done.2 = bf16[128,2,768]{2,1,0:T(2,128)(2,1)S(1)} async-done(((bf16[128,2,768]{2,1,0:T(2,128)(2,1)}), bf16[128,2,768]{2,1,0:T(2,128)(2,1)S(1)}, u32[]{:S(2)}, u32[]{:S(2)}) %all-to-all-start.2) | async-done | bytes 393248 | tf_op jit(solution)/shard_map/all_to_all | solution.py:87
  271.1 0.1 all_to_all.28
  271.3 0.9 gather_fusion.1
  272.2 1.2 convolution_convert_fusion.2
  273.4 3.2 %broadcast_multiply_fusion = f32[768,768]{1,0:T(8,128)} fusion(f32[768,768]{1,0:T(8,128)} %all-gather.5.cloned.1.call-done), kind=kLoop, calls=%fused_computation.25 | loop fusion | flops 589824 | bytes 4718592 | tf_op jit(solution)/shard_map/div | solution.py:75
  (22 shorter events, 0.1 us)
Async XLA Ops:
  7.2 1.7 copy-start
  7.2 98.5 %all-gather.3.cloned.1.call-start = ((), (), s32[]{:S(2)}) async-start(), calls=%async_computation.4 | async-start | bytes 12976128 | tf_op jit(solution)/shard_map/all_gather | solution.py:49
  46.1 227.3 %all-gather.5.cloned.1.call-start = ((), (), s32[]{:S(2)}) async-start(), calls=%async_computation.5 | async-start | bytes 2433024 | tf_op jit(solution)/shard_map/all_gather | solution.py:75
  48.2 63.2 %copy-start.5 = (s32[512]{0:T(512)S(1)}, s32[512]{0:T(512)}, u32[]{:S(2)}) copy-start(s32[512]{0:T(512)} %param.14) | copy-start | bytes 6148
  111.4 3.7 %copy-start.6 = (f32[512]{0:T(512)S(1)}, f32[512]{0:T(512)}, u32[]{:S(2)}) copy-start(f32[512]{0:T(512)} %param.15) | copy-start | bytes 6148
  122.6 11.0 %copy-start.1 = (f32[4096,768]{1,0:T(8,128)}, f32[4096,768]{1,0:T(8,128)S(1)}, u32[]{:S(2)}) copy-start(f32[4096,768]{1,0:T(8,128)S(1)} %fusion.27) | copy-start | bytes 37748740
  125.4 64.4 %collective-permute-start = (bf16[16,128,768]{2,1,0:T(8,128)(2,1)}, bf16[16,128,768]{2,1,0:T(8,128)(2,1)}, u32[]{:S(2)}, u32[]{:S(2)}) collective-permute-start(bf16[16,128,768]{2,1,0:T(8,128)(2,1)} %fusion.9), channel_id=1, source_target_pairs={{0,1},{1,0},{2,3},{3,2},{4,5},{5,4},{6,7},{7,6},{8,9},{9,8},{10,11... | collective-permute-start | bytes 9437192 | tf_op jit(solution)/shard_map/ppermute | solution.py:81
  133.6 7.7 %copy-start.3 = (bf16[512,768]{1,0:T(8,128)(2,1)}, bf16[512,768]{1,0:T(8,128)(2,1)S(1)}, u32[]{:S(2)}) copy-start(bf16[512,768]{1,0:T(8,128)(2,1)S(1)} %fusion.10) | copy-start | bytes 2359300
  133.6 7.7 %copy-start.2 = (bf16[512,768]{1,0:T(8,128)(2,1)S(1)}, bf16[512,768]{1,0:T(8,128)(2,1)}, u32[]{:S(2)}) copy-start(bf16[512,768]{1,0:T(8,128)(2,1)} %param.10) | copy-start | bytes 2359300
  179.6 3.8 %collective-permute-start.1 = (f32[24,768]{1,0:T(8,128)}, f32[24,768]{1,0:T(8,128)S(1)}, u32[]{:S(2)}, u32[]{:S(2)}) collective-permute-start(f32[24,768]{1,0:T(8,128)} %reduce_sum.52), channel_id=1, source_target_pairs={{0,32},{32,0},{64,96},{96,64},{1,33},{33,1},{65,97},{97,65},{2,34}... | collective-permute-start | bytes 221192 | tf_op jit(solution)/shard_map/ppermute | solution.py:73
  184.4 4.8 %collective-permute-start.2 = (f32[24,768]{1,0:T(8,128)S(1)}, f32[24,768]{1,0:T(8,128)S(1)}, u32[]{:S(2)}, u32[]{:S(2)}) collective-permute-start(f32[24,768]{1,0:T(8,128)S(1)} %add.57), channel_id=1, source_target_pairs={{0,64},{32,96},{64,0},{96,32},{1,65},{33,97},{65,1},{97,33},{2,66}... | collective-permute-start | bytes 221192 | tf_op jit(solution)/shard_map/ppermute | solution.py:73
  198.4 60.6 %copy-start.4 = (bf16[512,768]{1,0:T(8,128)(2,1)S(1)}, bf16[512,768]{1,0:T(8,128)(2,1)}, u32[]{:S(2)}) copy-start(bf16[512,768]{1,0:T(8,128)(2,1)} %copy-done.3) | copy-start | bytes 2359300
  198.4 43.0 %all-to-all-start.1 = ((bf16[16,128,768]{2,1,0:T(8,128)(2,1)}), bf16[16,128,768]{2,1,0:T(8,128)(2,1)}, u32[]{:S(2)}, u32[]{:S(2)}) async-start(bf16[16,128,768]{2,1,0:T(8,128)(2,1)} %fusion.4), calls=%async_computation.1 | async-start | bytes 6291456 | tf_op jit(solution)/shard_map/all_to_all | solution.py:82
  245.9 25.2 %all-to-all-start.2 = ((bf16[128,2,768]{2,1,0:T(2,128)(2,1)}), bf16[128,2,768]{2,1,0:T(2,128)(2,1)S(1)}, u32[]{:S(2)}, u32[]{:S(2)}) async-start(bf16[128,2,768]{2,1,0:T(2,128)(2,1)} %all_to_all.26), calls=%async_computation.2 | async-start | bytes 786432 | tf_op jit(solution)/shard_map/all_to_all | solution.py:87
Sparse Core Ops, SparseCore 0:
  46.2 59.4 all-gather.2
  189.9 65.5 all-gather.4

commit v7 on v6

--- a/solution.py
+++ b/solution.py
@@ -46,7 +46,18 @@
     got_rows = got[:, : 2 * width]
     got_slots = got[:, 2 * width].astype(jnp.int32)
     relaid = jnp.zeros((rows, 2 * width), jnp.bfloat16).at[got_slots].set(got_rows, mode="drop")
-    group_both = lax.all_gather(relaid, MEMBER, axis=0, tiled=True)
+    chips = lax.axis_size("chip")
+    core = lax.axis_index("core")
+    swap = [(0, 1), (1, 0)]
+    chip_both = lax.all_gather(relaid, "chip", axis=0, tiled=True)
+    group_both = jnp.concatenate([chip_both, lax.ppermute(chip_both, "core", swap)], axis=0)
+    half = chips * rows
+    positive_member = positive // rows
+    positive = (
+        jnp.where(positive_member % 2 == core, 0, half)
+        + positive_member // 2 * rows
+        + positive % rows
+    )
     group_passages = group_both[:, :width]
     group_hidden = group_both[:, width:]
     scores = contract(query_emb, group_passages, 1, 1) * factor
@@ -63,9 +74,11 @@
     partial = contract(coef, query_emb, 0, 0)
     local_weight = contract(query_hidden, query_grad, 0, 0) + contract(group_hidden, partial, 0, 0)
     weight_rows = width // members
-    weight_pieces = lax.all_to_all(
-        local_weight.reshape(members, weight_rows, width), MEMBER, 0, 0, tiled=True
-    )
+    weight_split = local_weight.reshape(chips, 2, weight_rows, width)
+    weight_kept = jnp.where(core == 0, weight_split[:, 0], weight_split[:, 1])
+    weight_given = jnp.where(core == 0, weight_split[:, 1], weight_split[:, 0])
+    weight_paired = weight_kept + lax.ppermute(weight_given, "core", swap)
+    weight_pieces = lax.all_to_all(weight_paired, "chip", 0, 0, tiled=True)
     weight_share = jnp.sum(weight_pieces, axis=0)
     step = 1
     while step < groups:
@@ -73,12 +86,9 @@
         weight_share = weight_share + lax.ppermute(weight_share, "group", pairs)
         step *= 2
     grad_weight = lax.all_gather(weight_share, MEMBER, axis=0, tiled=True) / devices
-    chips = lax.axis_size("chip")
-    core = lax.axis_index("core")
-    split = partial.reshape(chips, 2, rows, width)
-    kept = jnp.where(core == 0, split[:, 0], split[:, 1])
-    given = jnp.where(core == 0, split[:, 1], split[:, 0]).astype(jnp.bfloat16)
-    paired = kept + lax.ppermute(given, "core", [(0, 1), (1, 0)]).astype(jnp.float32)
+    kept = partial[:half].reshape(chips, rows, width)
+    given = partial[half:].reshape(chips, rows, width).astype(jnp.bfloat16)
+    paired = kept + lax.ppermute(given, "core", swap).astype(jnp.float32)
     pieces = lax.all_to_all(
         paired.astype(jnp.bfloat16), "chip", split_axis=0, concat_axis=0, tiled=True
     )

time: 284 us -> 275 us (0.968)
  blocking collectives: 64.9 us -> 50.6 us
  local copies, waits for them, and re-layouts: 8.46 us -> 19.8 us
  other arithmetic: 30.8 us -> 24.5 us
  matrix products: 31.9 us -> 26.6 us
  waiting for transfers between devices: 111 us -> 114 us
    all_to_all x1, blocking collectives: 36.7 us -> 22.4 us  [body(): weight_pieces = lax.all_to_all(weight_paired, 'chip', 0, 0, tiled=True)]
    ppermute x1 -> x3, waiting for transfers between devices: 0.01 us -> 5.08 us  [the longest x1 4.69 us: body(): lax.ppermute(chip_both, 'core', swap)]
    slice x0 -> x3, local copies, waits for them, and re-layouts: none -> 4.72 us  [the longest x2 2.77 us: body(): kept = partial[:half].reshape(chips, rows, width)]
    dot_general x1, matrix products: 7.93 us -> 3.44 us  [body(): jnp.dot(coef, group_passages, preferred_element_type=jnp.float32)]
    convert_element_type x1, other arithmetic: 8.58 us -> 4.36 us  [body(): paired.astype(jnp.bfloat16)]
    unnamed x14 -> x17, local copies, waits for them, and re-layouts: 0.04 us -> 3.52 us
    concatenate x0 -> x1, local copies, waits for them, and re-layouts: none -> 3.19 us  [body(): jnp.concatenate([chip_both, lax.ppermute(chip_both, 'core', swap)], axis=0)]
  transfers between devices with their start and end apart: 7 -> 9, of which waited for: 5 -> 7; matrix products, arithmetic and copies ran while one was open for 13% -> 7% of each run, Pallas kernels for 0% -> 0%
where the time goes in v7:
time: 275 us; the launch traced here: 274 us
  waiting for transfers between devices  114 us (41%)
  blocking collectives  50.6 us (18%)
  matrix products  26.6 us (10%)
  other arithmetic  24.5 us (9%)
  starting transfers between devices  24.3 us (9%)
  local copies, waits for them, and re-layouts  19.8 us (7%)
  between operations  14.3 us (5%)
    all_gather x1, waiting for transfers between devices, body(): chip_both = lax.all_gather(relaid, 'chip', axis=0, tiled=True)  57.4 us
    all_to_all x1, waiting for transfers between devices, body(): lax.all_to_all(paired.astype(jnp.bfloat16), 'chip', split_axis=0, concat_...  36.9 us
    all_to_all x1, blocking collectives, body(): lax.all_to_all(send_rows, ALL, split_axis=0, concat_axis=0, tiled=True)  28.2 us
    all_to_all x1, blocking collectives, body(): weight_pieces = lax.all_to_all(weight_paired, 'chip', 0, 0, tiled=True)  22.4 us
    dot_general x6, matrix products, contract(): lax.dot_general(left, right, (((left_dim,), (right_dim,)), ((), ())), pre...  20 us
    all_to_all x1, starting transfers between devices, body(): lax.all_to_all(back_rows, ALL, split_axis=0, concat_axis=0, tiled=True)  14 us
    all_to_all x1, waiting for transfers between devices, body(): lax.all_to_all(back_rows, ALL, split_axis=0, concat_axis=0, tiled=True)  10.5 us
  transfers between devices with their start and end apart: 9, of which 7 were waited for; matrix products, arithmetic and copies ran while one was open for 7% of the time, Pallas kernels for 0%

profile of v7, /device:TPU:1, one launch (start us, length us, event | category | flops | bytes accessed | tf_op | source)
XLA Modules:
  0.0 274.3 jit_solution(16754641150239423233)
XLA Ops:
  7.2 0.8 fusion.32
  8.0 0.7 and_select_fusion.1
  8.7 0.2 convert_reduce_fusion
  8.9 1.3 convolution_convert_fusion.3
  10.3 2.1 scatter_custom_fusion
  12.5 0.3 all_to_all.22
  12.8 28.2 %all_to_all.34 = bf16[128,2,1664]{2,1,0:T(2,128)(2,1)} all-to-all(bf16[128,2,1664]{2,1,0:T(2,128)(2,1)S(1)} %all_to_all.22), channel_id=1, replica_groups=mesh['group'=4,'chip'=16,'core'=2] {'group','chip','core'}, dimensions={0} | all-to-all | bytes 1703936 | tf_op jit(solution)/shard_map/all_to_all | solution.py:45
  41.1 2.4 all_to_all.24
  43.4 0.2 fusion.23
  43.6 2.5 scatter_custom_fusion.1
  46.1 57.4 %all-gather.3.cloned.1.call-done = bf16[2048,1536]{1,0:T(8,128)(2,1)} async-done(((bf16[128,1536]{1,0:T(8,128)(2,1)}), bf16[2048,1536]{1,0:T(8,128)(2,1)}) %all-gather.3.cloned.1.call-update) | async-done | bytes 6291472 | tf_op jit(solution)/shard_map/all_gather | solution.py:52
  103.5 0.8 collective-permute-start
  104.4 1.9 convolution_convert_fusion.1
  106.3 3.5 %constant_dynamic-update-slice_fusion.1 = bf16[4096,1536]{1,0:T(8,128)(2,1)S(1)} fusion(bf16[2048,1536]{1,0:T(8,128)(2,1)} %all-gather.3.cloned.1.call-done), kind=kLoop, calls=%fused_computation.48 | loop fusion | bytes 12582912
  109.8 4.7 %collective-permute-done = bf16[2048,1536]{1,0:T(8,128)(2,1)} collective-permute-done((bf16[2048,1536]{1,0:T(8,128)(2,1)}, bf16[2048,1536]{1,0:T(8,128)(2,1)}, u32[]{:S(2)}, u32[]{:S(2)}) %collective-permute-start) | collective-permute-done | bytes 6291488 | tf_op jit(solution)/shard_map/ppermute | solution.py:53
  114.5 3.2 %constant_dynamic-update-slice_fusion = bf16[4096,1536]{1,0:T(8,128)(2,1)S(1)} fusion(bf16[4096,1536]{1,0:T(8,128)(2,1)S(1)} %constant_dynamic-update-slice_fusion.1, bf16[2048,1536]{1,0:T(8,128)(2,1)} %collective-permute-done), kind=kLoop, calls=%fused_computation.47 | loop fusion | bytes 12582912 | tf_op jit(solution)/shard_map/concatenate | solution.py:53
  117.7 3.5 %multiply_reduce_fusion = (f32[512]{0:T(512)S(1)}, f32[512,4096]{1,0:T(8,128)S(1)}) fusion(bf16[512,768]{1,0:T(8,128)(2,1)S(1)} %convolution_convert_fusion.1, bf16[4096,1536]{1,0:T(8,128)(2,1)S(1)} %constant_dynamic-update-slice_fusion), kind=kOutput, calls=%fused_computation.8 | convolution fusion | flops 3225419264 | bytes 15468544 | tf_op jit(solution)/shard_map/dot_general | solution.py:14
  121.2 3.3 %select_reduce_fusion = (f32[512]{0:T(512)S(1)}, f32[512]{0:T(512)S(1)}) fusion(f32[512,4096]{1,0:T(8,128)S(1)} %get-tuple-element.25, s32[512]{0:T(512)S(1)} %fusion.28, f32[512]{0:T(512)S(1)} %get-tuple-element.24), kind=kLoop, calls=%fused_computation.5 | loop fusion | flops 12581888 | bytes 8396800 | tf_op jit(solution)/shard_map/reduce_sum | solution.py:67
  124.5 0.6 fusion.33
  125.1 3.9 %multiply_convert_fusion = bf16[512,4096]{1,0:T(8,128)(2,1)S(1)} fusion(f32[512,4096]{1,0:T(8,128)S(1)} %get-tuple-element.25, f32[512]{0:T(512)S(1)} %get-tuple-element.21, f32[512]{0:T(512)S(1)} %copy-done.4, s32[512]{0:T(512)S(1)} %fusion.28), kind=kLoop, calls=%fused_computation.4 | loop fusion | flops 16777216 | bytes 12589056 | tf_op jit(solution)/shard_map/convert_element_type | solution.py:70
  129.0 3.5 %fusion.34 = f32[4096,768]{1,0:T(8,128)S(1)} fusion(bf16[512,4096]{1,0:T(8,128)(2,1)S(1)} %multiply_convert_fusion, bf16[512,768]{1,0:T(8,128)(2,1)S(1)} %copy-done.7), kind=kOutput, calls=%fused_computation.78 | convolution fusion | flops 3221225472 | bytes 17563648 | tf_op jit(solution)/shard_map/dot_general | solution.py:14
  132.6 3.4 %fusion.8 = bf16[512,768]{1,0:T(8,128)(2,1)S(1)} fusion(bf16[512,4096]{1,0:T(8,128)(2,1)S(1)} %multiply_convert_fusion, bf16[4096,1536]{1,0:T(8,128)(2,1)S(1)} %constant_dynamic-update-slice_fusion), kind=kOutput, calls=%fused_computation.20 | convolution fusion | flops 3221618688 | bytes 11272192 | tf_op jit(solution)/shard_map/dot_general | solution.py:71
  136.0 2.2 fusion.35
  138.3 7.8 %bitcast_add_fusion = f32[768,768]{1,0:T(8,128)} fusion(f32[768,768]{0,1:T(8,128)} %fusion.35, f32[4096,768]{1,0:T(8,128)S(1)} %fusion.34, bf16[4096,1536]{1,0:T(8,128)(2,1)S(1)} %constant_dynamic-update-slice_fusion), kind=kOutput, calls=%fused_computation.17 | convolution fusion | flops 4832428032 | bytes 23592960 | tf_op jit(solution)/shard_map/dot_general | solution.py:14
  146.1 1.9 select_bitcast_fusion
  148.0 0.5 collective-permute-start.2
  148.5 2.0 slice.82
  150.6 0.4 collective-permute-done.2
  150.9 0.2 fusion.12
  151.1 22.4 %all_to_all.35 = f32[16,24,768]{2,1,0:T(8,128)S(1)} all-to-all(f32[16,24,768]{2,1,0:T(8,128)S(1)} %fusion.12), channel_id=1, replica_groups=mesh['group'=4,'chip'=16,'core'=2] {'chip'}, dimensions={0} | all-to-all | bytes 2359296 | tf_op jit(solution)/shard_map/all_to_all | solution.py:81
  173.6 1.4 collective-permute-start.3
  174.9 1.9 collective-permute-done.3
  176.9 2.9 %collective-permute-start.4 = (f32[24,768]{1,0:T(8,128)S(1)}, f32[24,768]{1,0:T(8,128)S(1)}, u32[]{:S(2)}, u32[]{:S(2)}) collective-permute-start(f32[24,768]{1,0:T(8,128)S(1)} %add.83), channel_id=1, source_target_pairs={{0,64},{32,96},{64,0},{96,32},{1,65},{33,97},{65,1},{97,33},{2,66}... | collective-permute-start | bytes 221192 | tf_op jit(solution)/shard_map/ppermute | solution.py:86
  179.8 2.4 collective-permute-done.4
  182.2 0.6 add.84
  182.9 2.8 %slice-done = f32[2048,768]{1,0:T(8,128)S(1)} async-done(((f32[4096,768]{1,0:T(8,128)}), f32[2048,768]{1,0:T(8,128)S(1)}, s32[]{:S(2)}) %slice-start) | async-done | bytes 6291480 | tf_op jit(solution)/shard_map/slice | solution.py:89
  185.7 4.4 %add_convert_fusion = bf16[16,128,768]{2,1,0:T(8,128)(2,1)} fusion(f32[16,128,768]{2,1,0:T(8,128)S(1)} %bitcast.38, bf16[16,128,768]{2,1,0:T(8,128)(2,1)} %collective-permute-done.1), kind=kLoop, calls=%fused_computation.12 | loop fusion | flops 4718592 | bytes 12582912 | tf_op jit(solution)/shard_map/convert_element_type | solution.py:93
  190.0 4.5 %all-to-all-start.1 = ((bf16[16,128,768]{2,1,0:T(8,128)(2,1)}), bf16[16,128,768]{2,1,0:T(8,128)(2,1)}, u32[]{:S(2)}, u32[]{:S(2)}) async-start(bf16[16,128,768]{2,1,0:T(8,128)(2,1)} %add_convert_fusion), calls=%async_computation.1 | async-start | bytes 6291456 | tf_op jit(solution)/shard_map/all_to_all | solution.py:92
  194.5 36.9 %all-to-all-done.1 = bf16[16,128,768]{2,1,0:T(8,128)(2,1)} async-done(((bf16[16,128,768]{2,1,0:T(8,128)(2,1)}), bf16[16,128,768]{2,1,0:T(8,128)(2,1)}, u32[]{:S(2)}, u32[]{:S(2)}) %all-to-all-start.1) | async-done | bytes 3145760 | tf_op jit(solution)/shard_map/all_to_all | solution.py:92
  231.4 2.3 reduce_sum.51
  233.7 1.2 gather_fusion
  234.9 0.9 all_to_all.26
  235.8 14.0 %all-to-all-start.2 = ((bf16[128,2,768]{2,1,0:T(2,128)(2,1)}), bf16[128,2,768]{2,1,0:T(2,128)(2,1)S(1)}, u32[]{:S(2)}, u32[]{:S(2)}) async-start(bf16[128,2,768]{2,1,0:T(2,128)(2,1)} %all_to_all.26), calls=%async_computation.2 | async-start | bytes 786432 | tf_op jit(solution)/shard_map/all_to_all | solution.py:97
  249.8 1.7 convolution_convert_fusion
  251.5 10.5 %all-to-all-done.2 = bf16[128,2,768]{2,1,0:T(2,128)(2,1)S(1)} async-done(((bf16[128,2,768]{2,1,0:T(2,128)(2,1)}), bf16[128,2,768]{2,1,0:T(2,128)(2,1)S(1)}, u32[]{:S(2)}, u32[]{:S(2)}) %all-to-all-start.2) | async-done | bytes 393248 | tf_op jit(solution)/shard_map/all_to_all | solution.py:97
  262.1 0.9 gather_fusion.1
  263.0 1.2 convolution_convert_fusion.2
  264.2 3.2 %broadcast_multiply_fusion = f32[768,768]{1,0:T(8,128)} fusion(f32[768,768]{1,0:T(8,128)} %all-gather.5.cloned.1.call-done), kind=kLoop, calls=%fused_computation.24 | loop fusion | flops 589824 | bytes 4718592 | tf_op jit(solution)/shard_map/div | solution.py:88
  (35 shorter events, 0.7 us)
Async XLA Ops:
  7.2 1.7 copy-start
  7.2 97.2 %copy-start.5 = (s32[512]{0:T(512)S(1)}, s32[512]{0:T(512)}, u32[]{:S(2)}) copy-start(s32[512]{0:T(512)} %param.14) | copy-start | bytes 6148
  7.2 96.3 %all-gather.3.cloned.1.call-start = ((), (), s32[]{:S(2)}) async-start(), calls=%async_computation.4 | async-start | bytes 6684672 | tf_op jit(solution)/shard_map/all_gather | solution.py:52
  46.1 218.2 %all-gather.5.cloned.1.call-start = ((), (), s32[]{:S(2)}) async-start(), calls=%async_computation.5 | async-start | bytes 2433024 | tf_op jit(solution)/shard_map/all_gather | solution.py:88
  103.5 11.0 %collective-permute-start = (bf16[2048,1536]{1,0:T(8,128)(2,1)}, bf16[2048,1536]{1,0:T(8,128)(2,1)}, u32[]{:S(2)}, u32[]{:S(2)}) collective-permute-start(bf16[2048,1536]{1,0:T(8,128)(2,1)} %all-gather.3.cloned.1.call-done), channel_id=1, source_target_pairs={{0,1},{1,0},{2,3},{3,2},{4,5},{5,4},{6,7},{7,6},{8,9},{9,8},{10,11... | collective-permute-start | bytes 18874376 | tf_op jit(solution)/shard_map/ppermute | solution.py:53
  106.3 11.4 %copy-start.6 = (bf16[512,768]{1,0:T(8,128)(2,1)}, bf16[512,768]{1,0:T(8,128)(2,1)S(1)}, u32[]{:S(2)}) copy-start(bf16[512,768]{1,0:T(8,128)(2,1)S(1)} %convolution_convert_fusion.1) | copy-start | bytes 2359300
  121.2 3.9 %copy-start.4 = (f32[512]{0:T(512)S(1)}, f32[512]{0:T(512)}, u32[]{:S(2)}) copy-start(f32[512]{0:T(512)} %param.15) | copy-start | bytes 6148
  125.1 3.9 %copy-start.7 = (bf16[512,768]{1,0:T(8,128)(2,1)S(1)}, bf16[512,768]{1,0:T(8,128)(2,1)}, u32[]{:S(2)}) copy-start(bf16[512,768]{1,0:T(8,128)(2,1)} %copy-done.6) | copy-start | bytes 2359300
  132.6 15.9 %copy-start.1 = (f32[4096,768]{1,0:T(8,128)}, f32[4096,768]{1,0:T(8,128)S(1)}, u32[]{:S(2)}) copy-start(f32[4096,768]{1,0:T(8,128)S(1)} %fusion.34) | copy-start | bytes 37748740
  132.6 3.5 %copy-start.3 = (bf16[512,768]{1,0:T(8,128)(2,1)S(1)}, bf16[512,768]{1,0:T(8,128)(2,1)}, u32[]{:S(2)}) copy-start(bf16[512,768]{1,0:T(8,128)(2,1)} %param.10) | copy-start | bytes 2359300
  146.1 4.9 %copy-start.2 = (f32[768,768]{1,0:T(8,128)S(1)}, f32[768,768]{1,0:T(8,128)}, u32[]{:S(2)}) copy-start(f32[768,768]{1,0:T(8,128)} %bitcast_add_fusion) | copy-start | bytes 7077892
  148.0 2.9 %collective-permute-start.2 = (f32[16,24,768]{2,1,0:T(8,128)S(1)}, f32[16,24,768]{2,1,0:T(8,128)S(1)}, u32[]{:S(2)}, u32[]{:S(2)}) collective-permute-start(f32[16,24,768]{2,1,0:T(8,128)S(1)} %select_bitcast_fusion), channel_id=1, source_target_pairs={{0,1},{1,0},{2,3},{3,2},{4,5},{5,4},{6,7},{7,6},{8,9},{9,8},{10,11... | collective-permute-start | bytes 3538952 | tf_op jit(solution)/shard_map/ppermute | solution.py:80
  150.4 32.5 %collective-permute-start.1 = (bf16[16,128,768]{2,1,0:T(8,128)(2,1)}, bf16[16,128,768]{2,1,0:T(8,128)(2,1)}, u32[]{:S(2)}, u32[]{:S(2)}) collective-permute-start(bf16[16,128,768]{2,1,0:T(8,128)(2,1)} %bitcast.1), channel_id=1, source_target_pairs={{0,1},{1,0},{2,3},{3,2},{4,5},{5,4},{6,7},{7,6},{8,9},{9,8},{10,11... | collective-permute-start | bytes 9437192 | tf_op jit(solution)/shard_map/ppermute | solution.py:91
  173.6 3.3 %collective-permute-start.3 = (f32[24,768]{1,0:T(8,128)S(1)}, f32[24,768]{1,0:T(8,128)S(1)}, u32[]{:S(2)}, u32[]{:S(2)}) collective-permute-start(f32[24,768]{1,0:T(8,128)S(1)} %reduce_sum.52), channel_id=1, source_target_pairs={{0,32},{32,0},{64,96},{96,64},{1,33},{33,1},{65,97},{97,65},{2,34}... | collective-permute-start | bytes 221192 | tf_op jit(solution)/shard_map/ppermute | solution.py:86
  176.9 5.3 %collective-permute-start.4 = (f32[24,768]{1,0:T(8,128)S(1)}, f32[24,768]{1,0:T(8,128)S(1)}, u32[]{:S(2)}, u32[]{:S(2)}) collective-permute-start(f32[24,768]{1,0:T(8,128)S(1)} %add.83), channel_id=1, source_target_pairs={{0,64},{32,96},{64,0},{96,32},{1,65},{33,97},{65,1},{97,33},{2,66}... | collective-permute-start | bytes 221192 | tf_op jit(solution)/shard_map/ppermute | solution.py:86
  182.9 2.8 %slice-start = ((f32[4096,768]{1,0:T(8,128)}), f32[2048,768]{1,0:T(8,128)S(1)}, s32[]{:S(2)}) async-start(f32[4096,768]{1,0:T(8,128)} %copy-done.1), calls=%async_computation.6 | async-start | bytes 12582912 | tf_op jit(solution)/shard_map/slice | solution.py:89
  190.0 41.4 %all-to-all-start.1 = ((bf16[16,128,768]{2,1,0:T(8,128)(2,1)}), bf16[16,128,768]{2,1,0:T(8,128)(2,1)}, u32[]{:S(2)}, u32[]{:S(2)}) async-start(bf16[16,128,768]{2,1,0:T(8,128)(2,1)} %add_convert_fusion), calls=%async_computation.1 | async-start | bytes 6291456 | tf_op jit(solution)/shard_map/all_to_all | solution.py:92
  235.8 26.2 %all-to-all-start.2 = ((bf16[128,2,768]{2,1,0:T(2,128)(2,1)}), bf16[128,2,768]{2,1,0:T(2,128)(2,1)S(1)}, u32[]{:S(2)}, u32[]{:S(2)}) async-start(bf16[128,2,768]{2,1,0:T(2,128)(2,1)} %all_to_all.26), calls=%async_computation.2 | async-start | bytes 786432 | tf_op jit(solution)/shard_map/all_to_all | solution.py:97
Sparse Core Ops, SparseCore 0:
  46.2 57.2 all-gather.2
  183.0 65.6 all-gather.4

commit v8 on v6

--- a/solution.py
+++ b/solution.py
@@ -62,25 +62,38 @@
     )
     partial = contract(coef, query_emb, 0, 0)
     local_weight = contract(query_hidden, query_grad, 0, 0) + contract(group_hidden, partial, 0, 0)
+    chips = lax.axis_size("chip")
+    core = lax.axis_index("core")
+    swap = [(0, 1), (1, 0)]
+    split = partial.reshape(chips, 2, rows, width)
+    kept = jnp.where(core == 0, split[:, 0], split[:, 1])
+    given = jnp.where(core == 0, split[:, 1], split[:, 0]).astype(jnp.bfloat16)
+    paired = (kept + lax.ppermute(given, "core", swap).astype(jnp.float32)).astype(jnp.bfloat16)
+    paired, local_weight = lax.optimization_barrier((paired, local_weight))
     weight_rows = width // members
-    weight_pieces = lax.all_to_all(
-        local_weight.reshape(members, weight_rows, width), MEMBER, 0, 0, tiled=True
-    )
-    weight_share = jnp.sum(weight_pieces, axis=0)
+    weight_split = local_weight.reshape(chips, 2, weight_rows, width)
+    weight_kept = jnp.where(core == 0, weight_split[:, 0], weight_split[:, 1])
+    weight_given = jnp.where(core == 0, weight_split[:, 1], weight_split[:, 0])
+    weight_share = weight_kept + lax.ppermute(weight_given, "core", swap)
+    chip = lax.axis_index("chip")
+    bit = chips // 2
+    while bit >= 1:
+        halves = weight_share.reshape(2, -1, weight_rows, width)
+        upper = (chip // bit) % 2 == 1
+        kept = jnp.where(upper, halves[1], halves[0])
+        given = jnp.where(upper, halves[0], halves[1])
+        pairs = [(index, index ^ bit) for index in range(chips)]
+        weight_share = kept + lax.ppermute(given, "chip", pairs)
+        bit //= 2
+    weight_share = weight_share.reshape(weight_rows, width)
     step = 1
     while step < groups:
         pairs = [(index, index ^ step) for index in range(groups)]
         weight_share = weight_share + lax.ppermute(weight_share, "group", pairs)
         step *= 2
     grad_weight = lax.all_gather(weight_share, MEMBER, axis=0, tiled=True) / devices
-    chips = lax.axis_size("chip")
-    core = lax.axis_index("core")
-    split = partial.reshape(chips, 2, rows, width)
-    kept = jnp.where(core == 0, split[:, 0], split[:, 1])
-    given = jnp.where(core == 0, split[:, 1], split[:, 0]).astype(jnp.bfloat16)
-    paired = kept + lax.ppermute(given, "core", [(0, 1), (1, 0)]).astype(jnp.float32)
     pieces = lax.all_to_all(
-        paired.astype(jnp.bfloat16), "chip", split_axis=0, concat_axis=0, tiled=True
+        paired, "chip", split_axis=0, concat_axis=0, tiled=True
     )
     relaid_grad = jnp.sum(pieces.astype(jnp.float32), axis=0).astype(jnp.bfloat16)
     back_rows = relaid_grad[jnp.minimum(got_slots, rows - 1)]

time: 284 us -> 293 us (1.032)
  blocking collectives: 64.9 us -> 28.2 us
  waiting for transfers between devices: 111 us -> 135 us
  starting transfers between devices: 22.4 us -> 35.9 us
  local copies, waits for them, and re-layouts: 8.46 us -> 11.5 us
    all_to_all x1 -> x0, blocking collectives: 36.7 us -> none  [body(): lax.all_to_all(local_weight.reshape(members, weight_rows, width), MEMBER,...]
    ppermute x1 -> x6, waiting for transfers between devices: 0.01 us -> 28 us  [the longest x4 25.1 us: body(): weight_share = kept + lax.ppermute(given, 'chip', pairs)]
    ppermute x1 -> x6, starting transfers between devices: 0.26 us -> 8.05 us  [the longest x4 7.52 us: body(): weight_share = kept + lax.ppermute(given, 'chip', pairs)]
    all_to_all x1, starting transfers between devices: 13 us -> 18.4 us  [body(): lax.all_to_all(back_rows, ALL, split_axis=0, concat_axis=0, tiled=True)]
    all_to_all x1, waiting for transfers between devices: 38.4 us -> 34.9 us  [body(): lax.all_to_all(paired, 'chip', split_axis=0, concat_axis=0, tiled=True)]
  transfers between devices with their start and end apart: 7 -> 12, of which waited for: 5 -> 10; matrix products, arithmetic and copies ran while one was open for 13% -> 10% of each run, Pallas kernels for 0% -> 0%
where the time goes in v8:
time: 293 us
  waiting for transfers between devices  135 us (46%)
  starting transfers between devices  35.9 us (12%)
  matrix products  34.6 us (12%)
  other arithmetic  33.1 us (11%)
  blocking collectives  28.2 us (10%)
  between operations  14.4 us (5%)
  local copies, waits for them, and re-layouts  11.5 us (4%)
    all_gather x1, waiting for transfers between devices, body(): group_both = lax.all_gather(relaid, MEMBER, axis=0, tiled=True)  57.4 us
    all_to_all x1, waiting for transfers between devices, body(): lax.all_to_all(paired, 'chip', split_axis=0, concat_axis=0, tiled=True)  34.9 us
    all_to_all x1, blocking collectives, body(): lax.all_to_all(send_rows, ALL, split_axis=0, concat_axis=0, tiled=True)  28.2 us
    ppermute x4, waiting for transfers between devices, body(): weight_share = kept + lax.ppermute(given, 'chip', pairs)  25.1 us
    dot_general x6, matrix products, contract(): lax.dot_general(left, right, (((left_dim,), (right_dim,)), ((), ())), pre...  23.5 us
    all_to_all x1, starting transfers between devices, body(): lax.all_to_all(back_rows, ALL, split_axis=0, concat_axis=0, tiled=True)  18.4 us
    all_to_all x1, waiting for transfers between devices, body(): lax.all_to_all(back_rows, ALL, split_axis=0, concat_axis=0, tiled=True)  10.5 us
    convert_element_type x1, other arithmetic, body(): (kept + lax.ppermute(given, 'core', swap).astype(jnp.float32)).astype(jnp...  8.5 us
  transfers between devices with their start and end apart: 12, of which 10 were waited for; matrix products, arithmetic and copies ran while one was open for 10% of the time, Pallas kernels for 0%

profile of v8, /device:TPU:1, one launch (start us, length us, event | category | flops | bytes accessed | tf_op | source)
XLA Modules:
  0.0 292.7 jit_solution(10800126529369360873)
XLA Ops:
  7.2 0.8 fusion.27
  8.0 0.7 and_select_fusion.1
  8.9 1.3 convolution_convert_fusion.3
  10.3 2.1 scatter_custom_fusion
  12.8 28.2 %all_to_all.29 = bf16[128,2,1664]{2,1,0:T(2,128)(2,1)} all-to-all(bf16[128,2,1664]{2,1,0:T(2,128)(2,1)S(1)} %all_to_all.19), channel_id=1, replica_groups=mesh['group'=4,'chip'=16,'core'=2] {'group','chip','core'}, dimensions={0} | all-to-all | bytes 1703936 | tf_op jit(solution)/shard_map/all_to_all | solution.py:45
  41.0 2.4 all_to_all.21
  43.6 2.5 scatter_custom_fusion.1
  46.3 1.9 convolution_convert_fusion.1
  48.2 57.4 %all-gather.3.cloned.1.call-done = bf16[4096,1536]{1,0:T(8,128)(2,1)} async-done(((bf16[128,1536]{1,0:T(8,128)(2,1)}), bf16[4096,1536]{1,0:T(8,128)(2,1)}) %all-gather.3.cloned.1.call-update) | async-done | bytes 12582928 | tf_op jit(solution)/shard_map/all_gather | solution.py:49
  105.6 5.7 %multiply_reduce_fusion = (f32[512]{0:T(512)S(1)}, f32[512,4096]{1,0:T(8,128)S(1)}) fusion(bf16[512,768]{1,0:T(8,128)(2,1)S(1)} %convolution_convert_fusion.1, bf16[4096,1536]{1,0:T(8,128)(2,1)} %all-gather.3.cloned.1.call-done), kind=kOutput, calls=%fused_computation.8 | convolution fusion | flops 3225419264 | bytes 15468544 | tf_op jit(solution)/shard_map/dot_general | solution.py:14
  111.4 3.1 %select_reduce_fusion = (f32[512]{0:T(512)S(1)}, f32[512]{0:T(512)S(1)}) fusion(f32[512,4096]{1,0:T(8,128)S(1)} %get-tuple-element.29, s32[512]{0:T(512)S(1)} %copy-done.6, f32[512]{0:T(512)S(1)} %get-tuple-element.28), kind=kLoop, calls=%fused_computation.5 | loop fusion | flops 12581888 | bytes 8396800 | tf_op jit(solution)/shard_map/reduce_sum | solution.py:56
  115.1 3.9 %multiply_convert_fusion = bf16[512,4096]{1,0:T(8,128)(2,1)S(1)} fusion(f32[512,4096]{1,0:T(8,128)S(1)} %get-tuple-element.29, f32[512]{0:T(512)S(1)} %get-tuple-element.25, f32[512]{0:T(512)S(1)} %copy-done.7, s32[512]{0:T(512)S(1)} %copy-done.6), kind=kLoop, calls=%fused_computation.4 | loop fusion | flops 16777216 | bytes 12589056 | tf_op jit(solution)/shard_map/convert_element_type | solution.py:59
  119.0 3.6 %fusion.29 = f32[4096,768]{1,0:T(8,128)S(1)} fusion(bf16[512,4096]{1,0:T(8,128)(2,1)S(1)} %multiply_convert_fusion, bf16[512,768]{1,0:T(8,128)(2,1)S(1)} %convolution_convert_fusion.1), kind=kOutput, calls=%fused_computation.69 | convolution fusion | flops 3221225472 | bytes 17563648 | tf_op jit(solution)/shard_map/dot_general | solution.py:14
  122.7 2.7 fusion.9
  125.6 7.9 %fusion.10 = bf16[512,768]{1,0:T(8,128)(2,1)S(1)} fusion(bf16[512,4096]{1,0:T(8,128)(2,1)S(1)} %multiply_convert_fusion, bf16[4096,1536]{1,0:T(8,128)(2,1)} %all-gather.3.cloned.1.call-done), kind=kOutput, calls=%fused_computation.24 | convolution fusion | flops 3221618688 | bytes 11272192 | tf_op jit(solution)/shard_map/dot_general | solution.py:60
  133.6 9.0 %fusion = f32[768,768]{0,1:T(8,128)S(1)} fusion(f32[4096,768]{1,0:T(8,128)S(1)} %fusion.29, bf16[4096,1536]{1,0:T(8,128)(2,1)} %all-gather.3.cloned.1.call-done), kind=kOutput, calls=%fused_computation.9 | convolution fusion | flops 4831838208 | bytes 21233664 | tf_op jit(solution)/shard_map/dot_general | solution.py:14
  142.7 2.2 bitcast_add_fusion
  144.9 8.5 %fusion.4 = bf16[16,128,768]{2,1,0:T(8,128)(2,1)} fusion(bf16[16,128,768]{2,1,0:T(8,128)(2,1)} %collective-permute-done, f32[16,2,128,768]{3,2,1,0:T(8,128)} %bitcast.66, pred[]{:T(512)S(6)} %eq.57), kind=kLoop, calls=%fused_computation.14 | loop fusion | flops 6291456 | bytes 18874368 | tf_op jit(solution)/shard_map/convert_element_type | solution.py:71
  153.4 2.0 copy.43
  155.5 1.1 select_bitcast_fusion
  156.9 2.9 collective-permute-done.1
  159.8 1.5 fusion.14
  161.3 1.0 copy-done.2
  162.4 2.8 collective-permute-start.2
  165.1 13.4 %collective-permute-done.2 = f32[8,24,768]{2,1,0:T(8,128)S(1)} collective-permute-done((f32[8,24,768]{2,1,0:T(8,128)S(1)}, f32[8,24,768]{2,1,0:T(8,128)S(1)}, u32[]{:S(2)}, u32[]{:S(2)}) %collective-permute-start.2) | collective-permute-done | bytes 589856 | tf_op jit(solution)/shard_map/ppermute | solution.py:86
  178.6 1.3 select_add_fusion
  179.9 1.3 collective-permute-start.3
  181.2 6.3 %collective-permute-done.3 = f32[4,24,768]{2,1,0:T(8,128)S(1)} collective-permute-done((f32[4,24,768]{2,1,0:T(8,128)S(1)}, f32[4,24,768]{2,1,0:T(8,128)S(1)}, u32[]{:S(2)}, u32[]{:S(2)}) %collective-permute-start.3) | collective-permute-done | bytes 294944 | tf_op jit(solution)/shard_map/ppermute | solution.py:86
  187.5 2.5 collective-permute-start.4
  190.0 3.1 %collective-permute-done.4 = f32[2,24,768]{2,1,0:T(8,128)S(1)} collective-permute-done((f32[2,24,768]{2,1,0:T(8,128)S(1)}, f32[2,24,768]{2,1,0:T(8,128)S(1)}, u32[]{:S(2)}, u32[]{:S(2)}) %collective-permute-start.4) | collective-permute-done | bytes 147488 | tf_op jit(solution)/shard_map/ppermute | solution.py:86
  193.2 1.0 collective-permute-start.5
  194.1 2.3 collective-permute-done.5
  196.5 1.4 collective-permute-start.6
  197.8 2.2 collective-permute-done.6
  200.1 2.9 %collective-permute-start.7 = (f32[24,768]{1,0:T(8,128)S(1)}, f32[24,768]{1,0:T(8,128)S(1)}, u32[]{:S(2)}, u32[]{:S(2)}) collective-permute-start(f32[24,768]{1,0:T(8,128)S(1)} %add.98), channel_id=1, source_target_pairs={{0,64},{32,96},{64,0},{96,32},{1,65},{33,97},{65,1},{97,33},{2,66}... | collective-permute-start | bytes 221192 | tf_op jit(solution)/shard_map/ppermute | solution.py:92
  203.0 1.8 collective-permute-done.7
  204.9 0.6 add.99
  205.5 4.9 %all-to-all-start.1 = ((bf16[16,128,768]{2,1,0:T(8,128)(2,1)}), bf16[16,128,768]{2,1,0:T(8,128)(2,1)}, u32[]{:S(2)}, u32[]{:S(2)}) async-start(bf16[16,128,768]{2,1,0:T(8,128)(2,1)} %fusion.4), calls=%async_computation.1 | async-start | bytes 6291456 | tf_op jit(solution)/shard_map/all_to_all | solution.py:95
  210.5 34.9 %all-to-all-done.1 = bf16[16,128,768]{2,1,0:T(8,128)(2,1)} async-done(((bf16[16,128,768]{2,1,0:T(8,128)(2,1)}), bf16[16,128,768]{2,1,0:T(8,128)(2,1)}, u32[]{:S(2)}, u32[]{:S(2)}) %all-to-all-start.1) | async-done | bytes 3145760 | tf_op jit(solution)/shard_map/all_to_all | solution.py:95
  245.4 2.3 reduce_sum.42
  247.7 1.2 gather_fusion
  248.9 0.9 all_to_all.23
  249.8 18.4 %all-to-all-start.2 = ((bf16[128,2,768]{2,1,0:T(2,128)(2,1)}), bf16[128,2,768]{2,1,0:T(2,128)(2,1)S(1)}, u32[]{:S(2)}, u32[]{:S(2)}) async-start(bf16[128,2,768]{2,1,0:T(2,128)(2,1)} %all_to_all.23), calls=%async_computation.2 | async-start | bytes 786432 | tf_op jit(solution)/shard_map/all_to_all | solution.py:100
  268.2 1.7 convolution_convert_fusion
  269.9 10.5 %all-to-all-done.2 = bf16[128,2,768]{2,1,0:T(2,128)(2,1)S(1)} async-done(((bf16[128,2,768]{2,1,0:T(2,128)(2,1)}), bf16[128,2,768]{2,1,0:T(2,128)(2,1)S(1)}, u32[]{:S(2)}, u32[]{:S(2)}) %all-to-all-start.2) | async-done | bytes 393248 | tf_op jit(solution)/shard_map/all_to_all | solution.py:100
  280.5 0.9 gather_fusion.1
  281.4 1.2 convolution_convert_fusion.2
  282.6 3.2 %broadcast_multiply_fusion = f32[768,768]{1,0:T(8,128)} fusion(f32[768,768]{1,0:T(8,128)} %all-gather.5.cloned.1.call-done), kind=kLoop, calls=%fused_computation.28 | loop fusion | flops 589824 | bytes 4718592 | tf_op jit(solution)/shard_map/div | solution.py:94
  (43 shorter events, 2.7 us)
Async XLA Ops:
  7.2 1.7 copy-start
  7.2 98.5 %all-gather.3.cloned.1.call-start = ((), (), s32[]{:S(2)}) async-start(), calls=%async_computation.3 | async-start | bytes 12976128 | tf_op jit(solution)/shard_map/all_gather | solution.py:49
  46.1 236.5 %all-gather.5.cloned.1.call-start = ((), (), s32[]{:S(2)}) async-start(), calls=%async_computation.4 | async-start | bytes 2433024 | tf_op jit(solution)/shard_map/all_gather | solution.py:94
  48.2 63.1 %copy-start.6 = (s32[512]{0:T(512)S(1)}, s32[512]{0:T(512)}, u32[]{:S(2)}) copy-start(s32[512]{0:T(512)} %param.14) | copy-start | bytes 6148
  111.4 3.7 %copy-start.7 = (f32[512]{0:T(512)S(1)}, f32[512]{0:T(512)}, u32[]{:S(2)}) copy-start(f32[512]{0:T(512)} %param.15) | copy-start | bytes 6148
  122.6 10.9 %copy-start.1 = (f32[4096,768]{1,0:T(8,128)}, f32[4096,768]{1,0:T(8,128)S(1)}, u32[]{:S(2)}) copy-start(f32[4096,768]{1,0:T(8,128)S(1)} %fusion.29) | copy-start | bytes 37748740
  125.4 19.5 %collective-permute-start = (bf16[16,128,768]{2,1,0:T(8,128)(2,1)}, bf16[16,128,768]{2,1,0:T(8,128)(2,1)}, u32[]{:S(2)}, u32[]{:S(2)}) collective-permute-start(bf16[16,128,768]{2,1,0:T(8,128)(2,1)} %fusion.9), channel_id=1, source_target_pairs={{0,1},{1,0},{2,3},{3,2},{4,5},{5,4},{6,7},{7,6},{8,9},{9,8},{10,11... | collective-permute-start | bytes 9437192 | tf_op jit(solution)/shard_map/ppermute | solution.py:71
  133.6 9.0 %copy-start.4 = (bf16[512,768]{1,0:T(8,128)(2,1)}, bf16[512,768]{1,0:T(8,128)(2,1)S(1)}, u32[]{:S(2)}) copy-start(bf16[512,768]{1,0:T(8,128)(2,1)S(1)} %fusion.10) | copy-start | bytes 2359300
  133.6 9.0 %copy-start.3 = (bf16[512,768]{1,0:T(8,128)(2,1)S(1)}, bf16[512,768]{1,0:T(8,128)(2,1)}, u32[]{:S(2)}) copy-start(bf16[512,768]{1,0:T(8,128)(2,1)} %param.10) | copy-start | bytes 2359300
  156.6 3.2 %collective-permute-start.1 = (f32[16,24,768]{2,1,0:T(8,128)}, f32[16,24,768]{2,1,0:T(8,128)}, u32[]{:S(2)}, u32[]{:S(2)}) collective-permute-start(f32[16,24,768]{2,1,0:T(8,128)} %select_bitcast_fusion), channel_id=1, source_target_pairs={{0,1},{1,0},{2,3},{3,2},{4,5},{5,4},{6,7},{7,6},{8,9},{9,8},{10,11... | collective-permute-start | bytes 3538952 | tf_op jit(solution)/shard_map/ppermute | solution.py:77
  161.3 1.0 copy-start.2
  162.4 16.2 %collective-permute-start.2 = (f32[8,24,768]{2,1,0:T(8,128)S(1)}, f32[8,24,768]{2,1,0:T(8,128)S(1)}, u32[]{:S(2)}, u32[]{:S(2)}) collective-permute-start(f32[8,24,768]{2,1,0:T(8,128)S(1)} %slice_select_fusion), channel_id=1, source_target_pairs={{0,16},{2,18},{4,20},{6,22},{8,24},{10,26},{12,28},{14,30},{16,0},... | collective-permute-start | bytes 1769480 | tf_op jit(solution)/shard_map/ppermute | solution.py:86
  179.9 7.5 %collective-permute-start.3 = (f32[4,24,768]{2,1,0:T(8,128)S(1)}, f32[4,24,768]{2,1,0:T(8,128)S(1)}, u32[]{:S(2)}, u32[]{:S(2)}) collective-permute-start(f32[4,24,768]{2,1,0:T(8,128)S(1)} %slice_select_fusion.1), channel_id=1, source_target_pairs={{0,8},{2,10},{4,12},{6,14},{8,0},{10,2},{12,4},{14,6},{16,24},{18,... | collective-permute-start | bytes 884744 | tf_op jit(solution)/shard_map/ppermute | solution.py:86
  187.5 5.6 %collective-permute-start.4 = (f32[2,24,768]{2,1,0:T(8,128)S(1)}, f32[2,24,768]{2,1,0:T(8,128)S(1)}, u32[]{:S(2)}, u32[]{:S(2)}) collective-permute-start(f32[2,24,768]{2,1,0:T(8,128)S(1)} %slice_select_fusion.2), channel_id=1, source_target_pairs={{0,4},{2,6},{4,0},{6,2},{8,12},{10,14},{12,8},{14,10},{16,20},{18,... | collective-permute-start | bytes 442376 | tf_op jit(solution)/shard_map/ppermute | solution.py:86
  193.2 3.3 %collective-permute-start.5 = (f32[1,24,768]{2,1,0:T(8,128)S(1)}, f32[1,24,768]{2,1,0:T(8,128)S(1)}, u32[]{:S(2)}, u32[]{:S(2)}) collective-permute-start(f32[1,24,768]{2,1,0:T(8,128)S(1)} %slice_select_fusion.3), channel_id=1, source_target_pairs={{0,2},{2,0},{4,6},{6,4},{8,10},{10,8},{12,14},{14,12},{16,18},{18,... | collective-permute-start | bytes 221192 | tf_op jit(solution)/shard_map/ppermute | solution.py:86
  196.5 3.6 %collective-permute-start.6 = (f32[24,768]{1,0:T(8,128)S(1)}, f32[24,768]{1,0:T(8,128)S(1)}, u32[]{:S(2)}, u32[]{:S(2)}) collective-permute-start(f32[24,768]{1,0:T(8,128)S(1)} %add_bitcast_fusion), channel_id=1, source_target_pairs={{0,32},{32,0},{64,96},{96,64},{1,33},{33,1},{65,97},{97,65},{2,34}... | collective-permute-start | bytes 221192 | tf_op jit(solution)/shard_map/ppermute | solution.py:92
  200.1 4.8 %collective-permute-start.7 = (f32[24,768]{1,0:T(8,128)S(1)}, f32[24,768]{1,0:T(8,128)S(1)}, u32[]{:S(2)}, u32[]{:S(2)}) collective-permute-start(f32[24,768]{1,0:T(8,128)S(1)} %add.98), channel_id=1, source_target_pairs={{0,64},{32,96},{64,0},{96,32},{1,65},{33,97},{65,1},{97,33},{2,66}... | collective-permute-start | bytes 221192 | tf_op jit(solution)/shard_map/ppermute | solution.py:92
  205.5 39.9 %all-to-all-start.1 = ((bf16[16,128,768]{2,1,0:T(8,128)(2,1)}), bf16[16,128,768]{2,1,0:T(8,128)(2,1)}, u32[]{:S(2)}, u32[]{:S(2)}) async-start(bf16[16,128,768]{2,1,0:T(8,128)(2,1)} %fusion.4), calls=%async_computation.1 | async-start | bytes 6291456 | tf_op jit(solution)/shard_map/all_to_all | solution.py:95
  210.5 57.7 %copy-start.5 = (bf16[512,768]{1,0:T(8,128)(2,1)S(1)}, bf16[512,768]{1,0:T(8,128)(2,1)}, u32[]{:S(2)}) copy-start(bf16[512,768]{1,0:T(8,128)(2,1)} %copy-done.4) | copy-start | bytes 2359300
  249.8 30.5 %all-to-all-start.2 = ((bf16[128,2,768]{2,1,0:T(2,128)(2,1)}), bf16[128,2,768]{2,1,0:T(2,128)(2,1)S(1)}, u32[]{:S(2)}, u32[]{:S(2)}) async-start(bf16[128,2,768]{2,1,0:T(2,128)(2,1)} %all_to_all.23), calls=%async_computation.2 | async-start | bytes 786432 | tf_op jit(solution)/shard_map/all_to_all | solution.py:100
Sparse Core Ops, SparseCore 0:
  46.2 59.4 all-gather.2
  205.6 65.4 all-gather.4

commit v9 on v7

--- a/solution.py
+++ b/solution.py
@@ -47,17 +47,19 @@
     got_slots = got[:, 2 * width].astype(jnp.int32)
     relaid = jnp.zeros((rows, 2 * width), jnp.bfloat16).at[got_slots].set(got_rows, mode="drop")
     chips = lax.axis_size("chip")
+    chip = lax.axis_index("chip")
     core = lax.axis_index("core")
     swap = [(0, 1), (1, 0)]
-    chip_both = lax.all_gather(relaid, "chip", axis=0, tiled=True)
-    group_both = jnp.concatenate([chip_both, lax.ppermute(chip_both, "core", swap)], axis=0)
-    half = chips * rows
-    positive_member = positive // rows
-    positive = (
-        jnp.where(positive_member % 2 == core, 0, half)
-        + positive_member // 2 * rows
-        + positive % rows
-    )
+    me = chip * 2 + core
+    group_both = relaid
+    bit = 1
+    while bit < chips:
+        pairs = [(index, index ^ bit) for index in range(chips)]
+        group_both = jnp.concatenate([group_both, lax.ppermute(group_both, "chip", pairs)])
+        bit *= 2
+    group_both = jnp.concatenate([group_both, lax.ppermute(group_both, "core", swap)])
+    relative = positive // rows ^ me
+    positive = ((relative % 2) * chips + relative // 2) * rows + positive % rows
     group_passages = group_both[:, :width]
     group_hidden = group_both[:, width:]
     scores = contract(query_emb, group_passages, 1, 1) * factor
@@ -86,9 +88,10 @@
         weight_share = weight_share + lax.ppermute(weight_share, "group", pairs)
         step *= 2
     grad_weight = lax.all_gather(weight_share, MEMBER, axis=0, tiled=True) / devices
-    kept = partial[:half].reshape(chips, rows, width)
-    given = partial[half:].reshape(chips, rows, width).astype(jnp.bfloat16)
+    kept = partial[: chips * rows].reshape(chips, rows, width)
+    given = partial[chips * rows :].reshape(chips, rows, width).astype(jnp.bfloat16)
     paired = kept + lax.ppermute(given, "core", swap).astype(jnp.float32)
+    paired = jnp.take(paired, jnp.arange(chips) ^ chip, axis=0)
     pieces = lax.all_to_all(
         paired.astype(jnp.bfloat16), "chip", split_axis=0, concat_axis=0, tiled=True
     )

time: 275 us -> 375 us (1.36)
  waiting for transfers between devices: 114 us -> 190 us
  local copies, waits for them, and re-layouts: 19.8 us -> 30.8 us
  starting transfers between devices: 24.3 us -> 29.5 us
  matrix products: 26.6 us -> 31.6 us
    ppermute x1 -> x5, waiting for transfers between devices: 4.69 us -> 128 us  [the longest x4 119 us: body(): lax.ppermute(group_both, 'chip', pairs)]
    all_gather x1 -> x0, waiting for transfers between devices: 57.4 us -> none  [body(): chip_both = lax.all_gather(relaid, 'chip', axis=0, tiled=True)]
    ppermute x1 -> x5, starting transfers between devices: 0.84 us -> 10.2 us  [the longest x4 5.63 us: body(): lax.ppermute(group_both, 'chip', pairs)]
    ppermute x1, waiting for transfers between devices: 0.38 us -> 6.83 us  [body(): weight_paired = weight_kept + lax.ppermute(weight_given, 'core', swap)]
    dot_general x1, matrix products: 3.44 us -> 9.27 us  [body(): jnp.dot(coef, group_passages, preferred_element_type=jnp.float32)]
    concatenate x1 -> x2, local copies, waits for them, and re-layouts: 3.19 us -> 8.79 us  [the longest x1 5.79 us: body(): jnp.concatenate([group_both, lax.ppermute(group_both, 'core', swap)])]
    add x1 -> x2, other arithmetic: 0.02 us -> 4.38 us  [the longest x1 4.36 us: body(): paired = kept + lax.ppermute(given, 'core', swap).astype(jnp.float32)]
    gather x0 -> x1, local copies, waits for them, and re-layouts: none -> 4.31 us  [body(): paired = jnp.take(paired, jnp.arange(chips) ^ chip, axis=0)]
  transfers between devices with their start and end apart: 9 -> 12, of which waited for: 7 -> 10; matrix products, arithmetic and copies ran while one was open for 7% -> 7% of each run, Pallas kernels for 0% -> 0%
where the time goes in v9:
time: 375 us
  waiting for transfers between devices  190 us (51%)
  blocking collectives  51 us (14%)
  matrix products  31.6 us (8%)
  local copies, waits for them, and re-layouts  30.8 us (8%)
  starting transfers between devices  29.5 us (8%)
  other arithmetic  27.3 us (7%)
  between operations  14.3 us (4%)
    ppermute x4, waiting for transfers between devices, body(): lax.ppermute(group_both, 'chip', pairs)  119 us
    all_to_all x1, waiting for transfers between devices, body(): lax.all_to_all(paired.astype(jnp.bfloat16), 'chip', split_axis=0, concat_...  38.2 us
    all_to_all x1, blocking collectives, body(): lax.all_to_all(send_rows, ALL, split_axis=0, concat_axis=0, tiled=True)  28.2 us
    all_to_all x1, blocking collectives, body(): weight_pieces = lax.all_to_all(weight_paired, 'chip', 0, 0, tiled=True)  22.7 us
    dot_general x6, matrix products, contract(): lax.dot_general(left, right, (((left_dim,), (right_dim,)), ((), ())), pre...  20.3 us
    all_to_all x1, starting transfers between devices, body(): lax.all_to_all(back_rows, ALL, split_axis=0, concat_axis=0, tiled=True)  12.5 us
    all_to_all x1, waiting for transfers between devices, body(): lax.all_to_all(back_rows, ALL, split_axis=0, concat_axis=0, tiled=True)  10.5 us
    ppermute x1, waiting for transfers between devices, body(): lax.ppermute(group_both, 'core', swap)  9.31 us
  transfers between devices with their start and end apart: 12, of which 10 were waited for; matrix products, arithmetic and copies ran while one was open for 7% of the time, Pallas kernels for 0%

profile of v9, /device:TPU:1, one launch (start us, length us, event | category | flops | bytes accessed | tf_op | source)
XLA Modules:
  0.0 374.8 jit_solution(9035297223847358710)
XLA Ops:
  8.9 1.3 convolution_convert_fusion.3
  10.3 2.1 scatter_custom_fusion
  12.8 28.2 %all_to_all.34 = bf16[128,2,1664]{2,1,0:T(2,128)(2,1)} all-to-all(bf16[128,2,1664]{2,1,0:T(2,128)(2,1)S(1)} %all_to_all.22), channel_id=1, replica_groups=mesh['group'=4,'chip'=16,'core'=2] {'group','chip','core'}, dimensions={0} | all-to-all | bytes 1703936 | tf_op jit(solution)/shard_map/all_to_all | solution.py:45
  41.0 2.4 all_to_all.24
  43.6 1.9 scatter_custom_fusion.1
  45.5 9.5 %collective-permute-done = bf16[128,1536]{1,0:T(8,128)(2,1)S(1)} collective-permute-done((bf16[128,1536]{1,0:T(8,128)(2,1)S(1)}, bf16[128,1536]{1,0:T(8,128)(2,1)S(1)}, u32[]{:S(2)}, u32[]{:S(2)}) %collective-permute-start) | collective-permute-done | bytes 393248 | tf_op jit(solution)/shard_map/ppermute | solution.py:58
  55.0 1.3 collective-permute-start.1
  56.3 17.3 %collective-permute-done.1 = bf16[256,1536]{1,0:T(8,128)(2,1)S(1)} collective-permute-done((bf16[256,1536]{1,0:T(8,128)(2,1)S(1)}, bf16[256,1536]{1,0:T(8,128)(2,1)S(1)}, u32[]{:S(2)}, u32[]{:S(2)}) %collective-permute-start.1) | collective-permute-done | bytes 786464 | tf_op jit(solution)/shard_map/ppermute | solution.py:58
  74.0 32.9 %collective-permute-done.2 = bf16[512,1536]{1,0:T(8,128)(2,1)S(1)} collective-permute-done((bf16[512,1536]{1,0:T(8,128)(2,1)S(1)}, bf16[512,1536]{1,0:T(8,128)(2,1)S(1)}, u32[]{:S(2)}, u32[]{:S(2)}) %collective-permute-start.2) | collective-permute-done | bytes 1572896 | tf_op jit(solution)/shard_map/ppermute | solution.py:58
  107.1 4.0 %collective-permute-start.3 = (bf16[1024,1536]{1,0:T(8,128)(2,1)S(1)}, bf16[1024,1536]{1,0:T(8,128)(2,1)S(1)}, u32[]{:S(2)}, u32[]{:S(2)}) collective-permute-start(bf16[1024,1536]{1,0:T(8,128)(2,1)S(1)} %pad_maximum_fusion), channel_id=1, source_target_pairs={{0,16},{2,18},{4,20},{6,22},{8,24},{10,26},{12,28},{14,30},{16,0},... | collective-permute-start | bytes 9437192 | tf_op jit(solution)/shard_map/ppermute | solution.py:58
  111.1 1.0 constant_dynamic-update-slice_fusion.4
  112.1 1.0 constant_dynamic-update-slice_fusion.3
  113.1 1.3 constant_dynamic-update-slice_fusion.2
  114.4 1.8 constant_dynamic-update-slice_fusion.1
  116.2 59.4 %collective-permute-done.3 = bf16[1024,1536]{1,0:T(8,128)(2,1)S(1)} collective-permute-done((bf16[1024,1536]{1,0:T(8,128)(2,1)S(1)}, bf16[1024,1536]{1,0:T(8,128)(2,1)S(1)}, u32[]{:S(2)}, u32[]{:S(2)}) %collective-permute-start.3) | collective-permute-done | bytes 3145760 | tf_op jit(solution)/shard_map/ppermute | solution.py:58
  175.6 3.0 constant_dynamic-update-slice_fusion
  178.6 4.6 %collective-permute-start.4 = (bf16[2048,1536]{1,0:T(8,128)(2,1)}, bf16[2048,1536]{1,0:T(8,128)(2,1)}, u32[]{:S(2)}, u32[]{:S(2)}) collective-permute-start(bf16[2048,1536]{1,0:T(8,128)(2,1)} %get-tuple-element.24), channel_id=1, source_target_pairs={{0,1},{1,0},{2,3},{3,2},{4,5},{5,4},{6,7},{7,6},{8,9},{9,8},{10,11... | collective-permute-start | bytes 18874376 | tf_op jit(solution)/shard_map/ppermute | solution.py:60
  183.2 0.8 convolution_convert_fusion.1
  184.0 9.3 %collective-permute-done.4 = bf16[2048,1536]{1,0:T(8,128)(2,1)} collective-permute-done((bf16[2048,1536]{1,0:T(8,128)(2,1)}, bf16[2048,1536]{1,0:T(8,128)(2,1)}, u32[]{:S(2)}, u32[]{:S(2)}) %collective-permute-start.4) | collective-permute-done | bytes 6291488 | tf_op jit(solution)/shard_map/ppermute | solution.py:60
  193.3 5.8 %constant_dynamic-update-slice_fusion.5 = bf16[4096,1536]{1,0:T(8,128)(2,1)} fusion(bf16[4096,1536]{1,0:T(8,128)(2,1)} %get-tuple-element.25, bf16[2048,1536]{1,0:T(8,128)(2,1)} %collective-permute-done.4), kind=kLoop, calls=%fused_computation.55 | loop fusion | bytes 12582912 | tf_op jit(solution)/shard_map/concatenate | solution.py:60
  199.1 5.7 %multiply_reduce_fusion = (f32[512]{0:T(512)S(1)}, f32[512,4096]{1,0:T(8,128)S(1)}) fusion(bf16[512,768]{1,0:T(8,128)(2,1)S(1)} %convolution_convert_fusion.1, bf16[4096,1536]{1,0:T(8,128)(2,1)} %constant_dynamic-update-slice_fusion.5), kind=kOutput, calls=%fused_computation.9 | convolution fusion | flops 3225419264 | bytes 15468544 | tf_op jit(solution)/shard_map/dot_general | solution.py:14
  204.9 3.1 select_reduce_fusion
  208.6 3.9 %multiply_convert_fusion = bf16[512,4096]{1,0:T(8,128)(2,1)S(1)} fusion(f32[512,4096]{1,0:T(8,128)S(1)} %get-tuple-element.35, f32[512]{0:T(512)S(1)} %get-tuple-element.21, f32[512]{0:T(512)S(1)} %copy-done.3, s32[512]{0:T(512)S(1)} %fusion.29), kind=kLoop, calls=%fused_computation.5 | loop fusion | flops 16777216 | bytes 12589056 | tf_op jit(solution)/shard_map/convert_element_type | solution.py:72
  212.5 3.5 fusion.36
  216.0 9.3 %fusion.8 = bf16[512,768]{1,0:T(8,128)(2,1)S(1)} fusion(bf16[512,4096]{1,0:T(8,128)(2,1)S(1)} %multiply_convert_fusion, bf16[4096,1536]{1,0:T(8,128)(2,1)} %constant_dynamic-update-slice_fusion.5), kind=kOutput, calls=%fused_computation.24 | convolution fusion | flops 3221618688 | bytes 11272192 | tf_op jit(solution)/shard_map/dot_general | solution.py:73
  225.3 0.8 fusion.37
  226.1 2.0 slice.84
  228.2 7.3 %bitcast_add_fusion = f32[768,768]{1,0:T(8,128)S(1)} fusion(f32[768,768]{0,1:T(8,128)S(1)} %fusion.37, f32[4096,768]{1,0:T(8,128)S(1)} %fusion.36, bf16[4096,1536]{1,0:T(8,128)(2,1)} %constant_dynamic-update-slice_fusion.5), kind=kOutput, calls=%fused_computation.20 | convolution fusion | flops 4832428032 | bytes 23592960 | tf_op jit(solution)/shard_map/dot_general | solution.py:14
  236.3 6.8 %collective-permute-done.6 = f32[16,24,768]{2,1,0:T(8,128)S(1)} collective-permute-done((f32[16,24,768]{2,1,0:T(8,128)S(1)}, f32[16,24,768]{2,1,0:T(8,128)S(1)}, u32[]{:S(2)}, u32[]{:S(2)}) %collective-permute-start.6) | collective-permute-done | bytes 1179680 | tf_op jit(solution)/shard_map/ppermute | solution.py:82
  243.4 22.7 %all_to_all.35 = f32[16,24,768]{2,1,0:T(8,128)S(1)} all-to-all(f32[16,24,768]{2,1,0:T(8,128)S(1)} %fusion.12), channel_id=1, replica_groups=mesh['group'=4,'chip'=16,'core'=2] {'chip'}, dimensions={0} | all-to-all | bytes 2359296 | tf_op jit(solution)/shard_map/all_to_all | solution.py:83
  266.6 2.9 collective-permute-done.7
  269.4 1.2 collective-permute-start.8
  270.6 3.6 collective-permute-done.8
  274.9 2.8 slice-done
  277.7 4.4 %convert_add_fusion = bf16[16,128,768]{2,1,0:T(8,128)(2,1)} fusion(f32[16,128,768]{2,1,0:T(8,128)S(1)} %bitcast.40, bf16[16,128,768]{2,1,0:T(8,128)(2,1)} %collective-permute-done.5), kind=kLoop, calls=%fused_computation.14 | loop fusion | flops 4718592 | bytes 12582912 | tf_op jit(solution)/shard_map/add | solution.py:93
  282.1 4.3 %gather_fusion = bf16[16,128,768]{2,1,0:T(8,128)(2,1)} fusion(bf16[16,128,768]{2,1,0:T(8,128)(2,1)} %convert_add_fusion, s32[1024]{0:T(1024)S(1)} %pad_clamp_fusion.2), kind=kCustom, calls=%fused_computation | custom fusion | bytes 6291520 | tf_op jit(solution)/shard_map/jit(_take)/gather | solution.py:94
  286.4 4.4 %select_convert_fusion = bf16[16,128,768]{2,1,0:T(8,128)(2,1)} fusion(bf16[16,128,768]{2,1,0:T(8,128)(2,1)} %gather_fusion, pred[16]{0:T(512)(128)(4,1)S(1)} %compare_and_fusion), kind=kLoop, calls=%fused_computation.13 | loop fusion | flops 1572864 | bytes 6291472 | tf_op jit(solution)/shard_map/convert_element_type | solution.py:96
  290.7 4.5 %all-to-all-start.1 = ((bf16[16,128,768]{2,1,0:T(8,128)(2,1)}), bf16[16,128,768]{2,1,0:T(8,128)(2,1)}, u32[]{:S(2)}, u32[]{:S(2)}) async-start(bf16[16,128,768]{2,1,0:T(8,128)(2,1)} %select_convert_fusion), calls=%async_computation.1 | async-start | bytes 6291456 | tf_op jit(solution)/shard_map/all_to_all | solution.py:95
  295.2 38.2 %all-to-all-done.1 = bf16[16,128,768]{2,1,0:T(8,128)(2,1)} async-done(((bf16[16,128,768]{2,1,0:T(8,128)(2,1)}), bf16[16,128,768]{2,1,0:T(8,128)(2,1)}, u32[]{:S(2)}, u32[]{:S(2)}) %all-to-all-start.1) | async-done | bytes 3145760 | tf_op jit(solution)/shard_map/all_to_all | solution.py:95
  333.4 2.3 reduce_sum.51
  335.7 1.2 gather_fusion.1
  336.9 0.9 all_to_all.26
  337.8 12.5 %all-to-all-start.2 = ((bf16[128,2,768]{2,1,0:T(2,128)(2,1)}), bf16[128,2,768]{2,1,0:T(2,128)(2,1)S(1)}, u32[]{:S(2)}, u32[]{:S(2)}) async-start(bf16[128,2,768]{2,1,0:T(2,128)(2,1)} %all_to_all.26), calls=%async_computation.2 | async-start | bytes 786432 | tf_op jit(solution)/shard_map/all_to_all | solution.py:100
  350.3 1.7 convolution_convert_fusion
  352.0 10.5 %all-to-all-done.2 = bf16[128,2,768]{2,1,0:T(2,128)(2,1)S(1)} async-done(((bf16[128,2,768]{2,1,0:T(2,128)(2,1)}), bf16[128,2,768]{2,1,0:T(2,128)(2,1)S(1)}, u32[]{:S(2)}, u32[]{:S(2)}) %all-to-all-start.2) | async-done | bytes 393248 | tf_op jit(solution)/shard_map/all_to_all | solution.py:100
  362.6 0.9 gather_fusion.2
  363.5 1.2 convolution_convert_fusion.2
  364.7 3.2 broadcast_multiply_fusion
  (46 shorter events, 6.0 us)
Async XLA Ops:
  7.2 1.7 copy-start
  7.2 357.6 %all-gather.2.cloned.1.call-start = ((), (), s32[]{:S(2)}) async-start(), calls=%async_computation.4 | async-start | bytes 2433024 | tf_op jit(solution)/shard_map/all_gather | solution.py:90
  45.4 9.6 %collective-permute-start = (bf16[128,1536]{1,0:T(8,128)(2,1)S(1)}, bf16[128,1536]{1,0:T(8,128)(2,1)S(1)}, u32[]{:S(2)}, u32[]{:S(2)}) collective-permute-start(bf16[128,1536]{1,0:T(8,128)(2,1)S(1)} %scatter_custom_fusion.1), channel_id=1, source_target_pairs={{0,2},{2,0},{4,6},{6,4},{8,10},{10,8},{12,14},{14,12},{16,18},{18,... | collective-permute-start | bytes 1179656 | tf_op jit(solution)/shard_map/ppermute | solution.py:58
  55.0 18.6 %collective-permute-start.1 = (bf16[256,1536]{1,0:T(8,128)(2,1)S(1)}, bf16[256,1536]{1,0:T(8,128)(2,1)S(1)}, u32[]{:S(2)}, u32[]{:S(2)}) collective-permute-start(bf16[256,1536]{1,0:T(8,128)(2,1)S(1)} %pad_maximum_fusion.2), channel_id=1, source_target_pairs={{0,4},{2,6},{4,0},{6,2},{8,12},{10,14},{12,8},{14,10},{16,20},{18,... | collective-permute-start | bytes 2359304 | tf_op jit(solution)/shard_map/ppermute | solution.py:58
  73.8 33.1 %collective-permute-start.2 = (bf16[512,1536]{1,0:T(8,128)(2,1)S(1)}, bf16[512,1536]{1,0:T(8,128)(2,1)S(1)}, u32[]{:S(2)}, u32[]{:S(2)}) collective-permute-start(bf16[512,1536]{1,0:T(8,128)(2,1)S(1)} %pad_maximum_fusion.1), channel_id=1, source_target_pairs={{0,8},{2,10},{4,12},{6,14},{8,0},{10,2},{12,4},{14,6},{16,24},{18,... | collective-permute-start | bytes 4718600 | tf_op jit(solution)/shard_map/ppermute | solution.py:58
  107.1 68.5 %collective-permute-start.3 = (bf16[1024,1536]{1,0:T(8,128)(2,1)S(1)}, bf16[1024,1536]{1,0:T(8,128)(2,1)S(1)}, u32[]{:S(2)}, u32[]{:S(2)}) collective-permute-start(bf16[1024,1536]{1,0:T(8,128)(2,1)S(1)} %pad_maximum_fusion), channel_id=1, source_target_pairs={{0,16},{2,18},{4,20},{6,22},{8,24},{10,26},{12,28},{14,30},{16,0},... | collective-permute-start | bytes 9437192 | tf_op jit(solution)/shard_map/ppermute | solution.py:58
  114.4 68.8 %copy-start.4 = (s32[512]{0:T(512)S(1)}, s32[512]{0:T(512)}, u32[]{:S(2)}) copy-start(s32[512]{0:T(512)} %param.14) | copy-start | bytes 6148
  114.4 68.9 %copy-start.2 = (bf16[512,768]{1,0:T(8,128)(2,1)S(1)}, bf16[512,768]{1,0:T(8,128)(2,1)}, u32[]{:S(2)}) copy-start(bf16[512,768]{1,0:T(8,128)(2,1)} %param.10) | copy-start | bytes 2359300
  178.6 14.7 %collective-permute-start.4 = (bf16[2048,1536]{1,0:T(8,128)(2,1)}, bf16[2048,1536]{1,0:T(8,128)(2,1)}, u32[]{:S(2)}, u32[]{:S(2)}) collective-permute-start(bf16[2048,1536]{1,0:T(8,128)(2,1)} %get-tuple-element.24), channel_id=1, source_target_pairs={{0,1},{1,0},{2,3},{3,2},{4,5},{5,4},{6,7},{7,6},{8,9},{9,8},{10,11... | collective-permute-start | bytes 18874376 | tf_op jit(solution)/shard_map/ppermute | solution.py:60
  204.9 3.7 copy-start.3
  216.0 12.2 %copy-start.1 = (f32[4096,768]{1,0:T(8,128)}, f32[4096,768]{1,0:T(8,128)S(1)}, u32[]{:S(2)}) copy-start(f32[4096,768]{1,0:T(8,128)S(1)} %fusion.36) | copy-start | bytes 37748740
  235.5 39.4 %collective-permute-start.5 = (bf16[16,128,768]{2,1,0:T(8,128)(2,1)}, bf16[16,128,768]{2,1,0:T(8,128)(2,1)}, u32[]{:S(2)}, u32[]{:S(2)}) collective-permute-start(bf16[16,128,768]{2,1,0:T(8,128)(2,1)} %bitcast.1), channel_id=1, source_target_pairs={{0,1},{1,0},{2,3},{3,2},{4,5},{5,4},{6,7},{7,6},{8,9},{9,8},{10,11... | collective-permute-start | bytes 9437192 | tf_op jit(solution)/shard_map/ppermute | solution.py:93
  236.1 7.0 %collective-permute-start.6 = (f32[16,24,768]{2,1,0:T(8,128)S(1)}, f32[16,24,768]{2,1,0:T(8,128)S(1)}, u32[]{:S(2)}, u32[]{:S(2)}) collective-permute-start(f32[16,24,768]{2,1,0:T(8,128)S(1)} %select_bitcast_fusion), channel_id=1, source_target_pairs={{0,1},{1,0},{2,3},{3,2},{4,5},{5,4},{6,7},{7,6},{8,9},{9,8},{10,11... | collective-permute-start | bytes 3538952 | tf_op jit(solution)/shard_map/ppermute | solution.py:82
  266.2 3.3 collective-permute-start.7
  269.4 4.8 %collective-permute-start.8 = (f32[24,768]{1,0:T(8,128)S(1)}, f32[24,768]{1,0:T(8,128)S(1)}, u32[]{:S(2)}, u32[]{:S(2)}) collective-permute-start(f32[24,768]{1,0:T(8,128)S(1)} %add.104), channel_id=1, source_target_pairs={{0,64},{32,96},{64,0},{96,32},{1,65},{33,97},{65,1},{97,33},{2,66}... | collective-permute-start | bytes 221192 | tf_op jit(solution)/shard_map/ppermute | solution.py:88
  274.9 2.8 slice-start
  290.7 42.7 %all-to-all-start.1 = ((bf16[16,128,768]{2,1,0:T(8,128)(2,1)}), bf16[16,128,768]{2,1,0:T(8,128)(2,1)}, u32[]{:S(2)}, u32[]{:S(2)}) async-start(bf16[16,128,768]{2,1,0:T(8,128)(2,1)} %select_convert_fusion), calls=%async_computation.1 | async-start | bytes 6291456 | tf_op jit(solution)/shard_map/all_to_all | solution.py:95
  337.8 24.7 %all-to-all-start.2 = ((bf16[128,2,768]{2,1,0:T(2,128)(2,1)}), bf16[128,2,768]{2,1,0:T(2,128)(2,1)S(1)}, u32[]{:S(2)}, u32[]{:S(2)}) async-start(bf16[128,2,768]{2,1,0:T(2,128)(2,1)} %all_to_all.26), calls=%async_computation.2 | async-start | bytes 786432 | tf_op jit(solution)/shard_map/all_to_all | solution.py:100
Sparse Core Ops, SparseCore 0:
  275.0 67.0 all-gather.1
